TPU v7x, 128 devices: a whole 4x4x4 slice. The times are simulated.
128 devices in a mesh: xb: 16 (over y, z), yb: 8 (over x, core).
Axes of the slice: x: 4, y: 4, z: 4, core: 2. Of those that a mesh axis runs over, the one named last changes fastest.
Arguments:
- initial_guess: float32 [128, 512, 256], P('xb', 'yb'), may hold values from -4 to 4
- right_side: float32 [128, 512, 256], P('xb', 'yb'), may hold values from -8 to 8
- coefficient: float32 [128, 512, 256], P('xb', 'yb'), may hold values from 0.3 to 3
Outputs:
- fine_field: float32 [128, 512, 256], P('xb', 'yb')
- middle_field: float32 [64, 256, 128], P('xb', 'yb')
- lower_field: float32 [32, 128, 64], P('xb', 'yb')
- coarse_field: float32 [16, 64, 32], P('xb', 'yb')
All inputs are finite; a program needn't handle non-finite values.
Results may differ from a plain program's by a relative error of at most 0.00002.
Values sent between devices are 32-bit elements; how exact they have to be, the bound alone decides.
No kernel may reach another device: no remote copies, remote signals or barrier semaphores. Data moves between devices by JAX's collectives and lax.ppermute only.
A program may use at most 192 MiB of HBM per device.

v0:
```python
import jax
import jax.numpy as jnp
from jax import lax
from jax.sharding import PartitionSpec as P

COARSE_ITERS = 8


damping_alpha = 0.05
cheb_theta = 1.15
cheb_delta = 0.85
cheb_sigma = cheb_theta / cheb_delta
cheb_first = 1.0 / cheb_sigma
cheb_second = 1.0 / (2.0 * cheb_sigma - cheb_first)
cheb_carry = cheb_second * cheb_first
cheb_resid = 2.0 * cheb_second / cheb_delta
jacobi_weight = 0.8


def with_halo(block, sides, width):
    for axis, dim in sides:
        count = lax.axis_size(axis)
        forward = [(i, i + 1) for i in range(count - 1)]
        backward = [(target, source) for source, target in forward]
        low = lax.ppermute(
            lax.slice_in_dim(block, block.shape[dim] - width, None, axis=dim), axis, forward
        )
        high = lax.ppermute(lax.slice_in_dim(block, 0, width, axis=dim), axis, backward)
        block = jnp.concatenate([low, block, high], axis=dim)
    return block


def neighbours(padded):
    return [
        padded[2:, 1:-1, 1:-1],
        padded[:-2, 1:-1, 1:-1],
        padded[1:-1, 2:, 1:-1],
        padded[1:-1, :-2, 1:-1],
        padded[1:-1, 1:-1, 2:],
        padded[1:-1, 1:-1, :-2],
    ]


def face_weights(padded_coef, scale):
    centre = padded_coef[1:-1, 1:-1, 1:-1]
    weights = [0.5 * scale * (centre + other) for other in neighbours(padded_coef)]
    diagonal = damping_alpha + weights[0]
    for other in weights[1:]:
        diagonal = diagonal + other
    return (weights, diagonal)


def apply_operator(padded, field, weights, diagonal):
    result = diagonal * field
    for weight, other in zip(weights, neighbours(padded)):
        result = result - weight * other
    return result


def smooth_level(start, right_side, coefficient, scale, extend, padded_coef=None):
    padded_coef = extend(coefficient)
    weights, diagonal = face_weights(padded_coef, scale)
    if start is None:
        start = jnp.zeros_like(right_side)
        residual = right_side
    else:
        residual = right_side - apply_operator(extend(start), start, weights, diagonal)
    first_step = residual / (cheb_theta * diagonal)
    first = start + first_step
    residual = right_side - apply_operator(extend(first), first, weights, diagonal)
    second_step = cheb_carry * first_step + cheb_resid * residual / diagonal
    second = first + second_step
    residual = right_side - apply_operator(extend(second), second, weights, diagonal)
    return (second, residual)


def restrict_field(field):
    sx, sy, sz = field.shape
    return field.reshape(sx // 2, 2, sy // 2, 2, sz // 2, 2).sum(axis=(1, 3, 5)) * 0.125


def coarse_solve(right_side, coefficient, scale, extend):
    weights, diagonal = face_weights(extend(coefficient), scale)
    field = jnp.zeros_like(right_side)
    for repeat in range(COARSE_ITERS):
        field = (
            field
            + jacobi_weight
            * (right_side - apply_operator(extend(field), field, weights, diagonal))
            / diagonal
        )
    leftover = right_side - apply_operator(extend(field), field, weights, diagonal)
    ones_field = jnp.ones_like(right_side)
    image_ones = apply_operator(extend(ones_field), ones_field, weights, diagonal)
    return field + jnp.sum(leftover) / jnp.sum(image_ones)


def extend_all(field):
    return jnp.pad(field, 1)


def extend_local(field):
    padded = with_halo(field, (("xb", 0), ("yb", 1)), 1)
    return jnp.pad(padded, ((0, 0), (0, 0), (1, 1)))


def collect_grid(right_side, coefficient):
    sx, sy, sz = right_side.shape
    count_x = lax.axis_size("xb")
    count_y = lax.axis_size("yb")
    flat = (
        lax.all_gather(right_side.reshape(1, -1), ("xb", "yb"), axis=0, tiled=True),
        lax.all_gather(coefficient.reshape(1, -1), ("xb", "yb"), axis=0, tiled=True),
    )
    return tuple(
        (
            piece.reshape(count_x, count_y, sx, sy, sz)
            .transpose(0, 2, 1, 3, 4)
            .reshape(count_x * sx, count_y * sy, sz)
            for piece in flat
        )
    )


def own_block(whole, shape):
    start_x = lax.axis_index("xb") * shape[0]
    start_y = lax.axis_index("yb") * shape[1]
    return lax.dynamic_slice(whole, (start_x, start_y, jnp.int32(0)), shape)


def per_device(initial_guess, right_side, coefficient):
    fine, fine_res = smooth_level(initial_guess, right_side, coefficient, 1.0, extend_local, None)
    mid_coef = restrict_field(coefficient)
    middle, mid_res = smooth_level(
        None, restrict_field(fine_res), mid_coef, 0.25, extend_local, None
    )
    low_coef = restrict_field(mid_coef)
    low_rhs = restrict_field(mid_res)
    lower, low_res = smooth_level(None, low_rhs, low_coef, 0.0625, extend_local, None)
    coarse_rhs, coarse_coef = collect_grid(restrict_field(low_res), restrict_field(low_coef))
    coarse_whole = coarse_solve(coarse_rhs, coarse_coef, 0.015625, extend_all)
    sx, sy, sz = right_side.shape
    coarse = own_block(coarse_whole, (sx // 8, sy // 8, sz // 8))
    return (fine, middle, lower, coarse)


def solution(mesh):
    placed = (P("xb", "yb", None), P("xb", "yb", None), P("xb", "yb", None))
    return jax.shard_map(
        per_device,
        mesh=mesh,
        in_specs=placed,
        out_specs=(
            P("xb", "yb", None),
            P("xb", "yb", None),
            P("xb", "yb", None),
            P("xb", "yb", None),
        ),
        check_vma=False,
    )
```

profile of v0, /device:TPU:0, one launch (start us, length us, event | category | flops | bytes accessed | tf_op | source)
XLA Modules:
  0.0 352.5 jit_solution(16969961668847992912)
XLA Ops:
  0.6 0.9 fusion.305
  1.5 3.9 %collective-permute-start.1 = (f32[1,64,256]{2,1,0:T(8,128)S(1)}, f32[1,64,256]{2,1,0:T(8,128)S(1)}, u32[]{:S(2)}, u32[]{:S(2)}) collective-permute-start(f32[1,64,256]{2,1,0:T(8,128)S(1)} %get-tuple-element.31), channel_id=1, source_target_pairs={{0,8},{8,16},{16,24},{24,32},{32,40},{40,48},{48,56},{56,64},{64,7... | collective-permute-start | bytes 196616 | tf_op jit(solution)/shard_map/ppermute | solution.py:25
  5.5 1.3 collective-permute-start
  6.8 0.9 fusion.306
  7.6 4.5 %collective-permute-start.5 = (f32[1,64,256]{2,1,0:T(8,128)S(1)}, f32[1,64,256]{2,1,0:T(8,128)S(1)}, u32[]{:S(2)}, u32[]{:S(2)}) collective-permute-start(f32[1,64,256]{2,1,0:T(8,128)S(1)} %get-tuple-element.33), channel_id=1, source_target_pairs={{0,8},{8,16},{16,24},{24,32},{32,40},{40,48},{48,56},{56,64},{64,7... | collective-permute-start | bytes 196616 | tf_op jit(solution)/shard_map/ppermute | solution.py:25
  12.2 1.3 collective-permute-start.4
  13.5 35.6 %reshape.61 = f32[4,2,32,2,128,2]{5,4,3,2,1,0:T(8,128)} reshape(f32[8,64,256]{2,1,0:T(8,128)} %param.5) | data formatting | bytes 1048576 | tf_op jit(solution)/shard_map/reshape | solution.py:79
  49.1 12.9 %reduce_sum.87 = f32[4,32,128]{2,1,0:T(8,128)} reduce(f32[4,2,32,2,128,2]{5,4,3,2,1,0:T(8,128)} %reshape.61, f32[]{:T(128)} %constant.20.clone.1), dimensions={1,3,5}, to_apply=%region_1.2 | reduce | flops 114688 | bytes 589828 | tf_op jit(solution)/shard_map/reduce_sum | solution.py:79
  62.2 1.4 collective-permute-start.2
  63.6 3.0 collective-permute-start.3
  66.8 1.3 collective-permute-start.6
  68.1 3.6 %collective-permute-start.7 = (f32[10,1,256]{2,1,0:T(1,128)S(1)}, f32[10,1,256]{2,1,0:T(1,128)S(1)}, u32[]{:S(2)}, u32[]{:S(2)}) collective-permute-start(f32[10,1,256]{2,1,0:T(1,128)S(1)} %get-tuple-element.24), channel_id=1, source_target_pairs={{0,1},{1,2},{2,3},{3,4},{4,5},{5,6},{6,7},{8,9},{9,10},{10,11},{11... | collective-permute-start | bytes 30728 | tf_op jit(solution)/shard_map/ppermute | solution.py:25
  73.3 2.0 fusion.299
  75.3 1.3 collective-permute-start.8
  76.6 5.2 %collective-permute-start.9 = (f32[1,64,256]{2,1,0:T(8,128)S(1)}, f32[1,64,256]{2,1,0:T(8,128)S(1)}, u32[]{:S(2)}, u32[]{:S(2)}) collective-permute-start(f32[1,64,256]{2,1,0:T(8,128)S(1)} %get-tuple-element.28), channel_id=1, source_target_pairs={{0,8},{8,16},{16,24},{24,32},{32,40},{40,48},{48,56},{56,64},{64,7... | collective-permute-start | bytes 196616 | tf_op jit(solution)/shard_map/ppermute | solution.py:25
  82.1 1.6 collective-permute-done.9
  83.7 1.3 collective-permute-start.10
  85.0 3.4 collective-permute-start.11
  89.0 1.3 collective-permute-start.16
  90.3 5.2 %collective-permute-start.17 = (f32[1,32,128]{2,1,0:T(8,128)}, f32[1,32,128]{2,1,0:T(8,128)}, u32[]{:S(2)}, u32[]{:S(2)}) collective-permute-start(f32[1,32,128]{2,1,0:T(8,128)} %get-tuple-element.44), channel_id=1, source_target_pairs={{0,8},{8,16},{16,24},{24,32},{32,40},{40,48},{48,56},{56,64},{64,7... | collective-permute-start | bytes 49160 | tf_op jit(solution)/shard_map/ppermute | solution.py:25
  95.5 5.5 %mul.617 = f32[2,2,16,2,64,2]{5,4,3,2,1,0:T(8,128)} reshape(f32[4,32,128]{2,1,0:T(8,128)S(1)} %broadcast_multiply_fusion) | data formatting | bytes 131072 | tf_op jit(solution)/shard_map/mul | solution.py:79
  101.0 2.5 reduce_sum.89
  104.8 2.1 fusion.181
  107.0 1.3 collective-permute-start.12
  108.3 4.5 %collective-permute-start.13 = (f32[1,64,256]{2,1,0:T(8,128)S(1)}, f32[1,64,256]{2,1,0:T(8,128)S(1)}, u32[]{:S(2)}, u32[]{:S(2)}) collective-permute-start(f32[1,64,256]{2,1,0:T(8,128)S(1)} %get-tuple-element.26), channel_id=1, source_target_pairs={{0,8},{8,16},{16,24},{24,32},{32,40},{40,48},{48,56},{56,64},{64,7... | collective-permute-start | bytes 196616 | tf_op jit(solution)/shard_map/ppermute | solution.py:25
  113.6 1.3 collective-permute-start.18
  114.8 4.9 %collective-permute-start.19 = (f32[6,1,128]{2,1,0:T(1,128)S(1)}, f32[6,1,128]{2,1,0:T(1,128)S(1)}, u32[]{:S(2)}, u32[]{:S(2)}) collective-permute-start(f32[6,1,128]{2,1,0:T(1,128)S(1)} %get-tuple-element.38), channel_id=1, source_target_pairs={{0,1},{1,2},{2,3},{3,4},{4,5},{5,6},{6,7},{8,9},{9,10},{10,11},{11... | collective-permute-start | bytes 9224 | tf_op jit(solution)/shard_map/ppermute | solution.py:25
  119.8 1.3 collective-permute-start.14
  121.1 4.5 %collective-permute-start.15 = (f32[10,1,256]{2,1,0:T(1,128)S(1)}, f32[10,1,256]{2,1,0:T(1,128)S(1)}, u32[]{:S(2)}, u32[]{:S(2)}) collective-permute-start(f32[10,1,256]{2,1,0:T(1,128)S(1)} %get-tuple-element.18), channel_id=1, source_target_pairs={{0,1},{1,2},{2,3},{3,4},{4,5},{5,6},{6,7},{8,9},{9,10},{10,11},{11... | collective-permute-start | bytes 30728 | tf_op jit(solution)/shard_map/ppermute | solution.py:25
  125.6 1.6 select_maximum_fusion.20
  127.6 1.1 fusion.166
  128.8 34.9 %reshape.60 = f32[4,2,32,2,128,2]{5,4,3,2,1,0:T(8,128)} reshape(f32[8,64,256]{2,1,0:T(8,128)S(1)} %fusion.166) | data formatting | bytes 1048576 | tf_op jit(solution)/shard_map/reshape | solution.py:79
  163.7 12.3 %reduce_sum.86 = f32[4,32,128]{2,1,0:T(8,128)S(1)} reduce(f32[4,2,32,2,128,2]{5,4,3,2,1,0:T(8,128)} %reshape.60, f32[]{:T(128)} %constant.20.clone.1), dimensions={1,3,5}, to_apply=%region_0.1 | reduce | flops 114688 | bytes 589828 | tf_op jit(solution)/shard_map/reduce_sum | solution.py:79
  176.8 1.3 collective-permute-start.20
  178.1 5.9 %collective-permute-start.21 = (f32[1,32,128]{2,1,0:T(8,128)S(1)}, f32[1,32,128]{2,1,0:T(8,128)S(1)}, u32[]{:S(2)}, u32[]{:S(2)}) collective-permute-start(f32[1,32,128]{2,1,0:T(8,128)S(1)} %get-tuple-element.42), channel_id=1, source_target_pairs={{0,8},{8,16},{16,24},{24,32},{32,40},{40,48},{48,56},{56,64},{64,7... | collective-permute-start | bytes 49160 | tf_op jit(solution)/shard_map/ppermute | solution.py:25
  184.0 1.4 collective-permute-done.21
  185.4 1.3 collective-permute-start.22
  186.7 3.4 collective-permute-start.23
  190.1 1.3 collective-permute-start.28
  191.4 7.0 %collective-permute-start.29 = (f32[1,16,64]{2,1,0:T(8,128)S(1)}, f32[1,16,64]{2,1,0:T(8,128)S(1)}, u32[]{:S(2)}, u32[]{:S(2)}) collective-permute-start(f32[1,16,64]{2,1,0:T(8,128)S(1)} %get-tuple-element.57), channel_id=1, source_target_pairs={{0,8},{8,16},{16,24},{24,32},{32,40},{40,48},{48,56},{56,64},{64,7... | collective-permute-start | bytes 12296 | tf_op jit(solution)/shard_map/ppermute | solution.py:25
  198.6 0.9 fusion.232
  199.6 1.3 collective-permute-start.24
  200.9 6.4 %collective-permute-start.25 = (f32[1,32,128]{2,1,0:T(8,128)S(1)}, f32[1,32,128]{2,1,0:T(8,128)S(1)}, u32[]{:S(2)}, u32[]{:S(2)}) collective-permute-start(f32[1,32,128]{2,1,0:T(8,128)S(1)} %get-tuple-element.40), channel_id=1, source_target_pairs={{0,8},{8,16},{16,24},{24,32},{32,40},{40,48},{48,56},{56,64},{64,7... | collective-permute-start | bytes 49160 | tf_op jit(solution)/shard_map/ppermute | solution.py:25
  207.3 1.3 collective-permute-start.30
  208.6 4.1 %collective-permute-start.31 = (f32[4,1,64]{2,1,0:T(1,128)S(1)}, f32[4,1,64]{2,1,0:T(1,128)S(1)}, u32[]{:S(2)}, u32[]{:S(2)}) collective-permute-start(f32[4,1,64]{2,1,0:T(1,128)S(1)} %get-tuple-element.50), channel_id=1, source_target_pairs={{0,1},{1,2},{2,3},{3,4},{4,5},{5,6},{6,7},{8,9},{9,10},{10,11},{11... | collective-permute-start | bytes 3080 | tf_op jit(solution)/shard_map/ppermute | solution.py:25
  212.7 1.3 collective-permute-start.26
  214.0 4.3 %collective-permute-start.27 = (f32[6,1,128]{2,1,0:T(1,128)S(1)}, f32[6,1,128]{2,1,0:T(1,128)S(1)}, u32[]{:S(2)}, u32[]{:S(2)}) collective-permute-start(f32[6,1,128]{2,1,0:T(1,128)S(1)} %get-tuple-element.34), channel_id=1, source_target_pairs={{0,1},{1,2},{2,3},{3,4},{4,5},{5,6},{6,7},{8,9},{9,10},{10,11},{11... | collective-permute-start | bytes 9224 | tf_op jit(solution)/shard_map/ppermute | solution.py:25
  219.3 0.9 fusion.217
  220.2 5.5 %reshape.62 = f32[2,2,16,2,64,2]{5,4,3,2,1,0:T(8,128)} reshape(f32[4,32,128]{2,1,0:T(8,128)S(1)} %fusion.217) | data formatting | bytes 131072 | tf_op jit(solution)/shard_map/reshape | solution.py:79
  225.7 2.5 reduce_sum.88
  228.4 1.3 collective-permute-start.32
  229.7 6.7 %collective-permute-start.33 = (f32[1,16,64]{2,1,0:T(8,128)S(1)}, f32[1,16,64]{2,1,0:T(8,128)S(1)}, u32[]{:S(2)}, u32[]{:S(2)}) collective-permute-start(f32[1,16,64]{2,1,0:T(8,128)S(1)} %get-tuple-element.55), channel_id=1, source_target_pairs={{0,8},{8,16},{16,24},{24,32},{32,40},{40,48},{48,56},{56,64},{64,7... | collective-permute-start | bytes 12296 | tf_op jit(solution)/shard_map/ppermute | solution.py:25
  236.3 1.3 collective-permute-done.33
  237.7 1.3 collective-permute-start.34
  239.0 3.3 collective-permute-start.35
  243.3 1.3 collective-permute-start.36
  244.6 6.9 %collective-permute-start.37 = (f32[1,16,64]{2,1,0:T(8,128)S(1)}, f32[1,16,64]{2,1,0:T(8,128)S(1)}, u32[]{:S(2)}, u32[]{:S(2)}) collective-permute-start(f32[1,16,64]{2,1,0:T(8,128)S(1)} %get-tuple-element.53), channel_id=1, source_target_pairs={{0,8},{8,16},{16,24},{24,32},{32,40},{40,48},{48,56},{56,64},{64,7... | collective-permute-start | bytes 12296 | tf_op jit(solution)/shard_map/ppermute | solution.py:25
  251.7 1.3 collective-permute-done.37
  252.9 1.3 collective-permute-start.38
  254.2 4.7 %collective-permute-start.39 = (f32[4,1,64]{2,1,0:T(1,128)S(1)}, f32[4,1,64]{2,1,0:T(1,128)S(1)}, u32[]{:S(2)}, u32[]{:S(2)}) collective-permute-start(f32[4,1,64]{2,1,0:T(1,128)S(1)} %get-tuple-element.46), channel_id=1, source_target_pairs={{0,1},{1,2},{2,3},{3,4},{4,5},{5,6},{6,7},{8,9},{9,10},{10,11},{11... | collective-permute-start | bytes 3080 | tf_op jit(solution)/shard_map/ppermute | solution.py:25
  259.0 49.1 %all-gather.1 = f32[128,1,256]{2,1,0:T(1,128)S(1)} all-gather(f32[1,1,256]{2,1,0:T(1,128)S(1)} %reshape.65), channel_id=1, replica_groups=mesh['xb'=16,'yb'=8] {'xb','yb'}, dimensions={0}, use_global_device_ids=true | all-gather | bytes 132096 | tf_op jit(solution)/shard_map/all_gather | solution.py:113
  309.2 33.5 %all-gather = f32[128,1,256]{2,1,0:T(1,128)S(1)} all-gather(f32[1,1,256]{2,1,0:T(1,128)S(1)} %reshape.63), channel_id=1, replica_groups=mesh['xb'=16,'yb'=8] {'xb','yb'}, dimensions={0}, use_global_device_ids=true | all-gather | bytes 132096 | tf_op jit(solution)/shard_map/all_gather | solution.py:112
  343.2 1.0 fusion.147
  349.1 1.5 fusion.213
  (137 shorter events, 15.1 us)
Async XLA Ops:
  1.5 60.5 %collective-permute-start.1 = (f32[1,64,256]{2,1,0:T(8,128)S(1)}, f32[1,64,256]{2,1,0:T(8,128)S(1)}, u32[]{:S(2)}, u32[]{:S(2)}) collective-permute-start(f32[1,64,256]{2,1,0:T(8,128)S(1)} %get-tuple-element.31), channel_id=1, source_target_pairs={{0,8},{8,16},{16,24},{24,32},{32,40},{40,48},{48,56},{56,64},{64,7... | collective-permute-start | bytes 196616 | tf_op jit(solution)/shard_map/ppermute | solution.py:25
  5.5 56.7 %collective-permute-start = (f32[1,64,256]{2,1,0:T(8,128)S(1)}, f32[1,64,256]{2,1,0:T(8,128)S(1)}, u32[]{:S(2)}, u32[]{:S(2)}) collective-permute-start(f32[1,64,256]{2,1,0:T(8,128)S(1)} %get-tuple-element.30), channel_id=1, source_target_pairs={{8,0},{16,8},{24,16},{32,24},{40,32},{48,40},{56,48},{64,56},{72,6... | collective-permute-start | bytes 196616 | tf_op jit(solution)/shard_map/ppermute | solution.py:28
  7.6 59.0 %collective-permute-start.5 = (f32[1,64,256]{2,1,0:T(8,128)S(1)}, f32[1,64,256]{2,1,0:T(8,128)S(1)}, u32[]{:S(2)}, u32[]{:S(2)}) collective-permute-start(f32[1,64,256]{2,1,0:T(8,128)S(1)} %get-tuple-element.33), channel_id=1, source_target_pairs={{0,8},{8,16},{16,24},{24,32},{32,40},{40,48},{48,56},{56,64},{64,7... | collective-permute-start | bytes 196616 | tf_op jit(solution)/shard_map/ppermute | solution.py:25
  12.2 54.5 %collective-permute-start.4 = (f32[1,64,256]{2,1,0:T(8,128)S(1)}, f32[1,64,256]{2,1,0:T(8,128)S(1)}, u32[]{:S(2)}, u32[]{:S(2)}) collective-permute-start(f32[1,64,256]{2,1,0:T(8,128)S(1)} %get-tuple-element.32), channel_id=1, source_target_pairs={{8,0},{16,8},{24,16},{32,24},{40,32},{48,40},{56,48},{64,56},{72,6... | collective-permute-start | bytes 196616 | tf_op jit(solution)/shard_map/ppermute | solution.py:28
  49.1 12.9 %copy-start = (f32[8,64,256]{2,1,0:T(8,128)S(1)}, f32[8,64,256]{2,1,0:T(8,128)}, u32[]{:S(2)}) copy-start(f32[8,64,256]{2,1,0:T(8,128)} %param.5) | copy-start | bytes 1572868
  62.0 4.6 %copy-start.4 = (f32[8,64,256]{2,1,0:T(8,128)S(1)}, f32[8,64,256]{2,1,0:T(8,128)}, u32[]{:S(2)}) copy-start(f32[8,64,256]{2,1,0:T(8,128)} %param.3) | copy-start | bytes 1572868
  62.2 9.6 %collective-permute-start.2 = (f32[10,1,256]{2,1,0:T(1,128)S(1)}, f32[10,1,256]{2,1,0:T(1,128)S(1)}, u32[]{:S(2)}, u32[]{:S(2)}) collective-permute-start(f32[10,1,256]{2,1,0:T(1,128)S(1)} %get-tuple-element.23), channel_id=1, source_target_pairs={{1,0},{2,1},{3,2},{4,3},{5,4},{6,5},{7,6},{9,8},{10,9},{11,10},{12... | collective-permute-start | bytes 30728 | tf_op jit(solution)/shard_map/ppermute | solution.py:28
  63.6 8.2 %collective-permute-start.3 = (f32[10,1,256]{2,1,0:T(1,128)S(1)}, f32[10,1,256]{2,1,0:T(1,128)S(1)}, u32[]{:S(2)}, u32[]{:S(2)}) collective-permute-start(f32[10,1,256]{2,1,0:T(1,128)S(1)} %get-tuple-element.22), channel_id=1, source_target_pairs={{0,1},{1,2},{2,3},{3,4},{4,5},{5,6},{6,7},{8,9},{9,10},{10,11},{11... | collective-permute-start | bytes 30728 | tf_op jit(solution)/shard_map/ppermute | solution.py:25
  66.7 5.0 %copy-start.12 = (f32[1,64,256]{2,1,0:T(8,128)}, f32[1,64,256]{2,1,0:T(8,128)S(1)}, u32[]{:S(2)}) copy-start(f32[1,64,256]{2,1,0:T(8,128)S(1)} %collective-permute-done.4) | copy-start | bytes 196612
  66.8 5.5 %collective-permute-start.6 = (f32[10,1,256]{2,1,0:T(1,128)S(1)}, f32[10,1,256]{2,1,0:T(1,128)S(1)}, u32[]{:S(2)}, u32[]{:S(2)}) collective-permute-start(f32[10,1,256]{2,1,0:T(1,128)S(1)} %get-tuple-element.25), channel_id=1, source_target_pairs={{1,0},{2,1},{3,2},{4,3},{5,4},{6,5},{7,6},{9,8},{10,9},{11,10},{12... | collective-permute-start | bytes 30728 | tf_op jit(solution)/shard_map/ppermute | solution.py:28
  68.1 4.5 %collective-permute-start.7 = (f32[10,1,256]{2,1,0:T(1,128)S(1)}, f32[10,1,256]{2,1,0:T(1,128)S(1)}, u32[]{:S(2)}, u32[]{:S(2)}) collective-permute-start(f32[10,1,256]{2,1,0:T(1,128)S(1)} %get-tuple-element.24), channel_id=1, source_target_pairs={{0,1},{1,2},{2,3},{3,4},{4,5},{5,6},{6,7},{8,9},{9,10},{10,11},{11... | collective-permute-start | bytes 30728 | tf_op jit(solution)/shard_map/ppermute | solution.py:25
  71.7 1.3 copy-start.14
  71.8 1.2 copy-start.16
  72.2 1.0 copy-start.2
  72.2 1.0 copy-start.13
  73.3 8.5 %copy-start.11 = (f32[4,32,128]{2,1,0:T(8,128)S(1)}, f32[4,32,128]{2,1,0:T(8,128)}, u32[]{:S(2)}) copy-start(f32[4,32,128]{2,1,0:T(8,128)} %reduce_sum.87) | copy-start | bytes 196612
  75.3 6.8 %collective-permute-start.8 = (f32[1,64,256]{2,1,0:T(8,128)S(1)}, f32[1,64,256]{2,1,0:T(8,128)S(1)}, u32[]{:S(2)}, u32[]{:S(2)}) collective-permute-start(f32[1,64,256]{2,1,0:T(8,128)S(1)} %get-tuple-element.29), channel_id=1, source_target_pairs={{8,0},{16,8},{24,16},{32,24},{40,32},{48,40},{56,48},{64,56},{72,6... | collective-permute-start | bytes 196616 | tf_op jit(solution)/shard_map/ppermute | solution.py:28
  76.6 7.1 %collective-permute-start.9 = (f32[1,64,256]{2,1,0:T(8,128)S(1)}, f32[1,64,256]{2,1,0:T(8,128)S(1)}, u32[]{:S(2)}, u32[]{:S(2)}) collective-permute-start(f32[1,64,256]{2,1,0:T(8,128)S(1)} %get-tuple-element.28), channel_id=1, source_target_pairs={{0,8},{8,16},{16,24},{24,32},{32,40},{40,48},{48,56},{56,64},{64,7... | collective-permute-start | bytes 196616 | tf_op jit(solution)/shard_map/ppermute | solution.py:25
  82.1 21.6 %copy-start.8 = (f32[1,64,256]{2,1,0:T(8,128)}, f32[1,64,256]{2,1,0:T(8,128)S(1)}, u32[]{:S(2)}) copy-start(f32[1,64,256]{2,1,0:T(8,128)S(1)} %collective-permute-done.8) | copy-start | bytes 196612
  83.7 20.0 %copy-start.9 = (f32[1,64,256]{2,1,0:T(8,128)}, f32[1,64,256]{2,1,0:T(8,128)S(1)}, u32[]{:S(2)}) copy-start(f32[1,64,256]{2,1,0:T(8,128)S(1)} %collective-permute-done.9) | copy-start | bytes 196612
  83.7 19.9 %collective-permute-start.10 = (f32[10,1,256]{2,1,0:T(1,128)S(1)}, f32[10,1,256]{2,1,0:T(1,128)S(1)}, u32[]{:S(2)}, u32[]{:S(2)}) collective-permute-start(f32[10,1,256]{2,1,0:T(1,128)S(1)} %get-tuple-element.21), channel_id=1, source_target_pairs={{1,0},{2,1},{3,2},{4,3},{5,4},{6,5},{7,6},{9,8},{10,9},{11,10},{12... | collective-permute-start | bytes 30728 | tf_op jit(solution)/shard_map/ppermute | solution.py:28
  85.0 18.7 %collective-permute-start.11 = (f32[10,1,256]{2,1,0:T(1,128)S(1)}, f32[10,1,256]{2,1,0:T(1,128)S(1)}, u32[]{:S(2)}, u32[]{:S(2)}) collective-permute-start(f32[10,1,256]{2,1,0:T(1,128)S(1)} %get-tuple-element.20), channel_id=1, source_target_pairs={{0,1},{1,2},{2,3},{3,4},{4,5},{5,6},{6,7},{8,9},{9,10},{10,11},{11... | collective-permute-start | bytes 30728 | tf_op jit(solution)/shard_map/ppermute | solution.py:25
  89.0 23.8 %collective-permute-start.16 = (f32[1,32,128]{2,1,0:T(8,128)}, f32[1,32,128]{2,1,0:T(8,128)}, u32[]{:S(2)}, u32[]{:S(2)}) collective-permute-start(f32[1,32,128]{2,1,0:T(8,128)} %get-tuple-element.45), channel_id=1, source_target_pairs={{8,0},{16,8},{24,16},{32,24},{40,32},{48,40},{56,48},{64,56},{72,6... | collective-permute-start | bytes 49160 | tf_op jit(solution)/shard_map/ppermute | solution.py:28
  90.3 22.5 %collective-permute-start.17 = (f32[1,32,128]{2,1,0:T(8,128)}, f32[1,32,128]{2,1,0:T(8,128)}, u32[]{:S(2)}, u32[]{:S(2)}) collective-permute-start(f32[1,32,128]{2,1,0:T(8,128)} %get-tuple-element.44), channel_id=1, source_target_pairs={{0,8},{8,16},{16,24},{24,32},{32,40},{40,48},{48,56},{56,64},{64,7... | collective-permute-start | bytes 49160 | tf_op jit(solution)/shard_map/ppermute | solution.py:25
  103.6 1.1 copy-start.3
  103.6 1.2 copy-start.5
  103.6 1.2 copy-start.15
  103.6 1.2 copy-start.17
  103.7 0.6 copy-start.18
  103.7 0.6 copy-start.19
  106.9 20.7 %copy-start.1 = (f32[8,64,256]{2,1,0:T(8,128)}, f32[8,64,256]{2,1,0:T(8,128)S(1)}, u32[]{:S(2)}) copy-start(f32[8,64,256]{2,1,0:T(8,128)S(1)} %fusion.181) | copy-start | bytes 1572868
  107.0 12.8 %collective-permute-start.12 = (f32[1,64,256]{2,1,0:T(8,128)S(1)}, f32[1,64,256]{2,1,0:T(8,128)S(1)}, u32[]{:S(2)}, u32[]{:S(2)}) collective-permute-start(f32[1,64,256]{2,1,0:T(8,128)S(1)} %get-tuple-element.27), channel_id=1, source_target_pairs={{8,0},{16,8},{24,16},{32,24},{40,32},{48,40},{56,48},{64,56},{72,6... | collective-permute-start | bytes 196616 | tf_op jit(solution)/shard_map/ppermute | solution.py:28
  108.3 11.5 %collective-permute-start.13 = (f32[1,64,256]{2,1,0:T(8,128)S(1)}, f32[1,64,256]{2,1,0:T(8,128)S(1)}, u32[]{:S(2)}, u32[]{:S(2)}) collective-permute-start(f32[1,64,256]{2,1,0:T(8,128)S(1)} %get-tuple-element.26), channel_id=1, source_target_pairs={{0,8},{8,16},{16,24},{24,32},{32,40},{40,48},{48,56},{56,64},{64,7... | collective-permute-start | bytes 196616 | tf_op jit(solution)/shard_map/ppermute | solution.py:25
  113.6 12.0 %collective-permute-start.18 = (f32[6,1,128]{2,1,0:T(1,128)S(1)}, f32[6,1,128]{2,1,0:T(1,128)S(1)}, u32[]{:S(2)}, u32[]{:S(2)}) collective-permute-start(f32[6,1,128]{2,1,0:T(1,128)S(1)} %get-tuple-element.39), channel_id=1, source_target_pairs={{1,0},{2,1},{3,2},{4,3},{5,4},{6,5},{7,6},{9,8},{10,9},{11,10},{12... | collective-permute-start | bytes 9224 | tf_op jit(solution)/shard_map/ppermute | solution.py:28
  114.8 10.7 %collective-permute-start.19 = (f32[6,1,128]{2,1,0:T(1,128)S(1)}, f32[6,1,128]{2,1,0:T(1,128)S(1)}, u32[]{:S(2)}, u32[]{:S(2)}) collective-permute-start(f32[6,1,128]{2,1,0:T(1,128)S(1)} %get-tuple-element.38), channel_id=1, source_target_pairs={{0,1},{1,2},{2,3},{3,4},{4,5},{5,6},{6,7},{8,9},{9,10},{10,11},{11... | collective-permute-start | bytes 9224 | tf_op jit(solution)/shard_map/ppermute | solution.py:25
  119.8 7.4 %collective-permute-start.14 = (f32[10,1,256]{2,1,0:T(1,128)S(1)}, f32[10,1,256]{2,1,0:T(1,128)S(1)}, u32[]{:S(2)}, u32[]{:S(2)}) collective-permute-start(f32[10,1,256]{2,1,0:T(1,128)S(1)} %get-tuple-element.19), channel_id=1, source_target_pairs={{1,0},{2,1},{3,2},{4,3},{5,4},{6,5},{7,6},{9,8},{10,9},{11,10},{12... | collective-permute-start | bytes 30728 | tf_op jit(solution)/shard_map/ppermute | solution.py:28
  121.1 6.1 %collective-permute-start.15 = (f32[10,1,256]{2,1,0:T(1,128)S(1)}, f32[10,1,256]{2,1,0:T(1,128)S(1)}, u32[]{:S(2)}, u32[]{:S(2)}) collective-permute-start(f32[10,1,256]{2,1,0:T(1,128)S(1)} %get-tuple-element.18), channel_id=1, source_target_pairs={{0,1},{1,2},{2,3},{3,4},{4,5},{5,6},{6,7},{8,9},{9,10},{10,11},{11... | collective-permute-start | bytes 30728 | tf_op jit(solution)/shard_map/ppermute | solution.py:25
  163.7 12.3 %copy-start.6 = (f32[6,34,130]{2,1,0:T(8,128)S(1)}, f32[6,34,130]{2,1,0:T(8,128)}, u32[]{:S(2)}) copy-start(f32[6,34,130]{2,1,0:T(8,128)} %select_maximum_fusion.20) | copy-start | bytes 318244
  176.8 7.2 %collective-permute-start.20 = (f32[1,32,128]{2,1,0:T(8,128)S(1)}, f32[1,32,128]{2,1,0:T(8,128)S(1)}, u32[]{:S(2)}, u32[]{:S(2)}) collective-permute-start(f32[1,32,128]{2,1,0:T(8,128)S(1)} %get-tuple-element.43), channel_id=1, source_target_pairs={{8,0},{16,8},{24,16},{32,24},{40,32},{48,40},{56,48},{64,56},{72,6... | collective-permute-start | bytes 49160 | tf_op jit(solution)/shard_map/ppermute | solution.py:28
  178.1 7.3 %collective-permute-start.21 = (f32[1,32,128]{2,1,0:T(8,128)S(1)}, f32[1,32,128]{2,1,0:T(8,128)S(1)}, u32[]{:S(2)}, u32[]{:S(2)}) collective-permute-start(f32[1,32,128]{2,1,0:T(8,128)S(1)} %get-tuple-element.42), channel_id=1, source_target_pairs={{0,8},{8,16},{16,24},{24,32},{32,40},{40,48},{48,56},{56,64},{64,7... | collective-permute-start | bytes 49160 | tf_op jit(solution)/shard_map/ppermute | solution.py:25
  185.4 13.0 %collective-permute-start.22 = (f32[6,1,128]{2,1,0:T(1,128)S(1)}, f32[6,1,128]{2,1,0:T(1,128)S(1)}, u32[]{:S(2)}, u32[]{:S(2)}) collective-permute-start(f32[6,1,128]{2,1,0:T(1,128)S(1)} %get-tuple-element.37), channel_id=1, source_target_pairs={{1,0},{2,1},{3,2},{4,3},{5,4},{6,5},{7,6},{9,8},{10,9},{11,10},{12... | collective-permute-start | bytes 9224 | tf_op jit(solution)/shard_map/ppermute | solution.py:28
  186.7 11.8 %collective-permute-start.23 = (f32[6,1,128]{2,1,0:T(1,128)S(1)}, f32[6,1,128]{2,1,0:T(1,128)S(1)}, u32[]{:S(2)}, u32[]{:S(2)}) collective-permute-start(f32[6,1,128]{2,1,0:T(1,128)S(1)} %get-tuple-element.36), channel_id=1, source_target_pairs={{0,1},{1,2},{2,3},{3,4},{4,5},{5,6},{6,7},{8,9},{9,10},{10,11},{11... | collective-permute-start | bytes 9224 | tf_op jit(solution)/shard_map/ppermute | solution.py:25
  190.1 17.1 %collective-permute-start.28 = (f32[1,16,64]{2,1,0:T(8,128)S(1)}, f32[1,16,64]{2,1,0:T(8,128)S(1)}, u32[]{:S(2)}, u32[]{:S(2)}) collective-permute-start(f32[1,16,64]{2,1,0:T(8,128)S(1)} %get-tuple-element.58), channel_id=1, source_target_pairs={{8,0},{16,8},{24,16},{32,24},{40,32},{48,40},{56,48},{64,56},{72,6... | collective-permute-start | bytes 12296 | tf_op jit(solution)/shard_map/ppermute | solution.py:28
  191.4 15.8 %collective-permute-start.29 = (f32[1,16,64]{2,1,0:T(8,128)S(1)}, f32[1,16,64]{2,1,0:T(8,128)S(1)}, u32[]{:S(2)}, u32[]{:S(2)}) collective-permute-start(f32[1,16,64]{2,1,0:T(8,128)S(1)} %get-tuple-element.57), channel_id=1, source_target_pairs={{0,8},{8,16},{16,24},{24,32},{32,40},{40,48},{48,56},{56,64},{64,7... | collective-permute-start | bytes 12296 | tf_op jit(solution)/shard_map/ppermute | solution.py:25
  199.5 26.2 %copy-start.7 = (f32[4,32,128]{2,1,0:T(8,128)}, f32[4,32,128]{2,1,0:T(8,128)S(1)}, u32[]{:S(2)}) copy-start(f32[4,32,128]{2,1,0:T(8,128)S(1)} %fusion.232) | copy-start | bytes 196612
  199.6 13.1 %collective-permute-start.24 = (f32[1,32,128]{2,1,0:T(8,128)S(1)}, f32[1,32,128]{2,1,0:T(8,128)S(1)}, u32[]{:S(2)}, u32[]{:S(2)}) collective-permute-start(f32[1,32,128]{2,1,0:T(8,128)S(1)} %get-tuple-element.41), channel_id=1, source_target_pairs={{8,0},{16,8},{24,16},{32,24},{40,32},{48,40},{56,48},{64,56},{72,6... | collective-permute-start | bytes 49160 | tf_op jit(solution)/shard_map/ppermute | solution.py:28
  200.9 11.8 %collective-permute-start.25 = (f32[1,32,128]{2,1,0:T(8,128)S(1)}, f32[1,32,128]{2,1,0:T(8,128)S(1)}, u32[]{:S(2)}, u32[]{:S(2)}) collective-permute-start(f32[1,32,128]{2,1,0:T(8,128)S(1)} %get-tuple-element.40), channel_id=1, source_target_pairs={{0,8},{8,16},{16,24},{24,32},{32,40},{40,48},{48,56},{56,64},{64,7... | collective-permute-start | bytes 49160 | tf_op jit(solution)/shard_map/ppermute | solution.py:25
  207.3 11.0 %collective-permute-start.30 = (f32[4,1,64]{2,1,0:T(1,128)S(1)}, f32[4,1,64]{2,1,0:T(1,128)S(1)}, u32[]{:S(2)}, u32[]{:S(2)}) collective-permute-start(f32[4,1,64]{2,1,0:T(1,128)S(1)} %get-tuple-element.51), channel_id=1, source_target_pairs={{1,0},{2,1},{3,2},{4,3},{5,4},{6,5},{7,6},{9,8},{10,9},{11,10},{12... | collective-permute-start | bytes 3080 | tf_op jit(solution)/shard_map/ppermute | solution.py:28
  208.6 9.7 %collective-permute-start.31 = (f32[4,1,64]{2,1,0:T(1,128)S(1)}, f32[4,1,64]{2,1,0:T(1,128)S(1)}, u32[]{:S(2)}, u32[]{:S(2)}) collective-permute-start(f32[4,1,64]{2,1,0:T(1,128)S(1)} %get-tuple-element.50), channel_id=1, source_target_pairs={{0,1},{1,2},{2,3},{3,4},{4,5},{5,6},{6,7},{8,9},{9,10},{10,11},{11... | collective-permute-start | bytes 3080 | tf_op jit(solution)/shard_map/ppermute | solution.py:25
  212.7 5.7 %collective-permute-start.26 = (f32[6,1,128]{2,1,0:T(1,128)S(1)}, f32[6,1,128]{2,1,0:T(1,128)S(1)}, u32[]{:S(2)}, u32[]{:S(2)}) collective-permute-start(f32[6,1,128]{2,1,0:T(1,128)S(1)} %get-tuple-element.35), channel_id=1, source_target_pairs={{1,0},{2,1},{3,2},{4,3},{5,4},{6,5},{7,6},{9,8},{10,9},{11,10},{12... | collective-permute-start | bytes 9224 | tf_op jit(solution)/shard_map/ppermute | solution.py:28
  214.0 5.1 %collective-permute-start.27 = (f32[6,1,128]{2,1,0:T(1,128)S(1)}, f32[6,1,128]{2,1,0:T(1,128)S(1)}, u32[]{:S(2)}, u32[]{:S(2)}) collective-permute-start(f32[6,1,128]{2,1,0:T(1,128)S(1)} %get-tuple-element.34), channel_id=1, source_target_pairs={{0,1},{1,2},{2,3},{3,4},{4,5},{5,6},{6,7},{8,9},{9,10},{10,11},{11... | collective-permute-start | bytes 9224 | tf_op jit(solution)/shard_map/ppermute | solution.py:25
  228.4 8.0 %collective-permute-start.32 = (f32[1,16,64]{2,1,0:T(8,128)S(1)}, f32[1,16,64]{2,1,0:T(8,128)S(1)}, u32[]{:S(2)}, u32[]{:S(2)}) collective-permute-start(f32[1,16,64]{2,1,0:T(8,128)S(1)} %get-tuple-element.56), channel_id=1, source_target_pairs={{8,0},{16,8},{24,16},{32,24},{40,32},{48,40},{56,48},{64,56},{72,6... | collective-permute-start | bytes 12296 | tf_op jit(solution)/shard_map/ppermute | solution.py:28
  229.7 8.0 %collective-permute-start.33 = (f32[1,16,64]{2,1,0:T(8,128)S(1)}, f32[1,16,64]{2,1,0:T(8,128)S(1)}, u32[]{:S(2)}, u32[]{:S(2)}) collective-permute-start(f32[1,16,64]{2,1,0:T(8,128)S(1)} %get-tuple-element.55), channel_id=1, source_target_pairs={{0,8},{8,16},{16,24},{24,32},{32,40},{40,48},{48,56},{56,64},{64,7... | collective-permute-start | bytes 12296 | tf_op jit(solution)/shard_map/ppermute | solution.py:25
  237.7 5.0 %collective-permute-start.34 = (f32[4,1,64]{2,1,0:T(1,128)S(1)}, f32[4,1,64]{2,1,0:T(1,128)S(1)}, u32[]{:S(2)}, u32[]{:S(2)}) collective-permute-start(f32[4,1,64]{2,1,0:T(1,128)S(1)} %get-tuple-element.49), channel_id=1, source_target_pairs={{1,0},{2,1},{3,2},{4,3},{5,4},{6,5},{7,6},{9,8},{10,9},{11,10},{12... | collective-permute-start | bytes 3080 | tf_op jit(solution)/shard_map/ppermute | solution.py:28
  239.0 4.1 %collective-permute-start.35 = (f32[4,1,64]{2,1,0:T(1,128)S(1)}, f32[4,1,64]{2,1,0:T(1,128)S(1)}, u32[]{:S(2)}, u32[]{:S(2)}) collective-permute-start(f32[4,1,64]{2,1,0:T(1,128)S(1)} %get-tuple-element.48), channel_id=1, source_target_pairs={{0,1},{1,2},{2,3},{3,4},{4,5},{5,6},{6,7},{8,9},{9,10},{10,11},{11... | collective-permute-start | bytes 3080 | tf_op jit(solution)/shard_map/ppermute | solution.py:25
  243.3 99.7 %copy-start.10 = (f32[2,16,64]{2,1,0:T(8,128)}, f32[2,16,64]{2,1,0:T(8,128)S(1)}, u32[]{:S(2)}) copy-start(f32[2,16,64]{2,1,0:T(8,128)S(1)} %fusion.270) | copy-start | bytes 24580
  243.3 8.3 %collective-permute-start.36 = (f32[1,16,64]{2,1,0:T(8,128)S(1)}, f32[1,16,64]{2,1,0:T(8,128)S(1)}, u32[]{:S(2)}, u32[]{:S(2)}) collective-permute-start(f32[1,16,64]{2,1,0:T(8,128)S(1)} %get-tuple-element.54), channel_id=1, source_target_pairs={{8,0},{16,8},{24,16},{32,24},{40,32},{48,40},{56,48},{64,56},{72,6... | collective-permute-start | bytes 12296 | tf_op jit(solution)/shard_map/ppermute | solution.py:28
  244.6 8.3 %collective-permute-start.37 = (f32[1,16,64]{2,1,0:T(8,128)S(1)}, f32[1,16,64]{2,1,0:T(8,128)S(1)}, u32[]{:S(2)}, u32[]{:S(2)}) collective-permute-start(f32[1,16,64]{2,1,0:T(8,128)S(1)} %get-tuple-element.53), channel_id=1, source_target_pairs={{0,8},{8,16},{16,24},{24,32},{32,40},{40,48},{48,56},{56,64},{64,7... | collective-permute-start | bytes 12296 | tf_op jit(solution)/shard_map/ppermute | solution.py:25
  252.9 55.6 %collective-permute-start.38 = (f32[4,1,64]{2,1,0:T(1,128)S(1)}, f32[4,1,64]{2,1,0:T(1,128)S(1)}, u32[]{:S(2)}, u32[]{:S(2)}) collective-permute-start(f32[4,1,64]{2,1,0:T(1,128)S(1)} %get-tuple-element.47), channel_id=1, source_target_pairs={{1,0},{2,1},{3,2},{4,3},{5,4},{6,5},{7,6},{9,8},{10,9},{11,10},{12... | collective-permute-start | bytes 3080 | tf_op jit(solution)/shard_map/ppermute | solution.py:28
  254.2 54.3 %collective-permute-start.39 = (f32[4,1,64]{2,1,0:T(1,128)S(1)}, f32[4,1,64]{2,1,0:T(1,128)S(1)}, u32[]{:S(2)}, u32[]{:S(2)}) collective-permute-start(f32[4,1,64]{2,1,0:T(1,128)S(1)} %get-tuple-element.46), channel_id=1, source_target_pairs={{0,1},{1,2},{2,3},{3,4},{4,5},{5,6},{6,7},{8,9},{9,10},{10,11},{11... | collective-permute-start | bytes 3080 | tf_op jit(solution)/shard_map/ppermute | solution.py:25
where the time goes:
time: 356 us; the launch traced here: 352 us
  starting transfers between devices  121 us (34%)
  local copies, waits for them, and re-layouts  86.2 us (24%)
  blocking collectives  82.5 us (23%)
  other arithmetic  52 us (15%)
  waiting for transfers between devices  7.29 us (2%)
    ppermute x20, starting transfers between devices, with_halo(): lax.ppermute(lax.slice_in_dim(block, block.shape[dim] - width, None, axis...  95.5 us
    reshape x3, local copies, waits for them, and re-layouts, restrict_field(): field.reshape(sx // 2, 2, sy // 2, 2, sz // 2, 2).sum(axis=(1, 3, 5))  76.1 us
    all_gather x1, blocking collectives, collect_grid(): lax.all_gather(coefficient.reshape(1, -1), ('xb', 'yb'), axis=0, tiled=True)  49.1 us
    all_gather x1, blocking collectives, collect_grid(): lax.all_gather(right_side.reshape(1, -1), ('xb', 'yb'), axis=0, tiled=True)  33.5 us
    reduce_sum x7, other arithmetic, restrict_field(): field.reshape(sx // 2, 2, sy // 2, 2, sz // 2, 2).sum(axis=(1, 3, 5))  30.6 us
    ppermute x20, starting transfers between devices, with_halo(): lax.ppermute(lax.slice_in_dim(block, 0, width, axis=dim), axis, backward)  25.9 us
  transfers between devices with their start and end apart: 40, of which 8 were waited for; matrix products, arithmetic and copies ran while one was open for 19% of the time, Pallas kernels for 0%

commit v1 on v0

--- a/solution.py
+++ b/solution.py
@@ -74,9 +74,24 @@
     return (second, residual)
 
 
+def pair_matrix(count):
+    rows = jnp.arange(count // 2)[:, None]
+    cols = jnp.arange(count)[None, :] // 2
+    return (rows == cols).astype(jnp.float32)
+
+
 def restrict_field(field):
     sx, sy, sz = field.shape
-    return field.reshape(sx // 2, 2, sy // 2, 2, sz // 2, 2).sum(axis=(1, 3, 5)) * 0.125
+    halves = field.reshape(sx // 2, 2, sy, sz)
+    summed = halves[:, 0] + halves[:, 1]
+    summed = jnp.einsum(
+        "xyZ,zZ->xyz", summed, pair_matrix(sz), precision=lax.Precision.HIGHEST
+    )
+    pairs_y = jnp.broadcast_to(pair_matrix(sy), (sx // 2, sy // 2, sy))
+    summed = jnp.einsum(
+        "xyY,xYz->xyz", pairs_y, summed, precision=lax.Precision.HIGHEST
+    )
+    return summed * 0.125
 
 
 def coarse_solve(right_side, coefficient, scale, extend):

time: 356 us -> 241 us (0.68)
  local copies, waits for them, and re-layouts: 86.2 us -> 2.86 us
  other arithmetic: 52 us -> 15.3 us
    reshape x3 -> x0, local copies, waits for them, and re-layouts: 76.1 us -> none  [restrict_field(): field.reshape(sx // 2, 2, sy // 2, 2, sz // 2, 2).sum(axis=(1, 3, 5))]
    reduce_sum x7 -> x0, other arithmetic: 30.6 us -> none  [restrict_field(): field.reshape(sx // 2, 2, sy // 2, 2, sz // 2, 2).sum(axis=(1, 3, 5))]
    mul x1 -> x0, local copies, waits for them, and re-layouts: 5.53 us -> none  [restrict_field(): field.reshape(sx // 2, 2, sy // 2, 2, sz // 2, 2).sum(axis=(1, 3, 5))]
  transfers between devices with their start and end apart: 40 -> 40, of which waited for: 8 -> 10; matrix products, arithmetic and copies ran while one was open for 19% -> 3% of each run, Pallas kernels for 0% -> 0%
where the time goes in v1:
time: 241 us; the launch traced here: 238 us
  starting transfers between devices  123 us (51%)
  blocking collectives  83.8 us (35%)
  other arithmetic  15.3 us (6%)
  waiting for transfers between devices  7.6 us (3%)
  matrix products  3.23 us (1%)
  between operations  3.04 us (1%)
  local copies, waits for them, and re-layouts  2.86 us (1%)
    ppermute x20, starting transfers between devices, with_halo(): lax.ppermute(lax.slice_in_dim(block, block.shape[dim] - width, None, axis...  96.7 us
    all_gather x1, blocking collectives, collect_grid(): lax.all_gather(coefficient.reshape(1, -1), ('xb', 'yb'), axis=0, tiled=True)  48.7 us
    all_gather x1, blocking collectives, collect_grid(): lax.all_gather(right_side.reshape(1, -1), ('xb', 'yb'), axis=0, tiled=True)  35.1 us
    ppermute x20, starting transfers between devices, with_halo(): lax.ppermute(lax.slice_in_dim(block, 0, width, axis=dim), axis, backward)  25.8 us
    ppermute x20, waiting for transfers between devices, with_halo(): lax.ppermute(lax.slice_in_dim(block, block.shape[dim] - width, None, axis...  7.26 us
  transfers between devices with their start and end apart: 40, of which 10 were waited for; matrix products, arithmetic and copies ran while one was open for 3% of the time, Pallas kernels for 0%

profile of v1, /device:TPU:0, one launch (start us, length us, event | category | flops | bytes accessed | tf_op | source)
XLA Modules:
  0.0 238.4 jit_solution(1692704037954307134)
XLA Ops:
  0.6 0.9 fusion.348
  1.6 3.9 %collective-permute-start.1 = (f32[1,64,256]{2,1,0:T(8,128)S(1)}, f32[1,64,256]{2,1,0:T(8,128)S(1)}, u32[]{:S(2)}, u32[]{:S(2)}) collective-permute-start(f32[1,64,256]{2,1,0:T(8,128)S(1)} %get-tuple-element.31), channel_id=1, source_target_pairs={{0,8},{8,16},{16,24},{24,32},{32,40},{40,48},{48,56},{56,64},{64,7... | collective-permute-start | bytes 196616 | tf_op jit(solution)/shard_map/ppermute | solution.py:25
  5.5 1.3 collective-permute-start
  6.8 0.9 fusion.349
  7.7 4.5 %collective-permute-start.5 = (f32[1,64,256]{2,1,0:T(8,128)S(1)}, f32[1,64,256]{2,1,0:T(8,128)S(1)}, u32[]{:S(2)}, u32[]{:S(2)}) collective-permute-start(f32[1,64,256]{2,1,0:T(8,128)S(1)} %get-tuple-element.33), channel_id=1, source_target_pairs={{0,8},{8,16},{16,24},{24,32},{32,40},{40,48},{48,56},{56,64},{64,7... | collective-permute-start | bytes 196616 | tf_op jit(solution)/shard_map/ppermute | solution.py:25
  12.3 1.3 collective-permute-start.4
  13.6 1.4 fusion.217
  15.2 1.3 collective-permute-start.16
  16.8 5.2 %collective-permute-start.17 = (f32[1,32,128]{2,1,0:T(8,128)S(1)}, f32[1,32,128]{2,1,0:T(8,128)S(1)}, u32[]{:S(2)}, u32[]{:S(2)}) collective-permute-start(f32[1,32,128]{2,1,0:T(8,128)S(1)} %get-tuple-element.44), channel_id=1, source_target_pairs={{0,8},{8,16},{16,24},{24,32},{32,40},{40,48},{48,56},{56,64},{64,7... | collective-permute-start | bytes 49160 | tf_op jit(solution)/shard_map/ppermute | solution.py:25
  22.0 1.3 collective-permute-start.2
  23.4 3.0 %collective-permute-start.3 = (f32[10,1,256]{2,1,0:T(1,128)S(1)}, f32[10,1,256]{2,1,0:T(1,128)S(1)}, u32[]{:S(2)}, u32[]{:S(2)}) collective-permute-start(f32[10,1,256]{2,1,0:T(1,128)S(1)} %get-tuple-element.22), channel_id=1, source_target_pairs={{0,1},{1,2},{2,3},{3,4},{4,5},{5,6},{6,7},{8,9},{9,10},{10,11},{11... | collective-permute-start | bytes 30728 | tf_op jit(solution)/shard_map/ppermute | solution.py:25
  26.5 1.3 collective-permute-start.6
  27.8 3.7 %collective-permute-start.7 = (f32[10,1,256]{2,1,0:T(1,128)S(1)}, f32[10,1,256]{2,1,0:T(1,128)S(1)}, u32[]{:S(2)}, u32[]{:S(2)}) collective-permute-start(f32[10,1,256]{2,1,0:T(1,128)S(1)} %get-tuple-element.24), channel_id=1, source_target_pairs={{0,1},{1,2},{2,3},{3,4},{4,5},{5,6},{6,7},{8,9},{9,10},{10,11},{11... | collective-permute-start | bytes 30728 | tf_op jit(solution)/shard_map/ppermute | solution.py:25
  33.0 1.2 fusion.342
  34.2 1.3 collective-permute-start.8
  35.5 4.6 %collective-permute-start.9 = (f32[1,64,256]{2,1,0:T(8,128)S(1)}, f32[1,64,256]{2,1,0:T(8,128)S(1)}, u32[]{:S(2)}, u32[]{:S(2)}) collective-permute-start(f32[1,64,256]{2,1,0:T(8,128)S(1)} %get-tuple-element.28), channel_id=1, source_target_pairs={{0,8},{8,16},{16,24},{24,32},{32,40},{40,48},{48,56},{56,64},{64,7... | collective-permute-start | bytes 196616 | tf_op jit(solution)/shard_map/ppermute | solution.py:25
  40.4 1.6 collective-permute-done.9
  42.0 1.3 collective-permute-start.10
  43.3 3.4 %collective-permute-start.11 = (f32[10,1,256]{2,1,0:T(1,128)S(1)}, f32[10,1,256]{2,1,0:T(1,128)S(1)}, u32[]{:S(2)}, u32[]{:S(2)}) collective-permute-start(f32[10,1,256]{2,1,0:T(1,128)S(1)} %get-tuple-element.20), channel_id=1, source_target_pairs={{0,1},{1,2},{2,3},{3,4},{4,5},{5,6},{6,7},{8,9},{9,10},{10,11},{11... | collective-permute-start | bytes 30728 | tf_op jit(solution)/shard_map/ppermute | solution.py:25
  46.9 0.7 collective-permute-done.11
  48.0 1.2 fusion.181
  49.2 1.3 collective-permute-start.12
  50.5 4.6 %collective-permute-start.13 = (f32[1,64,256]{2,1,0:T(8,128)S(1)}, f32[1,64,256]{2,1,0:T(8,128)S(1)}, u32[]{:S(2)}, u32[]{:S(2)}) collective-permute-start(f32[1,64,256]{2,1,0:T(8,128)S(1)} %get-tuple-element.26), channel_id=1, source_target_pairs={{0,8},{8,16},{16,24},{24,32},{32,40},{40,48},{48,56},{56,64},{64,7... | collective-permute-start | bytes 196616 | tf_op jit(solution)/shard_map/ppermute | solution.py:25
  55.2 1.3 collective-permute-start.18
  56.5 5.4 %collective-permute-start.19 = (f32[6,1,128]{2,1,0:T(1,128)S(1)}, f32[6,1,128]{2,1,0:T(1,128)S(1)}, u32[]{:S(2)}, u32[]{:S(2)}) collective-permute-start(f32[6,1,128]{2,1,0:T(1,128)S(1)} %get-tuple-element.38), channel_id=1, source_target_pairs={{0,1},{1,2},{2,3},{3,4},{4,5},{5,6},{6,7},{8,9},{9,10},{10,11},{11... | collective-permute-start | bytes 9224 | tf_op jit(solution)/shard_map/ppermute | solution.py:25
  62.0 1.3 collective-permute-start.14
  63.3 5.1 %collective-permute-start.15 = (f32[10,1,256]{2,1,0:T(1,128)S(1)}, f32[10,1,256]{2,1,0:T(1,128)S(1)}, u32[]{:S(2)}, u32[]{:S(2)}) collective-permute-start(f32[10,1,256]{2,1,0:T(1,128)S(1)} %get-tuple-element.18), channel_id=1, source_target_pairs={{0,1},{1,2},{2,3},{3,4},{4,5},{5,6},{6,7},{8,9},{9,10},{10,11},{11... | collective-permute-start | bytes 30728 | tf_op jit(solution)/shard_map/ppermute | solution.py:25
  68.6 0.6 collective-permute-done.15
  69.6 1.1 fusion.166
  71.3 1.3 collective-permute-start.20
  72.6 6.1 %collective-permute-start.21 = (f32[1,32,128]{2,1,0:T(8,128)S(1)}, f32[1,32,128]{2,1,0:T(8,128)S(1)}, u32[]{:S(2)}, u32[]{:S(2)}) collective-permute-start(f32[1,32,128]{2,1,0:T(8,128)S(1)} %get-tuple-element.42), channel_id=1, source_target_pairs={{0,8},{8,16},{16,24},{24,32},{32,40},{40,48},{48,56},{56,64},{64,7... | collective-permute-start | bytes 49160 | tf_op jit(solution)/shard_map/ppermute | solution.py:25
  78.8 1.3 collective-permute-start.28
  80.1 6.7 %collective-permute-start.29 = (f32[1,16,64]{2,1,0:T(8,128)S(1)}, f32[1,16,64]{2,1,0:T(8,128)S(1)}, u32[]{:S(2)}, u32[]{:S(2)}) collective-permute-start(f32[1,16,64]{2,1,0:T(8,128)S(1)} %get-tuple-element.56), channel_id=1, source_target_pairs={{0,8},{8,16},{16,24},{24,32},{32,40},{40,48},{48,56},{56,64},{64,7... | collective-permute-start | bytes 12296 | tf_op jit(solution)/shard_map/ppermute | solution.py:25
  86.8 1.3 collective-permute-start.22
  88.1 3.7 %collective-permute-start.23 = (f32[6,1,128]{2,1,0:T(1,128)S(1)}, f32[6,1,128]{2,1,0:T(1,128)S(1)}, u32[]{:S(2)}, u32[]{:S(2)}) collective-permute-start(f32[6,1,128]{2,1,0:T(1,128)S(1)} %get-tuple-element.36), channel_id=1, source_target_pairs={{0,1},{1,2},{2,3},{3,4},{4,5},{5,6},{6,7},{8,9},{9,10},{10,11},{11... | collective-permute-start | bytes 9224 | tf_op jit(solution)/shard_map/ppermute | solution.py:25
  91.9 0.7 collective-permute-done.23
  92.9 1.3 collective-permute-start.24
  94.2 7.0 %collective-permute-start.25 = (f32[1,32,128]{2,1,0:T(8,128)S(1)}, f32[1,32,128]{2,1,0:T(8,128)S(1)}, u32[]{:S(2)}, u32[]{:S(2)}) collective-permute-start(f32[1,32,128]{2,1,0:T(8,128)S(1)} %get-tuple-element.40), channel_id=1, source_target_pairs={{0,8},{8,16},{16,24},{24,32},{32,40},{40,48},{48,56},{56,64},{64,7... | collective-permute-start | bytes 49160 | tf_op jit(solution)/shard_map/ppermute | solution.py:25
  101.3 1.3 collective-permute-start.30
  102.6 5.0 %collective-permute-start.31 = (f32[4,1,64]{2,1,0:T(1,128)S(1)}, f32[4,1,64]{2,1,0:T(1,128)S(1)}, u32[]{:S(2)}, u32[]{:S(2)}) collective-permute-start(f32[4,1,64]{2,1,0:T(1,128)S(1)} %get-tuple-element.50), channel_id=1, source_target_pairs={{0,1},{1,2},{2,3},{3,4},{4,5},{5,6},{6,7},{8,9},{9,10},{10,11},{11... | collective-permute-start | bytes 3080 | tf_op jit(solution)/shard_map/ppermute | solution.py:25
  107.6 1.3 collective-permute-start.26
  108.9 5.1 %collective-permute-start.27 = (f32[6,1,128]{2,1,0:T(1,128)S(1)}, f32[6,1,128]{2,1,0:T(1,128)S(1)}, u32[]{:S(2)}, u32[]{:S(2)}) collective-permute-start(f32[6,1,128]{2,1,0:T(1,128)S(1)} %get-tuple-element.34), channel_id=1, source_target_pairs={{0,1},{1,2},{2,3},{3,4},{4,5},{5,6},{6,7},{8,9},{9,10},{10,11},{11... | collective-permute-start | bytes 9224 | tf_op jit(solution)/shard_map/ppermute | solution.py:25
  114.2 0.7 collective-permute-done.27
  115.5 1.3 collective-permute-start.32
  116.8 6.7 %collective-permute-start.33 = (f32[1,16,64]{2,1,0:T(8,128)S(1)}, f32[1,16,64]{2,1,0:T(8,128)S(1)}, u32[]{:S(2)}, u32[]{:S(2)}) collective-permute-start(f32[1,16,64]{2,1,0:T(8,128)S(1)} %get-tuple-element.54), channel_id=1, source_target_pairs={{0,8},{8,16},{16,24},{24,32},{32,40},{40,48},{48,56},{56,64},{64,7... | collective-permute-start | bytes 12296 | tf_op jit(solution)/shard_map/ppermute | solution.py:25
  123.5 1.3 collective-permute-done.33
  124.8 1.3 collective-permute-start.34
  126.1 3.3 %collective-permute-start.35 = (f32[4,1,64]{2,1,0:T(1,128)S(1)}, f32[4,1,64]{2,1,0:T(1,128)S(1)}, u32[]{:S(2)}, u32[]{:S(2)}) collective-permute-start(f32[4,1,64]{2,1,0:T(1,128)S(1)} %get-tuple-element.48), channel_id=1, source_target_pairs={{0,1},{1,2},{2,3},{3,4},{4,5},{5,6},{6,7},{8,9},{9,10},{10,11},{11... | collective-permute-start | bytes 3080 | tf_op jit(solution)/shard_map/ppermute | solution.py:25
  130.5 1.3 collective-permute-start.36
  131.8 6.7 %collective-permute-start.37 = (f32[1,16,64]{2,1,0:T(8,128)S(1)}, f32[1,16,64]{2,1,0:T(8,128)S(1)}, u32[]{:S(2)}, u32[]{:S(2)}) collective-permute-start(f32[1,16,64]{2,1,0:T(8,128)S(1)} %get-tuple-element.52), channel_id=1, source_target_pairs={{0,8},{8,16},{16,24},{24,32},{32,40},{40,48},{48,56},{56,64},{64,7... | collective-permute-start | bytes 12296 | tf_op jit(solution)/shard_map/ppermute | solution.py:25
  138.4 48.7 %all-gather.1 = f32[128,1,256]{2,1,0:T(1,128)S(1)} all-gather(f32[1,1,256]{2,1,0:T(1,128)S(1)} %reshape.304), channel_id=1, replica_groups=mesh['xb'=16,'yb'=8] {'xb','yb'}, dimensions={0}, use_global_device_ids=true | all-gather | bytes 132096 | tf_op jit(solution)/shard_map/all_gather | solution.py:128
  187.6 1.3 collective-permute-start.38
  188.9 3.0 %collective-permute-start.39 = (f32[4,1,64]{2,1,0:T(1,128)S(1)}, f32[4,1,64]{2,1,0:T(1,128)S(1)}, u32[]{:S(2)}, u32[]{:S(2)}) collective-permute-start(f32[4,1,64]{2,1,0:T(1,128)S(1)} %get-tuple-element.46), channel_id=1, source_target_pairs={{0,1},{1,2},{2,3},{3,4},{4,5},{5,6},{6,7},{8,9},{9,10},{10,11},{11... | collective-permute-start | bytes 3080 | tf_op jit(solution)/shard_map/ppermute | solution.py:25
  192.0 0.8 collective-permute-done.39
  193.3 35.1 %all-gather = f32[128,1,256]{2,1,0:T(1,128)S(1)} all-gather(f32[1,1,256]{2,1,0:T(1,128)S(1)} %reshape.302), channel_id=1, replica_groups=mesh['xb'=16,'yb'=8] {'xb','yb'}, dimensions={0}, use_global_device_ids=true | all-gather | bytes 132096 | tf_op jit(solution)/shard_map/all_gather | solution.py:127
  229.0 1.0 fusion.147
  230.0 0.7 fusion.23
  230.6 0.7 fusion.39
  231.3 0.7 fusion.55
  232.0 0.7 fusion.71
  232.7 0.7 fusion.87
  233.4 0.7 fusion.103
  234.1 0.7 fusion.119
  234.8 1.6 fusion.213
  (110 shorter events, 8.6 us)
Async XLA Ops:
  0.6 21.3 %copy-start = (f32[8,64,256]{2,1,0:T(8,128)S(1)}, f32[8,64,256]{2,1,0:T(8,128)}, u32[]{:S(2)}) copy-start(f32[8,64,256]{2,1,0:T(8,128)} %param.5) | copy-start | bytes 1572868
  1.6 15.2 %collective-permute-start.1 = (f32[1,64,256]{2,1,0:T(8,128)S(1)}, f32[1,64,256]{2,1,0:T(8,128)S(1)}, u32[]{:S(2)}, u32[]{:S(2)}) collective-permute-start(f32[1,64,256]{2,1,0:T(8,128)S(1)} %get-tuple-element.31), channel_id=1, source_target_pairs={{0,8},{8,16},{16,24},{24,32},{32,40},{40,48},{48,56},{56,64},{64,7... | collective-permute-start | bytes 196616 | tf_op jit(solution)/shard_map/ppermute | solution.py:25
  5.5 16.5 %collective-permute-start = (f32[1,64,256]{2,1,0:T(8,128)S(1)}, f32[1,64,256]{2,1,0:T(8,128)S(1)}, u32[]{:S(2)}, u32[]{:S(2)}) collective-permute-start(f32[1,64,256]{2,1,0:T(8,128)S(1)} %get-tuple-element.30), channel_id=1, source_target_pairs={{8,0},{16,8},{24,16},{32,24},{40,32},{48,40},{56,48},{64,56},{72,6... | collective-permute-start | bytes 196616 | tf_op jit(solution)/shard_map/ppermute | solution.py:28
  7.7 15.6 %collective-permute-start.5 = (f32[1,64,256]{2,1,0:T(8,128)S(1)}, f32[1,64,256]{2,1,0:T(8,128)S(1)}, u32[]{:S(2)}, u32[]{:S(2)}) collective-permute-start(f32[1,64,256]{2,1,0:T(8,128)S(1)} %get-tuple-element.33), channel_id=1, source_target_pairs={{0,8},{8,16},{16,24},{24,32},{32,40},{40,48},{48,56},{56,64},{64,7... | collective-permute-start | bytes 196616 | tf_op jit(solution)/shard_map/ppermute | solution.py:25
  12.3 14.2 %collective-permute-start.4 = (f32[1,64,256]{2,1,0:T(8,128)S(1)}, f32[1,64,256]{2,1,0:T(8,128)S(1)}, u32[]{:S(2)}, u32[]{:S(2)}) collective-permute-start(f32[1,64,256]{2,1,0:T(8,128)S(1)} %get-tuple-element.32), channel_id=1, source_target_pairs={{8,0},{16,8},{24,16},{32,24},{40,32},{48,40},{56,48},{64,56},{72,6... | collective-permute-start | bytes 196616 | tf_op jit(solution)/shard_map/ppermute | solution.py:28
  13.6 12.8 %copy-start.3 = (f32[8,64,256]{2,1,0:T(8,128)S(1)}, f32[8,64,256]{2,1,0:T(8,128)}, u32[]{:S(2)}) copy-start(f32[8,64,256]{2,1,0:T(8,128)} %param.3) | copy-start | bytes 1572868
  15.2 39.9 %collective-permute-start.16 = (f32[1,32,128]{2,1,0:T(8,128)S(1)}, f32[1,32,128]{2,1,0:T(8,128)S(1)}, u32[]{:S(2)}, u32[]{:S(2)}) collective-permute-start(f32[1,32,128]{2,1,0:T(8,128)S(1)} %get-tuple-element.45), channel_id=1, source_target_pairs={{8,0},{16,8},{24,16},{32,24},{40,32},{48,40},{56,48},{64,56},{72,6... | collective-permute-start | bytes 49160 | tf_op jit(solution)/shard_map/ppermute | solution.py:28
  16.8 38.4 %collective-permute-start.17 = (f32[1,32,128]{2,1,0:T(8,128)S(1)}, f32[1,32,128]{2,1,0:T(8,128)S(1)}, u32[]{:S(2)}, u32[]{:S(2)}) collective-permute-start(f32[1,32,128]{2,1,0:T(8,128)S(1)} %get-tuple-element.44), channel_id=1, source_target_pairs={{0,8},{8,16},{16,24},{24,32},{32,40},{40,48},{48,56},{56,64},{64,7... | collective-permute-start | bytes 49160 | tf_op jit(solution)/shard_map/ppermute | solution.py:25
  22.0 5.8 %collective-permute-start.2 = (f32[10,1,256]{2,1,0:T(1,128)S(1)}, f32[10,1,256]{2,1,0:T(1,128)S(1)}, u32[]{:S(2)}, u32[]{:S(2)}) collective-permute-start(f32[10,1,256]{2,1,0:T(1,128)S(1)} %get-tuple-element.23), channel_id=1, source_target_pairs={{1,0},{2,1},{3,2},{4,3},{5,4},{6,5},{7,6},{9,8},{10,9},{11,10},{12... | collective-permute-start | bytes 30728 | tf_op jit(solution)/shard_map/ppermute | solution.py:28
  23.4 8.1 %collective-permute-start.3 = (f32[10,1,256]{2,1,0:T(1,128)S(1)}, f32[10,1,256]{2,1,0:T(1,128)S(1)}, u32[]{:S(2)}, u32[]{:S(2)}) collective-permute-start(f32[10,1,256]{2,1,0:T(1,128)S(1)} %get-tuple-element.22), channel_id=1, source_target_pairs={{0,1},{1,2},{2,3},{3,4},{4,5},{5,6},{6,7},{8,9},{9,10},{10,11},{11... | collective-permute-start | bytes 30728 | tf_op jit(solution)/shard_map/ppermute | solution.py:25
  26.5 5.5 %collective-permute-start.6 = (f32[10,1,256]{2,1,0:T(1,128)S(1)}, f32[10,1,256]{2,1,0:T(1,128)S(1)}, u32[]{:S(2)}, u32[]{:S(2)}) collective-permute-start(f32[10,1,256]{2,1,0:T(1,128)S(1)} %get-tuple-element.25), channel_id=1, source_target_pairs={{1,0},{2,1},{3,2},{4,3},{5,4},{6,5},{7,6},{9,8},{10,9},{11,10},{12... | collective-permute-start | bytes 30728 | tf_op jit(solution)/shard_map/ppermute | solution.py:28
  27.8 4.5 %collective-permute-start.7 = (f32[10,1,256]{2,1,0:T(1,128)S(1)}, f32[10,1,256]{2,1,0:T(1,128)S(1)}, u32[]{:S(2)}, u32[]{:S(2)}) collective-permute-start(f32[10,1,256]{2,1,0:T(1,128)S(1)} %get-tuple-element.24), channel_id=1, source_target_pairs={{0,1},{1,2},{2,3},{3,4},{4,5},{5,6},{6,7},{8,9},{9,10},{10,11},{11... | collective-permute-start | bytes 30728 | tf_op jit(solution)/shard_map/ppermute | solution.py:25
  32.0 1.0 copy-start.2
  34.2 6.2 %collective-permute-start.8 = (f32[1,64,256]{2,1,0:T(8,128)S(1)}, f32[1,64,256]{2,1,0:T(8,128)S(1)}, u32[]{:S(2)}, u32[]{:S(2)}) collective-permute-start(f32[1,64,256]{2,1,0:T(8,128)S(1)} %get-tuple-element.29), channel_id=1, source_target_pairs={{8,0},{16,8},{24,16},{32,24},{40,32},{48,40},{56,48},{64,56},{72,6... | collective-permute-start | bytes 196616 | tf_op jit(solution)/shard_map/ppermute | solution.py:28
  35.5 6.4 %collective-permute-start.9 = (f32[1,64,256]{2,1,0:T(8,128)S(1)}, f32[1,64,256]{2,1,0:T(8,128)S(1)}, u32[]{:S(2)}, u32[]{:S(2)}) collective-permute-start(f32[1,64,256]{2,1,0:T(8,128)S(1)} %get-tuple-element.28), channel_id=1, source_target_pairs={{0,8},{8,16},{16,24},{24,32},{32,40},{40,48},{48,56},{56,64},{64,7... | collective-permute-start | bytes 196616 | tf_op jit(solution)/shard_map/ppermute | solution.py:25
  42.0 4.9 %collective-permute-start.10 = (f32[10,1,256]{2,1,0:T(1,128)S(1)}, f32[10,1,256]{2,1,0:T(1,128)S(1)}, u32[]{:S(2)}, u32[]{:S(2)}) collective-permute-start(f32[10,1,256]{2,1,0:T(1,128)S(1)} %get-tuple-element.21), channel_id=1, source_target_pairs={{1,0},{2,1},{3,2},{4,3},{5,4},{6,5},{7,6},{9,8},{10,9},{11,10},{12... | collective-permute-start | bytes 30728 | tf_op jit(solution)/shard_map/ppermute | solution.py:28
  43.3 4.2 %collective-permute-start.11 = (f32[10,1,256]{2,1,0:T(1,128)S(1)}, f32[10,1,256]{2,1,0:T(1,128)S(1)}, u32[]{:S(2)}, u32[]{:S(2)}) collective-permute-start(f32[10,1,256]{2,1,0:T(1,128)S(1)} %get-tuple-element.20), channel_id=1, source_target_pairs={{0,1},{1,2},{2,3},{3,4},{4,5},{5,6},{6,7},{8,9},{9,10},{10,11},{11... | collective-permute-start | bytes 30728 | tf_op jit(solution)/shard_map/ppermute | solution.py:25
  49.2 20.4 %copy-start.1 = (f32[8,64,256]{2,1,0:T(8,128)}, f32[8,64,256]{2,1,0:T(8,128)S(1)}, u32[]{:S(2)}) copy-start(f32[8,64,256]{2,1,0:T(8,128)S(1)} %fusion.181) | copy-start | bytes 1572868
  49.2 12.7 %collective-permute-start.12 = (f32[1,64,256]{2,1,0:T(8,128)S(1)}, f32[1,64,256]{2,1,0:T(8,128)S(1)}, u32[]{:S(2)}, u32[]{:S(2)}) collective-permute-start(f32[1,64,256]{2,1,0:T(8,128)S(1)} %get-tuple-element.27), channel_id=1, source_target_pairs={{8,0},{16,8},{24,16},{32,24},{40,32},{48,40},{56,48},{64,56},{72,6... | collective-permute-start | bytes 196616 | tf_op jit(solution)/shard_map/ppermute | solution.py:28
  50.5 11.4 %collective-permute-start.13 = (f32[1,64,256]{2,1,0:T(8,128)S(1)}, f32[1,64,256]{2,1,0:T(8,128)S(1)}, u32[]{:S(2)}, u32[]{:S(2)}) collective-permute-start(f32[1,64,256]{2,1,0:T(8,128)S(1)} %get-tuple-element.26), channel_id=1, source_target_pairs={{0,8},{8,16},{16,24},{24,32},{32,40},{40,48},{48,56},{56,64},{64,7... | collective-permute-start | bytes 196616 | tf_op jit(solution)/shard_map/ppermute | solution.py:25
  55.2 13.2 %collective-permute-start.18 = (f32[6,1,128]{2,1,0:T(1,128)S(1)}, f32[6,1,128]{2,1,0:T(1,128)S(1)}, u32[]{:S(2)}, u32[]{:S(2)}) collective-permute-start(f32[6,1,128]{2,1,0:T(1,128)S(1)} %get-tuple-element.39), channel_id=1, source_target_pairs={{1,0},{2,1},{3,2},{4,3},{5,4},{6,5},{7,6},{9,8},{10,9},{11,10},{12... | collective-permute-start | bytes 9224 | tf_op jit(solution)/shard_map/ppermute | solution.py:28
  56.5 11.9 %collective-permute-start.19 = (f32[6,1,128]{2,1,0:T(1,128)S(1)}, f32[6,1,128]{2,1,0:T(1,128)S(1)}, u32[]{:S(2)}, u32[]{:S(2)}) collective-permute-start(f32[6,1,128]{2,1,0:T(1,128)S(1)} %get-tuple-element.38), channel_id=1, source_target_pairs={{0,1},{1,2},{2,3},{3,4},{4,5},{5,6},{6,7},{8,9},{9,10},{10,11},{11... | collective-permute-start | bytes 9224 | tf_op jit(solution)/shard_map/ppermute | solution.py:25
  62.0 6.6 %collective-permute-start.14 = (f32[10,1,256]{2,1,0:T(1,128)S(1)}, f32[10,1,256]{2,1,0:T(1,128)S(1)}, u32[]{:S(2)}, u32[]{:S(2)}) collective-permute-start(f32[10,1,256]{2,1,0:T(1,128)S(1)} %get-tuple-element.19), channel_id=1, source_target_pairs={{1,0},{2,1},{3,2},{4,3},{5,4},{6,5},{7,6},{9,8},{10,9},{11,10},{12... | collective-permute-start | bytes 30728 | tf_op jit(solution)/shard_map/ppermute | solution.py:28
  63.3 5.9 %collective-permute-start.15 = (f32[10,1,256]{2,1,0:T(1,128)S(1)}, f32[10,1,256]{2,1,0:T(1,128)S(1)}, u32[]{:S(2)}, u32[]{:S(2)}) collective-permute-start(f32[10,1,256]{2,1,0:T(1,128)S(1)} %get-tuple-element.18), channel_id=1, source_target_pairs={{0,1},{1,2},{2,3},{3,4},{4,5},{5,6},{6,7},{8,9},{9,10},{10,11},{11... | collective-permute-start | bytes 30728 | tf_op jit(solution)/shard_map/ppermute | solution.py:25
  71.3 15.4 %collective-permute-start.20 = (f32[1,32,128]{2,1,0:T(8,128)S(1)}, f32[1,32,128]{2,1,0:T(8,128)S(1)}, u32[]{:S(2)}, u32[]{:S(2)}) collective-permute-start(f32[1,32,128]{2,1,0:T(8,128)S(1)} %get-tuple-element.43), channel_id=1, source_target_pairs={{8,0},{16,8},{24,16},{32,24},{40,32},{48,40},{56,48},{64,56},{72,6... | collective-permute-start | bytes 49160 | tf_op jit(solution)/shard_map/ppermute | solution.py:28
  72.6 14.1 %collective-permute-start.21 = (f32[1,32,128]{2,1,0:T(8,128)S(1)}, f32[1,32,128]{2,1,0:T(8,128)S(1)}, u32[]{:S(2)}, u32[]{:S(2)}) collective-permute-start(f32[1,32,128]{2,1,0:T(8,128)S(1)} %get-tuple-element.42), channel_id=1, source_target_pairs={{0,8},{8,16},{16,24},{24,32},{32,40},{40,48},{48,56},{56,64},{64,7... | collective-permute-start | bytes 49160 | tf_op jit(solution)/shard_map/ppermute | solution.py:25
  78.8 22.5 %collective-permute-start.28 = (f32[1,16,64]{2,1,0:T(8,128)S(1)}, f32[1,16,64]{2,1,0:T(8,128)S(1)}, u32[]{:S(2)}, u32[]{:S(2)}) collective-permute-start(f32[1,16,64]{2,1,0:T(8,128)S(1)} %get-tuple-element.57), channel_id=1, source_target_pairs={{8,0},{16,8},{24,16},{32,24},{40,32},{48,40},{56,48},{64,56},{72,6... | collective-permute-start | bytes 12296 | tf_op jit(solution)/shard_map/ppermute | solution.py:28
  80.1 21.2 %collective-permute-start.29 = (f32[1,16,64]{2,1,0:T(8,128)S(1)}, f32[1,16,64]{2,1,0:T(8,128)S(1)}, u32[]{:S(2)}, u32[]{:S(2)}) collective-permute-start(f32[1,16,64]{2,1,0:T(8,128)S(1)} %get-tuple-element.56), channel_id=1, source_target_pairs={{0,8},{8,16},{16,24},{24,32},{32,40},{40,48},{48,56},{56,64},{64,7... | collective-permute-start | bytes 12296 | tf_op jit(solution)/shard_map/ppermute | solution.py:25
  86.8 5.1 %collective-permute-start.22 = (f32[6,1,128]{2,1,0:T(1,128)S(1)}, f32[6,1,128]{2,1,0:T(1,128)S(1)}, u32[]{:S(2)}, u32[]{:S(2)}) collective-permute-start(f32[6,1,128]{2,1,0:T(1,128)S(1)} %get-tuple-element.37), channel_id=1, source_target_pairs={{1,0},{2,1},{3,2},{4,3},{5,4},{6,5},{7,6},{9,8},{10,9},{11,10},{12... | collective-permute-start | bytes 9224 | tf_op jit(solution)/shard_map/ppermute | solution.py:28
  88.1 4.5 %collective-permute-start.23 = (f32[6,1,128]{2,1,0:T(1,128)S(1)}, f32[6,1,128]{2,1,0:T(1,128)S(1)}, u32[]{:S(2)}, u32[]{:S(2)}) collective-permute-start(f32[6,1,128]{2,1,0:T(1,128)S(1)} %get-tuple-element.36), channel_id=1, source_target_pairs={{0,1},{1,2},{2,3},{3,4},{4,5},{5,6},{6,7},{8,9},{9,10},{10,11},{11... | collective-permute-start | bytes 9224 | tf_op jit(solution)/shard_map/ppermute | solution.py:25
  92.9 94.5 %copy-start.4 = (f32[4,32,128]{2,1,0:T(8,128)}, f32[4,32,128]{2,1,0:T(8,128)S(1)}, u32[]{:S(2)}) copy-start(f32[4,32,128]{2,1,0:T(8,128)S(1)} %fusion.243) | copy-start | bytes 196612
  92.9 14.7 %collective-permute-start.24 = (f32[1,32,128]{2,1,0:T(8,128)S(1)}, f32[1,32,128]{2,1,0:T(8,128)S(1)}, u32[]{:S(2)}, u32[]{:S(2)}) collective-permute-start(f32[1,32,128]{2,1,0:T(8,128)S(1)} %get-tuple-element.41), channel_id=1, source_target_pairs={{8,0},{16,8},{24,16},{32,24},{40,32},{48,40},{56,48},{64,56},{72,6... | collective-permute-start | bytes 49160 | tf_op jit(solution)/shard_map/ppermute | solution.py:28
  94.2 13.4 %collective-permute-start.25 = (f32[1,32,128]{2,1,0:T(8,128)S(1)}, f32[1,32,128]{2,1,0:T(8,128)S(1)}, u32[]{:S(2)}, u32[]{:S(2)}) collective-permute-start(f32[1,32,128]{2,1,0:T(8,128)S(1)} %get-tuple-element.40), channel_id=1, source_target_pairs={{0,8},{8,16},{16,24},{24,32},{32,40},{40,48},{48,56},{56,64},{64,7... | collective-permute-start | bytes 49160 | tf_op jit(solution)/shard_map/ppermute | solution.py:25
  101.3 12.8 %collective-permute-start.30 = (f32[4,1,64]{2,1,0:T(1,128)S(1)}, f32[4,1,64]{2,1,0:T(1,128)S(1)}, u32[]{:S(2)}, u32[]{:S(2)}) collective-permute-start(f32[4,1,64]{2,1,0:T(1,128)S(1)} %get-tuple-element.51), channel_id=1, source_target_pairs={{1,0},{2,1},{3,2},{4,3},{5,4},{6,5},{7,6},{9,8},{10,9},{11,10},{12... | collective-permute-start | bytes 3080 | tf_op jit(solution)/shard_map/ppermute | solution.py:28
  102.6 11.5 %collective-permute-start.31 = (f32[4,1,64]{2,1,0:T(1,128)S(1)}, f32[4,1,64]{2,1,0:T(1,128)S(1)}, u32[]{:S(2)}, u32[]{:S(2)}) collective-permute-start(f32[4,1,64]{2,1,0:T(1,128)S(1)} %get-tuple-element.50), channel_id=1, source_target_pairs={{0,1},{1,2},{2,3},{3,4},{4,5},{5,6},{6,7},{8,9},{9,10},{10,11},{11... | collective-permute-start | bytes 3080 | tf_op jit(solution)/shard_map/ppermute | solution.py:25
  107.6 6.5 %collective-permute-start.26 = (f32[6,1,128]{2,1,0:T(1,128)S(1)}, f32[6,1,128]{2,1,0:T(1,128)S(1)}, u32[]{:S(2)}, u32[]{:S(2)}) collective-permute-start(f32[6,1,128]{2,1,0:T(1,128)S(1)} %get-tuple-element.35), channel_id=1, source_target_pairs={{1,0},{2,1},{3,2},{4,3},{5,4},{6,5},{7,6},{9,8},{10,9},{11,10},{12... | collective-permute-start | bytes 9224 | tf_op jit(solution)/shard_map/ppermute | solution.py:28
  108.9 5.9 %collective-permute-start.27 = (f32[6,1,128]{2,1,0:T(1,128)S(1)}, f32[6,1,128]{2,1,0:T(1,128)S(1)}, u32[]{:S(2)}, u32[]{:S(2)}) collective-permute-start(f32[6,1,128]{2,1,0:T(1,128)S(1)} %get-tuple-element.34), channel_id=1, source_target_pairs={{0,1},{1,2},{2,3},{3,4},{4,5},{5,6},{6,7},{8,9},{9,10},{10,11},{11... | collective-permute-start | bytes 9224 | tf_op jit(solution)/shard_map/ppermute | solution.py:25
  115.5 8.0 %collective-permute-start.32 = (f32[1,16,64]{2,1,0:T(8,128)S(1)}, f32[1,16,64]{2,1,0:T(8,128)S(1)}, u32[]{:S(2)}, u32[]{:S(2)}) collective-permute-start(f32[1,16,64]{2,1,0:T(8,128)S(1)} %get-tuple-element.55), channel_id=1, source_target_pairs={{8,0},{16,8},{24,16},{32,24},{40,32},{48,40},{56,48},{64,56},{72,6... | collective-permute-start | bytes 12296 | tf_op jit(solution)/shard_map/ppermute | solution.py:28
  116.8 8.0 %collective-permute-start.33 = (f32[1,16,64]{2,1,0:T(8,128)S(1)}, f32[1,16,64]{2,1,0:T(8,128)S(1)}, u32[]{:S(2)}, u32[]{:S(2)}) collective-permute-start(f32[1,16,64]{2,1,0:T(8,128)S(1)} %get-tuple-element.54), channel_id=1, source_target_pairs={{0,8},{8,16},{16,24},{24,32},{32,40},{40,48},{48,56},{56,64},{64,7... | collective-permute-start | bytes 12296 | tf_op jit(solution)/shard_map/ppermute | solution.py:25
  124.8 4.8 %collective-permute-start.34 = (f32[4,1,64]{2,1,0:T(1,128)S(1)}, f32[4,1,64]{2,1,0:T(1,128)S(1)}, u32[]{:S(2)}, u32[]{:S(2)}) collective-permute-start(f32[4,1,64]{2,1,0:T(1,128)S(1)} %get-tuple-element.49), channel_id=1, source_target_pairs={{1,0},{2,1},{3,2},{4,3},{5,4},{6,5},{7,6},{9,8},{10,9},{11,10},{12... | collective-permute-start | bytes 3080 | tf_op jit(solution)/shard_map/ppermute | solution.py:28
  126.1 4.1 %collective-permute-start.35 = (f32[4,1,64]{2,1,0:T(1,128)S(1)}, f32[4,1,64]{2,1,0:T(1,128)S(1)}, u32[]{:S(2)}, u32[]{:S(2)}) collective-permute-start(f32[4,1,64]{2,1,0:T(1,128)S(1)} %get-tuple-element.48), channel_id=1, source_target_pairs={{0,1},{1,2},{2,3},{3,4},{4,5},{5,6},{6,7},{8,9},{9,10},{10,11},{11... | collective-permute-start | bytes 3080 | tf_op jit(solution)/shard_map/ppermute | solution.py:25
  130.4 98.5 %copy-start.5 = (f32[2,16,64]{2,1,0:T(8,128)}, f32[2,16,64]{2,1,0:T(8,128)S(1)}, u32[]{:S(2)}) copy-start(f32[2,16,64]{2,1,0:T(8,128)S(1)} %fusion.296) | copy-start | bytes 24580
  130.5 57.1 %collective-permute-start.36 = (f32[1,16,64]{2,1,0:T(8,128)S(1)}, f32[1,16,64]{2,1,0:T(8,128)S(1)}, u32[]{:S(2)}, u32[]{:S(2)}) collective-permute-start(f32[1,16,64]{2,1,0:T(8,128)S(1)} %get-tuple-element.53), channel_id=1, source_target_pairs={{8,0},{16,8},{24,16},{32,24},{40,32},{48,40},{56,48},{64,56},{72,6... | collective-permute-start | bytes 12296 | tf_op jit(solution)/shard_map/ppermute | solution.py:28
  131.8 55.8 %collective-permute-start.37 = (f32[1,16,64]{2,1,0:T(8,128)S(1)}, f32[1,16,64]{2,1,0:T(8,128)S(1)}, u32[]{:S(2)}, u32[]{:S(2)}) collective-permute-start(f32[1,16,64]{2,1,0:T(8,128)S(1)} %get-tuple-element.52), channel_id=1, source_target_pairs={{0,8},{8,16},{16,24},{24,32},{32,40},{40,48},{48,56},{56,64},{64,7... | collective-permute-start | bytes 12296 | tf_op jit(solution)/shard_map/ppermute | solution.py:25
  187.6 4.3 %collective-permute-start.38 = (f32[4,1,64]{2,1,0:T(1,128)S(1)}, f32[4,1,64]{2,1,0:T(1,128)S(1)}, u32[]{:S(2)}, u32[]{:S(2)}) collective-permute-start(f32[4,1,64]{2,1,0:T(1,128)S(1)} %get-tuple-element.47), channel_id=1, source_target_pairs={{1,0},{2,1},{3,2},{4,3},{5,4},{6,5},{7,6},{9,8},{10,9},{11,10},{12... | collective-permute-start | bytes 3080 | tf_op jit(solution)/shard_map/ppermute | solution.py:28
  188.9 3.8 %collective-permute-start.39 = (f32[4,1,64]{2,1,0:T(1,128)S(1)}, f32[4,1,64]{2,1,0:T(1,128)S(1)}, u32[]{:S(2)}, u32[]{:S(2)}) collective-permute-start(f32[4,1,64]{2,1,0:T(1,128)S(1)} %get-tuple-element.46), channel_id=1, source_target_pairs={{0,1},{1,2},{2,3},{3,4},{4,5},{5,6},{6,7},{8,9},{9,10},{10,11},{11... | collective-permute-start | bytes 3080 | tf_op jit(solution)/shard_map/ppermute | solution.py:25

commit v2 on v1

--- a/solution.py
+++ b/solution.py
@@ -17,17 +17,66 @@
 jacobi_weight = 0.8
 
 
-def with_halo(block, sides, width):
-    for axis, dim in sides:
-        count = lax.axis_size(axis)
-        forward = [(i, i + 1) for i in range(count - 1)]
-        backward = [(target, source) for source, target in forward]
-        low = lax.ppermute(
-            lax.slice_in_dim(block, block.shape[dim] - width, None, axis=dim), axis, forward
-        )
-        high = lax.ppermute(lax.slice_in_dim(block, 0, width, axis=dim), axis, backward)
-        block = jnp.concatenate([low, block, high], axis=dim)
-    return block
+def exchange(items, axis, dim):
+    count = lax.axis_size(axis)
+    low = [[] for _ in items]
+    high = [[] for _ in items]
+    reach = max(-(-width // block.shape[dim]) for block, width in items)
+    for hop in range(1, reach + 1):
+        for sign in (1, -1):
+            pieces = []
+            for block, width in items:
+                size = block.shape[dim]
+                rows = min(size, width - (hop - 1) * size)
+                if rows <= 0:
+                    pieces.append(None)
+                elif sign == 1:
+                    pieces.append(lax.slice_in_dim(block, size - rows, size, axis=dim))
+                else:
+                    pieces.append(lax.slice_in_dim(block, 0, rows, axis=dim))
+            flat = jnp.concatenate([p.reshape(-1) for p in pieces if p is not None])
+            if sign == 1:
+                pairs = [(i, i + hop) for i in range(count - hop)]
+            else:
+                pairs = [(i + hop, i) for i in range(count - hop)]
+            got = lax.ppermute(flat, axis, pairs)
+            offset = 0
+            for index, piece in enumerate(pieces):
+                if piece is None:
+                    continue
+                part = got[offset : offset + piece.size].reshape(piece.shape)
+                offset += piece.size
+                if sign == 1:
+                    low[index].insert(0, part)
+                else:
+                    high[index].append(part)
+    return [
+        jnp.concatenate(low[i] + [block] + high[i], axis=dim)
+        for i, (block, width) in enumerate(items)
+    ]
+
+
+def exchange_xy(items):
+    widths = [width for _, width in items]
+    extended = exchange(items, "xb", 0)
+    return exchange(list(zip(extended, widths)), "yb", 1)
+
+
+def inside_mask(shape, halo):
+    sx, sy, _ = shape
+    gx = lax.axis_index("xb") * sx - halo + jnp.arange(sx + 2 * halo)
+    gy = lax.axis_index("yb") * sy - halo + jnp.arange(sy + 2 * halo)
+    in_x = (gx >= 0) & (gx < sx * lax.axis_size("xb"))
+    in_y = (gy >= 0) & (gy < sy * lax.axis_size("yb"))
+    return in_x[:, None, None] & in_y[None, :, None]
+
+
+def pad_z(box):
+    return jnp.pad(box, ((0, 0), (0, 0), (1, 1)))
+
+
+def trim(box):
+    return box[1:-1, 1:-1, :]
 
 
 def neighbours(padded):
@@ -57,9 +106,8 @@
     return result
 
 
-def smooth_level(start, right_side, coefficient, scale, extend, padded_coef=None):
-    padded_coef = extend(coefficient)
-    weights, diagonal = face_weights(padded_coef, scale)
+def smooth_level(start, right_side, coefficient, scale, extend):
+    weights, diagonal = face_weights(extend(coefficient), scale)
     if start is None:
         start = jnp.zeros_like(right_side)
         residual = right_side
@@ -114,25 +162,41 @@
     return jnp.pad(field, 1)
 
 
-def extend_local(field):
-    padded = with_halo(field, (("xb", 0), ("yb", 1)), 1)
-    return jnp.pad(padded, ((0, 0), (0, 0), (1, 1)))
+def smooth_box(start, right_side, coefficient, scale, shape):
+    weights, diagonal = face_weights(pad_z(coefficient), scale)
+    if start is None:
+        start = jnp.zeros_like(right_side)
+        residual = right_side
+    else:
+        residual = right_side - apply_operator(pad_z(start), trim(start), weights, diagonal)
+        start = trim(start)
+    first_step = residual / (cheb_theta * diagonal)
+    first = jnp.where(inside_mask(shape, 2), start + first_step, 0.0)
+    weights = [trim(w) for w in weights]
+    diagonal = trim(diagonal)
+    right_side = trim(right_side)
+    residual = right_side - apply_operator(pad_z(first), trim(first), weights, diagonal)
+    second_step = cheb_carry * trim(first_step) + cheb_resid * residual / diagonal
+    second = jnp.where(inside_mask(shape, 1), trim(first) + second_step, 0.0)
+    weights = [trim(w) for w in weights]
+    diagonal = trim(diagonal)
+    residual = trim(right_side) - apply_operator(pad_z(second), trim(second), weights, diagonal)
+    return (trim(second), residual)
 
 
 def collect_grid(right_side, coefficient):
     sx, sy, sz = right_side.shape
     count_x = lax.axis_size("xb")
     count_y = lax.axis_size("yb")
-    flat = (
-        lax.all_gather(right_side.reshape(1, -1), ("xb", "yb"), axis=0, tiled=True),
-        lax.all_gather(coefficient.reshape(1, -1), ("xb", "yb"), axis=0, tiled=True),
-    )
+    flat = jnp.concatenate([right_side.reshape(1, -1), coefficient.reshape(1, -1)], axis=1)
+    both = lax.all_gather(flat, ("xb", "yb"), axis=0, tiled=True)
+    size = sx * sy * sz
     return tuple(
         (
             piece.reshape(count_x, count_y, sx, sy, sz)
             .transpose(0, 2, 1, 3, 4)
             .reshape(count_x * sx, count_y * sy, sz)
-            for piece in flat
+            for piece in (both[:, :size], both[:, size:])
         )
     )
 
@@ -144,14 +208,18 @@
 
 
 def per_device(initial_guess, right_side, coefficient):
-    fine, fine_res = smooth_level(initial_guess, right_side, coefficient, 1.0, extend_local, None)
     mid_coef = restrict_field(coefficient)
-    middle, mid_res = smooth_level(
-        None, restrict_field(fine_res), mid_coef, 0.25, extend_local, None
-    )
     low_coef = restrict_field(mid_coef)
+    guess_b, rhs_b, coef_b, mid_coef_b, low_coef_b = exchange_xy(
+        [(initial_guess, 3), (right_side, 2), (coefficient, 3), (mid_coef, 3), (low_coef, 3)]
+    )
+    fine, fine_res = smooth_box(guess_b, rhs_b, coef_b, 1.0, right_side.shape)
+    mid_rhs = restrict_field(fine_res)
+    (mid_rhs_b,) = exchange_xy([(mid_rhs, 2)])
+    middle, mid_res = smooth_box(None, mid_rhs_b, mid_coef_b, 0.25, mid_rhs.shape)
     low_rhs = restrict_field(mid_res)
-    lower, low_res = smooth_level(None, low_rhs, low_coef, 0.0625, extend_local, None)
+    (low_rhs_b,) = exchange_xy([(low_rhs, 2)])
+    lower, low_res = smooth_box(None, low_rhs_b, low_coef_b, 0.0625, low_rhs.shape)
     coarse_rhs, coarse_coef = collect_grid(restrict_field(low_res), restrict_field(low_coef))
     coarse_whole = coarse_solve(coarse_rhs, coarse_coef, 0.015625, extend_all)
     sx, sy, sz = right_side.shape

time: 241 us -> 153 us (0.63)
  starting transfers between devices: 123 us -> 36.5 us
  blocking collectives: 83.8 us -> 38.6 us
  local copies, waits for them, and re-layouts: 2.86 us -> 27.1 us
  waiting for transfers between devices: 7.6 us -> 17.4 us
  other arithmetic: 15.3 us -> 24.2 us
    ppermute x40 -> x14, starting transfers between devices: 123 us -> 36.5 us  [exchange(): got = lax.ppermute(flat, axis, pairs)]
    all_gather x2 -> x1, blocking collectives: 83.8 us -> 38.6 us  [collect_grid(): both = lax.all_gather(flat, ('xb', 'yb'), axis=0, tiled=True)]
    slice x12 -> x37, local copies, waits for them, and re-layouts: 1.9 us -> 12.7 us  [the longest x27 10.8 us: exchange(): part = got[offset:offset + piece.size].reshape(piece.shape)]
    ppermute x40 -> x14, waiting for transfers between devices: 7.6 us -> 17.4 us  [exchange(): got = lax.ppermute(flat, axis, pairs)]
    unnamed x18 -> x139, local copies, waits for them, and re-layouts: 0.53 us -> 7.57 us
    reshape x0 -> x34, local copies, waits for them, and re-layouts: none -> 5.82 us  [the longest x18 4.33 us: exchange(): part = got[offset:offset + piece.size].reshape(piece.shape)]
    select_n x0 -> x6, other arithmetic: none -> 5.31 us  [the longest x3 3.1 us: smooth_box(): first = jnp.where(inside_mask(shape, 2), start + first_step, 0.0)]
    and x0 -> x18, other arithmetic: none -> 3.96 us  [the longest x6 3.33 us: inside_mask(): return in_x[:, None, None] & in_y[None, :, None]]
  transfers between devices with their start and end apart: 40 -> 14, of which waited for: 10 -> 6; matrix products, arithmetic and copies ran while one was open for 3% -> 6% of each run, Pallas kernels for 0% -> 0%
where the time goes in v2:
time: 153 us; the launch traced here: 151 us
  blocking collectives  38.6 us (25%)
  starting transfers between devices  36.5 us (24%)
  local copies, waits for them, and re-layouts  27.1 us (18%)
  other arithmetic  24.2 us (16%)
  waiting for transfers between devices  17.4 us (11%)
  matrix products  3.77 us (2%)
  between operations  3.3 us (2%)
    all_gather x1, blocking collectives, collect_grid(): both = lax.all_gather(flat, ('xb', 'yb'), axis=0, tiled=True)  38.6 us
    ppermute x14, starting transfers between devices, exchange(): got = lax.ppermute(flat, axis, pairs)  36.5 us
    ppermute x14, waiting for transfers between devices, exchange(): got = lax.ppermute(flat, axis, pairs)  17.4 us
    slice x27, local copies, waits for them, and re-layouts, exchange(): part = got[offset:offset + piece.size].reshape(piece.shape)  10.8 us
    unnamed x139, local copies, waits for them, and re-layouts  7.57 us
    add x7, other arithmetic, coarse_solve(): field + jacobi_weight * (right_side - apply_operator(extend(field), field...  4.78 us
    reshape x18, local copies, waits for them, and re-layouts, exchange(): part = got[offset:offset + piece.size].reshape(piece.shape)  4.33 us
    and x6, other arithmetic, inside_mask(): return in_x[:, None, None] & in_y[None, :, None]  3.33 us
  transfers between devices with their start and end apart: 14, of which 6 were waited for; matrix products, arithmetic and copies ran while one was open for 6% of the time, Pallas kernels for 0%

profile of v2, /device:TPU:0, one launch (start us, length us, event | category | flops | bytes accessed | tf_op | source)
XLA Modules:
  0.0 150.9 jit_solution(8204271768333074912)
XLA Ops:
  0.7 1.1 fusion.343
  1.9 1.3 fusion.213
  3.6 0.7 constant_dynamic-update-slice_fusion
  5.3 0.7 constant_dynamic-update-slice_fusion.24
  5.9 0.7 constant_dynamic-update-slice_fusion.22
  7.9 0.8 copy-done.33
  8.7 4.0 %collective-permute-start = (f32[145408]{0:T(1024)}, f32[145408]{0:T(1024)S(1)}, u32[]{:S(2)}, u32[]{:S(2)}) collective-permute-start(f32[145408]{0:T(1024)} %get-tuple-element.86), channel_id=1, source_target_pairs={{0,8},{8,16},{16,24},{24,32},{32,40},{40,48},{48,56},{56,64},{64,7... | collective-permute-start | bytes 1744904 | tf_op jit(solution)/shard_map/ppermute | solution.py:42
  12.7 1.3 collective-permute-start.1
  14.1 6.5 %collective-permute-start.2 = (f32[1024]{0:T(1024)S(1)}, f32[1024]{0:T(1024)S(1)}, u32[]{:S(2)}, u32[]{:S(2)}) collective-permute-start(f32[1024]{0:T(1024)S(1)} %reshape.837), channel_id=1, source_target_pairs={{0,16},{8,24},{16,32},{24,40},{32,48},{40,56},{48,64},{56,72},{64,... | collective-permute-start | bytes 12296 | tf_op jit(solution)/shard_map/ppermute | solution.py:42
  20.6 1.3 collective-permute-start.3
  22.2 0.7 broadcast_and_fusion
  22.9 0.6 broadcast_and_fusion.1
  24.1 0.7 broadcast_and_fusion.4
  24.8 0.7 broadcast_and_fusion.2
  25.4 0.7 convolution_multiply_fusion.4
  26.8 2.6 %collective-permute-done.3 = f32[1024]{0:T(1024)S(1)} collective-permute-done((f32[1024]{0:T(1024)S(1)}, f32[1024]{0:T(1024)S(1)}, u32[]{:S(2)}, u32[]{:S(2)}) %collective-permute-start.3) | collective-permute-done | bytes 4128 | tf_op jit(solution)/shard_map/ppermute | solution.py:42
  29.4 0.7 reshape.842
  30.7 0.8 copy-done.14
  31.6 0.7 fusion.341
  32.4 0.7 fusion.340
  33.9 0.8 slice-done
  35.0 0.8 copy-done.11
  36.0 0.8 slice.1170
  37.3 1.3 collective-permute-start.4
  38.9 1.3 collective-permute-start.5
  40.2 0.7 fusion.347
  40.9 3.0 %collective-permute-done.5 = f32[33024]{0:T(1024)S(1)} collective-permute-done((f32[33024]{0:T(1024)S(1)}, f32[33024]{0:T(1024)S(1)}, u32[]{:S(2)}, u32[]{:S(2)}) %collective-permute-start.5) | collective-permute-done | bytes 132128 | tf_op jit(solution)/shard_map/ppermute | solution.py:42
  43.8 0.7 fusion.348
  44.7 2.4 %add_add_fusion = (f32[12,68,256]{2,1,0:T(8,128)}, f32[12,68,256]{2,1,0:T(8,128)S(1)}, f32[12,68,256]{2,1,0:T(8,128)S(1)}, f32[12,68,256]{2,1,0:T(8,128)S(1)}, f...) fusion(f32[14,70,256]{2,1,0:T(8,128)S(1)} %pad_maximum_fusion.1), kind=kLoop, calls=%fused_computation.56 | loop fusion | flops 3760128 | bytes 11304960 | tf_op jit(solution)/shard_map/add | solution.py:98
  47.1 1.4 slice.935
  48.5 1.4 slice.942
  50.0 1.3 slice.1184
  51.3 1.4 reshape.849
  52.7 1.3 slice.1185
  54.0 1.3 reshape.850
  55.4 1.4 pad_maximum_fusion
  57.1 2.8 %add_select_fusion = (f32[12,68,256]{2,1,0:T(8,128)S(1)}, f32[12,68,256]{2,1,0:T(8,128)S(1)}, f32[12,68,256]{2,1,0:T(8,128)S(1)}) fusion(f32[14,70,256]{2,1,0:T(8,128)S(1)} %pad_maximum_fusion, pred[12,68]{1,0:T(8,128)(4,1)S(1)} %copy-done.37, f32[12,68,256]{2,1,0:T(8,128)S(1)} %copy-done, f32[12,68,256]{2,1,0:T(8,128)S(1)} %copy-done.1, ...), kind=kLoop, calls=%fused_computation.55 | loop fusion | flops 5431296 | bytes 14108672 | tf_op jit(solution)/shard_map/jit(_where)/select_n | solution.py:174
  59.9 1.8 %fusion.31 = f32[10,66,256]{2,1,0:T(8,128)S(1)} fusion(f32[12,68,256]{2,1,0:T(8,128)S(1)} %get-tuple-element.44, f32[12,68,256]{2,1,0:T(8,128)S(1)} %copy-done, f32[12,68,256]{2,1,0:T(8,128)S(1)} %copy-done.1, f32[12,68,256]{2,1,0:T(8,128)S(1)} %get-tuple-element.41, f32[12,68,256]{2,1,0:T(8,128)S(1)} %get-tuple-element.40, ...), kind=kLoop, calls=%fused_computation.129 | loop fusion | flops 3379200 | bytes 11884544 | tf_op jit(solution)/shard_map/jit(_where)/select_n | solution.py:180
  61.8 1.6 %fusion.172 = (f32[8,64,256]{2,1,0:T(8,128)S(1)}, f32[8,64,256]{2,1,0:T(8,128)}) fusion(f32[8,64,256]{2,1,0:T(8,128)S(1)} %copy-done.4, f32[10,66,256]{2,1,0:T(8,128)S(1)} %fusion.31, f32[12,68,256]{2,1,0:T(8,128)S(1)} %copy-done, f32[12,68,256]{2,1,0:T(8,128)S(1)} %copy-done.1, f32[12,68,256]{2,1,0:T(8,128)S(1)} %get-tuple-element.41, ...), kind=kLoop, calls=%fused_computation.270 | loop fusion | flops 1835008 | bytes 8601600 | tf_op jit(solution)/shard_map/sub | solution.py:183
  64.0 5.0 %collective-permute-start.6 = (f32[8192]{0:T(1024)S(1)}, f32[8192]{0:T(1024)S(1)}, u32[]{:S(2)}, u32[]{:S(2)}) collective-permute-start(f32[8192]{0:T(1024)S(1)} %bitcast.153), channel_id=1, source_target_pairs={{0,8},{8,16},{16,24},{24,32},{32,40},{40,48},{48,56},{56,64},{64,7... | collective-permute-start | bytes 98312 | tf_op jit(solution)/shard_map/ppermute | solution.py:42
  69.0 1.3 collective-permute-start.7
  70.3 0.7 slice.1228
  71.0 3.7 %collective-permute-done.7 = f32[8192]{0:T(1024)S(1)} collective-permute-done((f32[8192]{0:T(1024)S(1)}, f32[8192]{0:T(1024)S(1)}, u32[]{:S(2)}, u32[]{:S(2)}) %collective-permute-start.7) | collective-permute-done | bytes 32800 | tf_op jit(solution)/shard_map/ppermute | solution.py:42
  74.8 4.2 %collective-permute-start.8 = (f32[2048]{0:T(1024)S(1)}, f32[2048]{0:T(1024)S(1)}, u32[]{:S(2)}, u32[]{:S(2)}) collective-permute-start(f32[2048]{0:T(1024)S(1)} %bitcast.157), channel_id=1, source_target_pairs={{0,1},{1,2},{2,3},{3,4},{4,5},{5,6},{6,7},{8,9},{9,10},{10,11},{11... | collective-permute-start | bytes 24584 | tf_op jit(solution)/shard_map/ppermute | solution.py:42
  79.0 1.3 collective-permute-start.9
  80.4 2.4 %collective-permute-done.9 = f32[2048]{0:T(1024)S(1)} collective-permute-done((f32[2048]{0:T(1024)S(1)}, f32[2048]{0:T(1024)S(1)}, u32[]{:S(2)}, u32[]{:S(2)}) %collective-permute-start.9) | collective-permute-done | bytes 8224 | tf_op jit(solution)/shard_map/ppermute | solution.py:42
  83.7 0.7 fusion.251
  84.8 3.8 %collective-permute-start.10 = (f32[2048]{0:T(1024)S(1)}, f32[2048]{0:T(1024)S(1)}, u32[]{:S(2)}, u32[]{:S(2)}) collective-permute-start(f32[2048]{0:T(1024)S(1)} %reshape.861), channel_id=1, source_target_pairs={{0,8},{8,16},{16,24},{24,32},{32,40},{40,48},{48,56},{56,64},{64,7... | collective-permute-start | bytes 24584 | tf_op jit(solution)/shard_map/ppermute | solution.py:42
  88.6 1.3 collective-permute-start.11
  90.2 0.7 slice.1263
  91.0 3.1 %collective-permute-done.11 = f32[2048]{0:T(1024)S(1)} collective-permute-done((f32[2048]{0:T(1024)S(1)}, f32[2048]{0:T(1024)S(1)}, u32[]{:S(2)}, u32[]{:S(2)}) %collective-permute-start.11) | collective-permute-done | bytes 8224 | tf_op jit(solution)/shard_map/ppermute | solution.py:42
  94.3 2.9 %collective-permute-start.12 = (f32[768]{0:T(1024)S(1)}, f32[768]{0:T(1024)S(1)}, u32[]{:S(2)}, u32[]{:S(2)}) collective-permute-start(f32[768]{0:T(1024)S(1)} %reshape.864), channel_id=1, source_target_pairs={{0,1},{1,2},{2,3},{3,4},{4,5},{5,6},{6,7},{8,9},{9,10},{10,11},{11... | collective-permute-start | bytes 9224 | tf_op jit(solution)/shard_map/ppermute | solution.py:42
  97.3 1.3 collective-permute-start.13
  98.7 2.6 %collective-permute-done.13 = f32[768]{0:T(1024)S(1)} collective-permute-done((f32[768]{0:T(1024)S(1)}, f32[768]{0:T(1024)S(1)}, u32[]{:S(2)}, u32[]{:S(2)}) %collective-permute-start.13) | collective-permute-done | bytes 3104 | tf_op jit(solution)/shard_map/ppermute | solution.py:42
  102.6 38.6 %all-gather = f32[128,1,512]{2,1,0:T(1,128)S(1)} all-gather(f32[1,1,512]{2,1,0:T(1,128)S(1)} %maximum_bitcast_fusion), channel_id=1, replica_groups=mesh['xb'=16,'yb'=8] {'xb','yb'}, dimensions={0}, use_global_device_ids=true | all-gather | bytes 264192 | tf_op jit(solution)/shard_map/all_gather | solution.py:192
  141.7 1.0 fusion.183
  142.7 0.7 fusion.54
  143.4 0.7 fusion.70
  144.1 0.7 fusion.86
  144.7 0.7 fusion.102
  145.4 0.7 fusion.118
  146.1 0.7 fusion.134
  146.8 0.7 fusion.150
  147.5 1.5 %fusion.205 = (f32[]{:T(128)}, f32[]{:T(128)}) fusion(f32[16,64,32]{2,1,0:T(8,128)S(1)} %get-tuple-element.7, f32[16,64,32]{2,1,0:T(8,128)S(1)} %broadcast_in_dim.143, f32[16,64,32]{2,1,0:T(8,128)S(1)} %get-tuple-element.8, f32[16,64,32]{2,1,0:T(8,128)S(1)} %get-tuple-element.9, f32[16,64,32]{2,1,0:T(8,128)S(1)} %get-tuple-element.10, ...), kind=kLoop, calls=%fused_computation.309 | loop fusion | flops 1114110 | bytes 1179656 | tf_op jit(solution)/shard_map/reduce_sum | solution.py:158
  (253 shorter events, 12.1 us)
Async XLA Ops:
  0.6 2.8 %copy-start.9 = (f32[8,64,256]{2,1,0:T(8,128)S(1)}, f32[8,64,256]{2,1,0:T(8,128)}, u32[]{:S(2)}) copy-start(f32[8,64,256]{2,1,0:T(8,128)} %param.3) | copy-start | bytes 1572868
  0.7 21.4 %copy-start.38 = (s32[64]{0:T(128)}, s32[64]{0:T(128)S(1)}, u32[]{:S(2)}) copy-start(s32[64]{0:T(128)S(1)} %and_select_fusion.4) | copy-start | bytes 772
  0.7 2.8 %copy-start.42 = (s32[256]{0:T(256)}, s32[256]{0:T(256)S(1)}, u32[]{:S(2)}) copy-start(s32[256]{0:T(256)S(1)} %and_select_fusion.3) | copy-start | bytes 3076
  0.7 4.2 %copy-start.45 = (s32[128]{0:T(128)}, s32[128]{0:T(128)S(1)}, u32[]{:S(2)}) copy-start(s32[128]{0:T(128)S(1)} %and_select_fusion.1) | copy-start | bytes 1540
  0.7 2.7 %copy-start.24 = (f32[32,64]{1,0:T(8,128)}, f32[32,64]{1,0:T(8,128)S(1)}, u32[]{:S(2)}) copy-start(f32[32,64]{1,0:T(8,128)S(1)} %fusion.300) | copy-start | bytes 24580
  3.2 1.2 copy-start.3
  3.4 33.4 %copy-start.7 = (f32[4,32,128]{2,1,0:T(8,128)}, f32[4,32,128]{2,1,0:T(8,128)S(1)}, u32[]{:S(2)}) copy-start(f32[4,32,128]{2,1,0:T(8,128)S(1)} %convolution_multiply_fusion.1) | copy-start | bytes 196612
  4.9 3.0 %copy-start.31 = (f32[16,32]{1,0:T(8,128)}, f32[16,32]{1,0:T(8,128)S(1)}, u32[]{:S(2)}) copy-start(f32[16,32]{1,0:T(8,128)S(1)} %fusion.311) | copy-start | bytes 6148
  8.7 21.9 %collective-permute-start = (f32[145408]{0:T(1024)}, f32[145408]{0:T(1024)S(1)}, u32[]{:S(2)}, u32[]{:S(2)}) collective-permute-start(f32[145408]{0:T(1024)} %get-tuple-element.86), channel_id=1, source_target_pairs={{0,8},{8,16},{16,24},{24,32},{32,40},{40,48},{48,56},{56,64},{64,7... | collective-permute-start | bytes 1744904 | tf_op jit(solution)/shard_map/ppermute | solution.py:42
  12.7 18.9 %collective-permute-start.1 = (f32[145408]{0:T(1024)}, f32[145408]{0:T(1024)S(1)}, u32[]{:S(2)}, u32[]{:S(2)}) collective-permute-start(f32[145408]{0:T(1024)} %copy-done.33), channel_id=1, source_target_pairs={{8,0},{16,8},{24,16},{32,24},{40,32},{48,40},{56,48},{64,56},{72,6... | collective-permute-start | bytes 1744904 | tf_op jit(solution)/shard_map/ppermute | solution.py:42
  14.1 12.7 %collective-permute-start.2 = (f32[1024]{0:T(1024)S(1)}, f32[1024]{0:T(1024)S(1)}, u32[]{:S(2)}, u32[]{:S(2)}) collective-permute-start(f32[1024]{0:T(1024)S(1)} %reshape.837), channel_id=1, source_target_pairs={{0,16},{8,24},{16,32},{24,40},{32,48},{40,56},{48,64},{56,72},{64,... | collective-permute-start | bytes 12296 | tf_op jit(solution)/shard_map/ppermute | solution.py:42
  20.6 8.8 %collective-permute-start.3 = (f32[1024]{0:T(1024)S(1)}, f32[1024]{0:T(1024)S(1)}, u32[]{:S(2)}, u32[]{:S(2)}) collective-permute-start(f32[1024]{0:T(1024)S(1)} %reshape.841), channel_id=1, source_target_pairs={{16,0},{24,8},{32,16},{40,24},{48,32},{56,40},{64,48},{72,56},{80,... | collective-permute-start | bytes 12296 | tf_op jit(solution)/shard_map/ppermute | solution.py:42
  25.4 5.2 %copy-start.47 = (s32[16]{0:T(128)}, s32[16]{0:T(128)S(1)}, u32[]{:S(2)}) copy-start(s32[16]{0:T(128)S(1)} %and_select_fusion) | copy-start | bytes 196
  31.6 2.2 %slice-start.2 = ((f32[145408]{0:T(1024)}), f32[32768]{0:T(1024)S(1)}, s32[]{:S(2)}) async-start(f32[145408]{0:T(1024)} %copy-done.14), calls=%async_computation.2 | async-start | bytes 262144 | tf_op jit(solution)/shard_map/slice | solution.py:47
  31.6 2.1 %copy-start.12 = (f32[145408]{0:T(1024)}, f32[145408]{0:T(1024)S(1)}, u32[]{:S(2)}) copy-start(f32[145408]{0:T(1024)S(1)} %collective-permute-done.1) | copy-start | bytes 1744900
  32.4 1.5 copy-start.6
  33.9 1.1 copy-start.5
  34.8 1.2 copy-start.10
  34.8 1.1 copy-start.11
  34.9 1.9 %copy-start.13 = (f32[145408]{0:T(1024)S(1)}, f32[145408]{0:T(1024)}, u32[]{:S(2)}) copy-start(f32[145408]{0:T(1024)} %copy-done.12) | copy-start | bytes 1744900
  35.0 1.9 %slice-start.3 = ((f32[145408]{0:T(1024)}), f32[2048]{0:T(1024)S(1)}, s32[]{:S(2)}) async-start(f32[145408]{0:T(1024)} %copy-done.14), calls=%async_computation.3 | async-start | bytes 16384 | tf_op jit(solution)/shard_map/slice | solution.py:47
  35.0 2.0 %copy-start.21 = (f32[8,16,64]{2,1,0:T(8,128)S(1)}, f32[8,16,64]{2,1,0:T(8,128)}, u32[]{:S(2)}) copy-start(f32[8,16,64]{2,1,0:T(8,128)} %constant_dynamic-update-slice_fusion.15) | copy-start | bytes 98308
  35.0 2.0 %slice-start.1 = ((f32[145408]{0:T(1024)}), f32[2048]{0:T(1024)S(1)}, s32[]{:S(2)}) async-start(f32[145408]{0:T(1024)} %copy-done.12), calls=%async_computation.1 | async-start | bytes 16384 | tf_op jit(solution)/shard_map/slice | solution.py:47
  35.0 2.1 %copy-start.34 = (f32[1,16,64]{2,1,0:T(8,128)S(1)}, f32[1,16,64]{2,1,0:T(8,128)}, u32[]{:S(2)}) copy-start(f32[1,16,64]{2,1,0:T(8,128)} %reshape.842) | copy-start | bytes 12292
  35.0 2.2 %copy-start.20 = (f32[10752]{0:T(1024)S(1)}, f32[10752]{0:T(1024)}, u32[]{:S(2)}) copy-start(f32[10752]{0:T(1024)} %reshape.827) | copy-start | bytes 129028
  35.0 2.2 %copy-start.50 = (f32[33024]{0:T(1024)S(1)}, f32[33024]{0:T(1024)}, u32[]{:S(2)}) copy-start(f32[33024]{0:T(1024)} %custom-call.1) | copy-start | bytes 396292
  35.9 2.7 %copy-start.19 = (f32[14,3,256]{2,1,0:T(4,128)S(1)}, f32[14,3,256]{2,1,0:T(4,128)}, u32[]{:S(2)}) copy-start(f32[14,3,256]{2,1,0:T(4,128)} %get-tuple-element.49) | copy-start | bytes 129028
  35.9 2.8 %copy-start.49 = (f32[33024]{0:T(1024)S(1)}, f32[33024]{0:T(1024)}, u32[]{:S(2)}) copy-start(f32[33024]{0:T(1024)} %custom-call) | copy-start | bytes 396292
  36.9 7.7 %copy-start.15 = (f32[12288]{0:T(1024)}, f32[12288]{0:T(1024)S(1)}, u32[]{:S(2)}) copy-start(f32[12288]{0:T(1024)S(1)} %slice.1170) | copy-start | bytes 147460
  36.9 7.7 %copy-start.17 = (f32[12288]{0:T(1024)}, f32[12288]{0:T(1024)S(1)}, u32[]{:S(2)}) copy-start(f32[12288]{0:T(1024)S(1)} %slice.1171) | copy-start | bytes 147460
  37.1 7.4 %copy-start.22 = (f32[8,16,64]{2,1,0:T(8,128)}, f32[8,16,64]{2,1,0:T(8,128)S(1)}, u32[]{:S(2)}) copy-start(f32[8,16,64]{2,1,0:T(8,128)S(1)} %constant_dynamic-update-slice_fusion.11) | copy-start | bytes 98308
  37.3 2.9 %collective-permute-start.4 = (f32[33024]{0:T(1024)S(1)}, f32[33024]{0:T(1024)S(1)}, u32[]{:S(2)}, u32[]{:S(2)}) collective-permute-start(f32[33024]{0:T(1024)S(1)} %constant_dynamic-update-slice_fusion.26), channel_id=1, source_target_pairs={{0,1},{1,2},{2,3},{3,4},{4,5},{5,6},{6,7},{8,9},{9,10},{10,11},{11... | collective-permute-start | bytes 396296 | tf_op jit(solution)/shard_map/ppermute | solution.py:42
  38.9 5.0 %collective-permute-start.5 = (f32[33024]{0:T(1024)S(1)}, f32[33024]{0:T(1024)S(1)}, u32[]{:S(2)}, u32[]{:S(2)}) collective-permute-start(f32[33024]{0:T(1024)S(1)} %constant_dynamic-update-slice_fusion.27), channel_id=1, source_target_pairs={{1,0},{2,1},{3,2},{4,3},{5,4},{6,5},{7,6},{9,8},{10,9},{11,10},{12... | collective-permute-start | bytes 396296 | tf_op jit(solution)/shard_map/ppermute | solution.py:42
  40.2 4.4 %copy-start.26 = (f32[33024]{0:T(1024)}, f32[33024]{0:T(1024)S(1)}, u32[]{:S(2)}) copy-start(f32[33024]{0:T(1024)S(1)} %collective-permute-done.4) | copy-start | bytes 396292
  55.4 1.5 copy-start
  55.4 1.8 %copy-start.1 = (f32[12,68,256]{2,1,0:T(8,128)S(1)}, f32[12,68,256]{2,1,0:T(8,128)}, u32[]{:S(2)}) copy-start(f32[12,68,256]{2,1,0:T(8,128)} %get-tuple-element.43) | copy-start | bytes 2506756
  55.4 1.8 %copy-start.29 = (f32[12,2,256]{2,1,0:T(2,128)S(1)}, f32[12,2,256]{2,1,0:T(2,128)}, u32[]{:S(2)}) copy-start(f32[12,2,256]{2,1,0:T(2,128)} %reshape.849) | copy-start | bytes 73732
  55.4 1.8 %copy-start.30 = (f32[12,2,256]{2,1,0:T(2,128)S(1)}, f32[12,2,256]{2,1,0:T(2,128)}, u32[]{:S(2)}) copy-start(f32[12,2,256]{2,1,0:T(2,128)} %reshape.850) | copy-start | bytes 73732
  55.4 1.8 %copy-start.37 = (pred[12,68]{1,0:T(8,128)(4,1)S(1)}, pred[12,68]{1,0:T(8,128)(4,1)}, u32[]{:S(2)}) copy-start(pred[12,68]{1,0:T(8,128)(4,1)} %broadcast_and_fusion) | copy-start | bytes 2452
  57.1 2.8 %copy-start.2 = (f32[12,68,256]{2,1,0:T(8,128)S(1)}, f32[12,68,256]{2,1,0:T(8,128)}, u32[]{:S(2)}) copy-start(f32[12,68,256]{2,1,0:T(8,128)} %get-tuple-element.37) | copy-start | bytes 2506756
  57.1 2.8 %copy-start.36 = (pred[10,66]{1,0:T(8,128)(4,1)S(1)}, pred[10,66]{1,0:T(8,128)(4,1)}, u32[]{:S(2)}) copy-start(pred[10,66]{1,0:T(8,128)(4,1)} %broadcast_and_fusion.1) | copy-start | bytes 1984
  59.9 1.9 %copy-start.4 = (f32[8,64,256]{2,1,0:T(8,128)S(1)}, f32[8,64,256]{2,1,0:T(8,128)}, u32[]{:S(2)}) copy-start(f32[8,64,256]{2,1,0:T(8,128)} %param.4) | copy-start | bytes 1572868
  61.8 1.7 %copy-start.43 = (s32[256]{0:T(256)S(1)}, s32[256]{0:T(256)}, u32[]{:S(2)}) copy-start(s32[256]{0:T(256)} %copy-done.42) | copy-start | bytes 3076
  61.8 1.9 %copy-start.25 = (f32[32,64]{1,0:T(8,128)S(1)}, f32[32,64]{1,0:T(8,128)}, u32[]{:S(2)}) copy-start(f32[32,64]{1,0:T(8,128)} %copy-done.24) | copy-start | bytes 24580
  61.8 8.5 %slice-start.4 = ((f32[33024]{0:T(1024)}), f32[3840]{0:T(1024)S(1)}, s32[]{:S(2)}) async-start(f32[33024]{0:T(1024)} %copy-done.26), calls=%async_computation.4 | async-start | bytes 32768 | tf_op jit(solution)/shard_map/slice | solution.py:47
  63.4 16.9 %copy-start.8 = (f32[4,32,128]{2,1,0:T(8,128)S(1)}, f32[4,32,128]{2,1,0:T(8,128)}, u32[]{:S(2)}) copy-start(f32[4,32,128]{2,1,0:T(8,128)} %copy-done.7) | copy-start | bytes 196612
  63.4 16.9 %copy-start.16 = (f32[12288]{0:T(1024)S(1)}, f32[12288]{0:T(1024)}, u32[]{:S(2)}) copy-start(f32[12288]{0:T(1024)} %copy-done.15) | copy-start | bytes 147460
  63.4 16.9 %copy-start.18 = (f32[12288]{0:T(1024)S(1)}, f32[12288]{0:T(1024)}, u32[]{:S(2)}) copy-start(f32[12288]{0:T(1024)} %copy-done.17) | copy-start | bytes 147460
  63.4 19.3 %copy-start.41 = (pred[8,36]{1,0:T(8,128)(4,1)S(1)}, pred[8,36]{1,0:T(8,128)(4,1)}, u32[]{:S(2)}) copy-start(pred[8,36]{1,0:T(8,128)(4,1)} %broadcast_and_fusion.3) | copy-start | bytes 868
  64.0 7.0 %collective-permute-start.6 = (f32[8192]{0:T(1024)S(1)}, f32[8192]{0:T(1024)S(1)}, u32[]{:S(2)}, u32[]{:S(2)}) collective-permute-start(f32[8192]{0:T(1024)S(1)} %bitcast.153), channel_id=1, source_target_pairs={{0,8},{8,16},{16,24},{24,32},{32,40},{40,48},{48,56},{56,64},{64,7... | collective-permute-start | bytes 98312 | tf_op jit(solution)/shard_map/ppermute | solution.py:42
  69.0 5.8 %collective-permute-start.7 = (f32[8192]{0:T(1024)S(1)}, f32[8192]{0:T(1024)S(1)}, u32[]{:S(2)}, u32[]{:S(2)}) collective-permute-start(f32[8192]{0:T(1024)S(1)} %bitcast.152), channel_id=1, source_target_pairs={{8,0},{16,8},{24,16},{32,24},{40,32},{48,40},{56,48},{64,56},{72,6... | collective-permute-start | bytes 98312 | tf_op jit(solution)/shard_map/ppermute | solution.py:42
  74.8 5.6 %collective-permute-start.8 = (f32[2048]{0:T(1024)S(1)}, f32[2048]{0:T(1024)S(1)}, u32[]{:S(2)}, u32[]{:S(2)}) collective-permute-start(f32[2048]{0:T(1024)S(1)} %bitcast.157), channel_id=1, source_target_pairs={{0,1},{1,2},{2,3},{3,4},{4,5},{5,6},{6,7},{8,9},{9,10},{10,11},{11... | collective-permute-start | bytes 24584 | tf_op jit(solution)/shard_map/ppermute | solution.py:42
  79.0 3.7 %collective-permute-start.9 = (f32[2048]{0:T(1024)S(1)}, f32[2048]{0:T(1024)S(1)}, u32[]{:S(2)}, u32[]{:S(2)}) collective-permute-start(f32[2048]{0:T(1024)S(1)} %bitcast.156), channel_id=1, source_target_pairs={{1,0},{2,1},{3,2},{4,3},{5,4},{6,5},{7,6},{9,8},{10,9},{11,10},{12... | collective-permute-start | bytes 24584 | tf_op jit(solution)/shard_map/ppermute | solution.py:42
  83.7 0.9 copy-start.32
  83.7 6.2 %copy-start.51 = (pred[4]{0:T(512)(128)(4,1)S(1)}, pred[4]{0:T(512)(128)(4,1)}, u32[]{:S(2)}) copy-start(pred[4]{0:T(512)(128)(4,1)} %compare_and_fusion.3) | copy-start | bytes 16
  83.7 6.3 %copy-start.35 = (f32[8,32]{1,0:T(8,128)S(1)}, f32[8,32]{1,0:T(8,128)}, u32[]{:S(2)}) copy-start(f32[8,32]{1,0:T(8,128)} %convolution_multiply_fusion.4) | copy-start | bytes 3076
  83.7 6.4 %copy-start.27 = (f32[33024]{0:T(1024)S(1)}, f32[33024]{0:T(1024)}, u32[]{:S(2)}) copy-start(f32[33024]{0:T(1024)} %copy-done.26) | copy-start | bytes 396292
  83.7 14.9 %copy-start.23 = (f32[8,16,64]{2,1,0:T(8,128)S(1)}, f32[8,16,64]{2,1,0:T(8,128)}, u32[]{:S(2)}) copy-start(f32[8,16,64]{2,1,0:T(8,128)} %copy-done.22) | copy-start | bytes 98308
  83.7 17.7 %copy-start.44 = (pred[6,20]{1,0:T(8,128)(4,1)S(1)}, pred[6,20]{1,0:T(8,128)(4,1)}, u32[]{:S(2)}) copy-start(pred[6,20]{1,0:T(8,128)(4,1)} %broadcast_and_fusion.2) | copy-start | bytes 364
  84.8 6.1 %collective-permute-start.10 = (f32[2048]{0:T(1024)S(1)}, f32[2048]{0:T(1024)S(1)}, u32[]{:S(2)}, u32[]{:S(2)}) collective-permute-start(f32[2048]{0:T(1024)S(1)} %reshape.861), channel_id=1, source_target_pairs={{0,8},{8,16},{16,24},{24,32},{32,40},{40,48},{48,56},{56,64},{64,7... | collective-permute-start | bytes 24584 | tf_op jit(solution)/shard_map/ppermute | solution.py:42
  88.6 5.5 %collective-permute-start.11 = (f32[2048]{0:T(1024)S(1)}, f32[2048]{0:T(1024)S(1)}, u32[]{:S(2)}, u32[]{:S(2)}) collective-permute-start(f32[2048]{0:T(1024)S(1)} %reshape.861), channel_id=1, source_target_pairs={{8,0},{16,8},{24,16},{32,24},{40,32},{48,40},{56,48},{64,56},{72,6... | collective-permute-start | bytes 24584 | tf_op jit(solution)/shard_map/ppermute | solution.py:42
  94.3 4.3 %collective-permute-start.12 = (f32[768]{0:T(1024)S(1)}, f32[768]{0:T(1024)S(1)}, u32[]{:S(2)}, u32[]{:S(2)}) collective-permute-start(f32[768]{0:T(1024)S(1)} %reshape.864), channel_id=1, source_target_pairs={{0,1},{1,2},{2,3},{3,4},{4,5},{5,6},{6,7},{8,9},{9,10},{10,11},{11... | collective-permute-start | bytes 9224 | tf_op jit(solution)/shard_map/ppermute | solution.py:42
  97.3 4.0 %collective-permute-start.13 = (f32[768]{0:T(1024)S(1)}, f32[768]{0:T(1024)S(1)}, u32[]{:S(2)}, u32[]{:S(2)}) collective-permute-start(f32[768]{0:T(1024)S(1)} %reshape.866), channel_id=1, source_target_pairs={{1,0},{2,1},{3,2},{4,3},{5,4},{6,5},{7,6},{9,8},{10,9},{11,10},{12... | collective-permute-start | bytes 9224 | tf_op jit(solution)/shard_map/ppermute | solution.py:42
  101.4 1.0 copy-start.48
  (7 other events, 5.6 us)

commit v3 on v2

--- a/solution.py
+++ b/solution.py
@@ -17,11 +17,12 @@
 jacobi_weight = 0.8
 
 
-def exchange(items, axis, dim):
+def exchange(items, axis, dim, forwards=()):
     count = lax.axis_size(axis)
     low = [[] for _ in items]
     high = [[] for _ in items]
     reach = max(-(-width // block.shape[dim]) for block, width in items)
+    boxes = [box for box, _, _ in forwards]
     for hop in range(1, reach + 1):
         for sign in (1, -1):
             pieces = []
@@ -34,6 +35,10 @@
                     pieces.append(lax.slice_in_dim(block, size - rows, size, axis=dim))
                 else:
                     pieces.append(lax.slice_in_dim(block, 0, rows, axis=dim))
+            if hop == 1:
+                for box, rows_low, rows_high in forwards:
+                    rows = rows_low if sign == 1 else rows_high
+                    pieces.append(lax.slice_in_dim(box, rows[0], rows[1], axis=dim))
             flat = jnp.concatenate([p.reshape(-1) for p in pieces if p is not None])
             if sign == 1:
                 pairs = [(i, i + hop) for i in range(count - hop)]
@@ -41,25 +46,38 @@
                 pairs = [(i + hop, i) for i in range(count - hop)]
             got = lax.ppermute(flat, axis, pairs)
             offset = 0
-            for index, piece in enumerate(pieces):
+            parts = []
+            for piece in pieces:
                 if piece is None:
+                    parts.append(None)
                     continue
-                part = got[offset : offset + piece.size].reshape(piece.shape)
+                parts.append(got[offset : offset + piece.size].reshape(piece.shape))
                 offset += piece.size
+            for index in range(len(items)):
+                if parts[index] is None:
+                    continue
                 if sign == 1:
-                    low[index].insert(0, part)
+                    low[index].insert(0, parts[index])
                 else:
-                    high[index].append(part)
-    return [
+                    high[index].append(parts[index])
+            if hop == 1:
+                for index, part in enumerate(parts[len(items) :]):
+                    if sign == 1:
+                        boxes[index] = jnp.concatenate([part, boxes[index]], axis=dim)
+                    else:
+                        boxes[index] = jnp.concatenate([boxes[index], part], axis=dim)
+    extended = [
         jnp.concatenate(low[i] + [block] + high[i], axis=dim)
         for i, (block, width) in enumerate(items)
     ]
-
-
-def exchange_xy(items):
-    widths = [width for _, width in items]
-    extended = exchange(items, "xb", 0)
-    return exchange(list(zip(extended, widths)), "yb", 1)
+    return extended, boxes
+
+
+def exchange_xy(items, forwards=()):
+    widths = [item[-1] for item in items]
+    extended, boxes = exchange([item[:2] for item in items], "xb", 0, forwards)
+    extended, _ = exchange(list(zip(extended, widths)), "yb", 1)
+    return extended, boxes
 
 
 def inside_mask(shape, halo):
@@ -171,13 +189,14 @@
         residual = right_side - apply_operator(pad_z(start), trim(start), weights, diagonal)
         start = trim(start)
     first_step = residual / (cheb_theta * diagonal)
-    first = jnp.where(inside_mask(shape, 2), start + first_step, 0.0)
+    inside = inside_mask(shape, 2)
+    first = jnp.where(inside, start + first_step, 0.0)
     weights = [trim(w) for w in weights]
     diagonal = trim(diagonal)
     right_side = trim(right_side)
     residual = right_side - apply_operator(pad_z(first), trim(first), weights, diagonal)
     second_step = cheb_carry * trim(first_step) + cheb_resid * residual / diagonal
-    second = jnp.where(inside_mask(shape, 1), trim(first) + second_step, 0.0)
+    second = jnp.where(trim(inside), trim(first) + second_step, 0.0)
     weights = [trim(w) for w in weights]
     diagonal = trim(diagonal)
     residual = trim(right_side) - apply_operator(pad_z(second), trim(second), weights, diagonal)
@@ -189,7 +208,8 @@
     count_x = lax.axis_size("xb")
     count_y = lax.axis_size("yb")
     flat = jnp.concatenate([right_side.reshape(1, -1), coefficient.reshape(1, -1)], axis=1)
-    both = lax.all_gather(flat, ("xb", "yb"), axis=0, tiled=True)
+    both = lax.all_gather(flat, "yb", axis=0, tiled=True)
+    both = lax.all_gather(both, "xb", axis=0, tiled=True)
     size = sx * sy * sz
     return tuple(
         (
@@ -210,15 +230,25 @@
 def per_device(initial_guess, right_side, coefficient):
     mid_coef = restrict_field(coefficient)
     low_coef = restrict_field(mid_coef)
-    guess_b, rhs_b, coef_b, mid_coef_b, low_coef_b = exchange_xy(
-        [(initial_guess, 3), (right_side, 2), (coefficient, 3), (mid_coef, 3), (low_coef, 3)]
+    low_size = low_coef.shape[0]
+    low_first = min(3, low_size)
+    assert low_first == 3 or 2 * low_first >= 3
+    (guess_b, rhs_b, coef_b, mid_coef_b, low_coef_b), _ = exchange_xy(
+        [(initial_guess, 3), (right_side, 2), (coefficient, 3), (mid_coef, 3), (low_coef, low_first, 3)]
     )
     fine, fine_res = smooth_box(guess_b, rhs_b, coef_b, 1.0, right_side.shape)
     mid_rhs = restrict_field(fine_res)
-    (mid_rhs_b,) = exchange_xy([(mid_rhs, 2)])
+    (mid_rhs_b,), _ = exchange_xy([(mid_rhs, 2)])
     middle, mid_res = smooth_box(None, mid_rhs_b, mid_coef_b, 0.25, mid_rhs.shape)
     low_rhs = restrict_field(mid_res)
-    (low_rhs_b,) = exchange_xy([(low_rhs, 2)])
+    forwards = ()
+    if low_first < 3:
+        forwards = (
+            (low_coef_b, (2 * low_size - 3, low_size), (2 * low_size, low_size + 3)),
+        )
+    (low_rhs_b,), boxes = exchange_xy([(low_rhs, 2)], forwards)
+    if low_first < 3:
+        (low_coef_b,) = boxes
     lower, low_res = smooth_box(None, low_rhs_b, low_coef_b, 0.0625, low_rhs.shape)
     coarse_rhs, coarse_coef = collect_grid(restrict_field(low_res), restrict_field(low_coef))
     coarse_whole = coarse_solve(coarse_rhs, coarse_coef, 0.015625, extend_all)

time: 153 us -> 158 us (1.033)
  local copies, waits for them, and re-layouts: 27.1 us -> 36.4 us
  starting transfers between devices: 36.5 us -> 27.7 us
  waiting for transfers between devices: 17.4 us -> 23.5 us
    ppermute x14 -> x12, starting transfers between devices: 36.5 us -> 27.7 us  [exchange(): got = lax.ppermute(flat, axis, pairs)]
    ppermute x14 -> x12, waiting for transfers between devices: 17.4 us -> 23.5 us  [exchange(): got = lax.ppermute(flat, axis, pairs)]
    unnamed x139 -> x145, local copies, waits for them, and re-layouts: 7.57 us -> 13 us
    reshape x18 -> x22, local copies, waits for them, and re-layouts: 4.33 us -> 6.66 us  [exchange(): parts.append(got[offset:offset + piece.size].reshape(piece.shape))]
    slice x27, local copies, waits for them, and re-layouts: 10.8 us -> 9.14 us  [the longest x25 8.99 us: exchange(): parts.append(got[offset:offset + piece.size].reshape(piece.shape))]
    and x6 -> x5, other arithmetic: 3.33 us -> 2.58 us  [inside_mask(): return in_x[:, None, None] & in_y[None, :, None]]
    all_gather x1 -> x2, blocking collectives: 38.6 us -> 39.1 us  [the longest x1 26 us: collect_grid(): both = lax.all_gather(both, 'xb', axis=0, tiled=True)]
  transfers between devices with their start and end apart: 14 -> 12, of which waited for: 6 -> 8; matrix products, arithmetic and copies ran while one was open for 6% -> 6% of each run, Pallas kernels for 0% -> 0%
where the time goes in v3:
time: 158 us; the launch traced here: 157 us
  blocking collectives  39.1 us (25%)
  local copies, waits for them, and re-layouts  36.4 us (23%)
  starting transfers between devices  27.7 us (18%)
  other arithmetic  23.7 us (15%)
  waiting for transfers between devices  23.5 us (15%)
  between operations  3.26 us (2%)
  matrix products  3.18 us (2%)
    ppermute x12, starting transfers between devices, exchange(): got = lax.ppermute(flat, axis, pairs)  27.7 us
    all_gather x1, blocking collectives, collect_grid(): both = lax.all_gather(both, 'xb', axis=0, tiled=True)  26 us
    ppermute x12, waiting for transfers between devices, exchange(): got = lax.ppermute(flat, axis, pairs)  23.5 us
    all_gather x1, blocking collectives, collect_grid(): both = lax.all_gather(flat, 'yb', axis=0, tiled=True)  13.1 us
    unnamed x145, local copies, waits for them, and re-layouts  13 us
    slice x25, local copies, waits for them, and re-layouts, exchange(): parts.append(got[offset:offset + piece.size].reshape(piece.shape))  8.99 us
    reshape x22, local copies, waits for them, and re-layouts, exchange(): parts.append(got[offset:offset + piece.size].reshape(piece.shape))  6.66 us
    add x7, other arithmetic, coarse_solve(): field + jacobi_weight * (right_side - apply_operator(extend(field), field...  4.78 us
  transfers between devices with their start and end apart: 12, of which 8 were waited for; matrix products, arithmetic and copies ran while one was open for 6% of the time, Pallas kernels for 0%

profile of v3, /device:TPU:0, one launch (start us, length us, event | category | flops | bytes accessed | tf_op | source)
XLA Modules:
  0.0 156.8 jit_solution(18147381249840537939)
XLA Ops:
  0.7 1.1 fusion.344
  1.9 1.3 fusion.213
  3.6 0.7 constant_dynamic-update-slice_fusion
  5.3 0.7 constant_dynamic-update-slice_fusion.19
  5.9 0.7 constant_dynamic-update-slice_fusion.17
  7.9 0.8 copy-done.39
  8.7 4.0 %collective-permute-start = (f32[145408]{0:T(1024)}, f32[145408]{0:T(1024)S(1)}, u32[]{:S(2)}, u32[]{:S(2)}) collective-permute-start(f32[145408]{0:T(1024)} %get-tuple-element.87), channel_id=1, source_target_pairs={{0,8},{8,16},{16,24},{24,32},{32,40},{40,48},{48,56},{56,64},{64,7... | collective-permute-start | bytes 1744904 | tf_op jit(solution)/shard_map/ppermute | solution.py:47
  12.7 1.3 collective-permute-start.1
  14.7 0.7 broadcast_and_fusion.1
  16.4 0.7 reshape.781
  19.1 6.3 %collective-permute-done = f32[145408]{0:T(1024)S(1)} collective-permute-done((f32[145408]{0:T(1024)}, f32[145408]{0:T(1024)S(1)}, u32[]{:S(2)}, u32[]{:S(2)}) %collective-permute-start) | collective-permute-done | bytes 581664 | tf_op jit(solution)/shard_map/ppermute | solution.py:47
  25.3 0.7 fusion.343
  26.2 3.3 %collective-permute-done.1 = f32[145408]{0:T(1024)S(1)} collective-permute-done((f32[145408]{0:T(1024)}, f32[145408]{0:T(1024)S(1)}, u32[]{:S(2)}, u32[]{:S(2)}) %collective-permute-start.1) | collective-permute-done | bytes 581664 | tf_op jit(solution)/shard_map/ppermute | solution.py:47
  29.5 0.7 fusion.342
  30.4 0.7 fusion.341
  31.9 0.8 slice-done.1
  34.4 0.9 copy-done.20
  35.7 1.4 constant_dynamic-update-slice_fusion.11
  37.1 1.4 constant_dynamic-update-slice_fusion.27
  38.4 1.4 constant_dynamic-update-slice_fusion.25
  39.9 1.3 constant_dynamic-update-slice_fusion.23
  41.2 1.3 constant_dynamic-update-slice_fusion.21
  42.5 1.3 collective-permute-start.2
  44.1 1.3 collective-permute-start.3
  46.0 0.7 slice.982
  46.7 2.4 %collective-permute-done.3 = f32[32640]{0:T(1024)S(1)} collective-permute-done((f32[32640]{0:T(1024)S(1)}, f32[32640]{0:T(1024)S(1)}, u32[]{:S(2)}, u32[]{:S(2)}) %collective-permute-start.3) | collective-permute-done | bytes 130592 | tf_op jit(solution)/shard_map/ppermute | solution.py:47
  49.0 0.7 slice.984
  51.2 2.4 %add_add_fusion = (f32[12,68,256]{2,1,0:T(8,128)}, f32[12,68,256]{2,1,0:T(8,128)S(1)}, f32[12,68,256]{2,1,0:T(8,128)S(1)}, f32[12,68,256]{2,1,0:T(8,128)S(1)}, f...) fusion(f32[14,70,256]{2,1,0:T(8,128)S(1)} %pad_maximum_fusion.1), kind=kLoop, calls=%fused_computation.56 | loop fusion | flops 3760128 | bytes 11304960 | tf_op jit(solution)/shard_map/add | solution.py:116
  53.6 1.4 reshape.744
  55.0 1.4 reshape.750
  56.4 1.4 slice.1171
  57.8 1.4 reshape.751
  59.1 1.4 slice.1172
  60.5 1.4 reshape.752
  61.9 1.4 pad_maximum_fusion
  63.6 2.8 %add_select_fusion = (f32[12,68,256]{2,1,0:T(8,128)S(1)}, f32[12,68,256]{2,1,0:T(8,128)S(1)}, f32[12,68,256]{2,1,0:T(8,128)S(1)}) fusion(f32[14,70,256]{2,1,0:T(8,128)S(1)} %pad_maximum_fusion, pred[12,68]{1,0:T(8,128)(4,1)S(1)} %copy-done.41, f32[12,68,256]{2,1,0:T(8,128)S(1)} %copy-done, f32[12,68,256]{2,1,0:T(8,128)S(1)} %copy-done.1, ...), kind=kLoop, calls=%fused_computation.55 | loop fusion | flops 5431296 | bytes 14108672 | tf_op jit(solution)/shard_map/jit(_where)/select_n | solution.py:193
  66.4 1.8 %fusion.31 = f32[10,66,256]{2,1,0:T(8,128)S(1)} fusion(f32[12,68,256]{2,1,0:T(8,128)S(1)} %get-tuple-element.44, f32[12,68,256]{2,1,0:T(8,128)S(1)} %copy-done, f32[12,68,256]{2,1,0:T(8,128)S(1)} %copy-done.1, f32[12,68,256]{2,1,0:T(8,128)S(1)} %get-tuple-element.41, f32[12,68,256]{2,1,0:T(8,128)S(1)} %get-tuple-element.40, ...), kind=kLoop, calls=%fused_computation.129 | loop fusion | flops 3379200 | bytes 11884544 | tf_op jit(solution)/shard_map/jit(_where)/select_n | solution.py:199
  68.3 1.6 %fusion.172 = (f32[8,64,256]{2,1,0:T(8,128)S(1)}, f32[8,64,256]{2,1,0:T(8,128)}) fusion(f32[8,64,256]{2,1,0:T(8,128)S(1)} %copy-done.4, f32[10,66,256]{2,1,0:T(8,128)S(1)} %fusion.31, f32[12,68,256]{2,1,0:T(8,128)S(1)} %copy-done, f32[12,68,256]{2,1,0:T(8,128)S(1)} %copy-done.1, f32[12,68,256]{2,1,0:T(8,128)S(1)} %get-tuple-element.41, ...), kind=kLoop, calls=%fused_computation.270 | loop fusion | flops 1835008 | bytes 8601600 | tf_op jit(solution)/shard_map/sub | solution.py:202
  70.5 3.6 %collective-permute-start.4 = (f32[8192]{0:T(1024)S(1)}, f32[8192]{0:T(1024)S(1)}, u32[]{:S(2)}, u32[]{:S(2)}) collective-permute-start(f32[8192]{0:T(1024)S(1)} %bitcast.159), channel_id=1, source_target_pairs={{0,8},{8,16},{16,24},{24,32},{32,40},{40,48},{48,56},{56,64},{64,7... | collective-permute-start | bytes 98312 | tf_op jit(solution)/shard_map/ppermute | solution.py:47
  74.1 1.3 collective-permute-start.5
  75.5 0.7 slice.1249
  76.3 0.7 slice.1250
  77.1 2.9 %collective-permute-done.5 = f32[8192]{0:T(1024)S(1)} collective-permute-done((f32[8192]{0:T(1024)S(1)}, f32[8192]{0:T(1024)S(1)}, u32[]{:S(2)}, u32[]{:S(2)}) %collective-permute-start.5) | collective-permute-done | bytes 32800 | tf_op jit(solution)/shard_map/ppermute | solution.py:47
  80.0 4.0 %collective-permute-start.6 = (f32[2048]{0:T(1024)S(1)}, f32[2048]{0:T(1024)S(1)}, u32[]{:S(2)}, u32[]{:S(2)}) collective-permute-start(f32[2048]{0:T(1024)S(1)} %bitcast.163), channel_id=1, source_target_pairs={{0,1},{1,2},{2,3},{3,4},{4,5},{5,6},{6,7},{8,9},{9,10},{10,11},{11... | collective-permute-start | bytes 24584 | tf_op jit(solution)/shard_map/ppermute | solution.py:47
  84.0 1.3 collective-permute-start.7
  85.5 2.4 %collective-permute-done.7 = f32[2048]{0:T(1024)S(1)} collective-permute-done((f32[2048]{0:T(1024)S(1)}, f32[2048]{0:T(1024)S(1)}, u32[]{:S(2)}, u32[]{:S(2)}) %collective-permute-start.7) | collective-permute-done | bytes 8224 | tf_op jit(solution)/shard_map/ppermute | solution.py:47
  88.8 0.7 fusion.252
  90.0 3.9 %collective-permute-start.8 = (f32[3456]{0:T(1024)S(1)}, f32[3456]{0:T(1024)S(1)}, u32[]{:S(2)}, u32[]{:S(2)}) collective-permute-start(f32[3456]{0:T(1024)S(1)} %get-tuple-element.84), channel_id=1, source_target_pairs={{0,8},{8,16},{16,24},{24,32},{32,40},{40,48},{48,56},{56,64},{64,7... | collective-permute-start | bytes 41480 | tf_op jit(solution)/shard_map/ppermute | solution.py:47
  93.9 1.3 collective-permute-start.9
  95.4 4.1 %collective-permute-done.9 = f32[3456]{0:T(1024)S(1)} collective-permute-done((f32[3456]{0:T(1024)S(1)}, f32[3456]{0:T(1024)S(1)}, u32[]{:S(2)}, u32[]{:S(2)}) %collective-permute-start.9) | collective-permute-done | bytes 13856 | tf_op jit(solution)/shard_map/ppermute | solution.py:47
  99.7 3.1 %collective-permute-start.10 = (f32[768]{0:T(1024)S(1)}, f32[768]{0:T(1024)S(1)}, u32[]{:S(2)}, u32[]{:S(2)}) collective-permute-start(f32[768]{0:T(1024)S(1)} %reshape.772), channel_id=1, source_target_pairs={{0,1},{1,2},{2,3},{3,4},{4,5},{5,6},{6,7},{8,9},{9,10},{10,11},{11... | collective-permute-start | bytes 9224 | tf_op jit(solution)/shard_map/ppermute | solution.py:47
  102.9 1.3 collective-permute-start.11
  104.6 2.1 %collective-permute-done.11 = f32[768]{0:T(1024)S(1)} collective-permute-done((f32[768]{0:T(1024)S(1)}, f32[768]{0:T(1024)S(1)}, u32[]{:S(2)}, u32[]{:S(2)}) %collective-permute-start.11) | collective-permute-done | bytes 3104 | tf_op jit(solution)/shard_map/ppermute | solution.py:47
  108.1 13.1 %all-gather = f32[8,1,512]{2,1,0:T(1,128)S(1)} all-gather(f32[1,1,512]{2,1,0:T(1,128)S(1)} %maximum_bitcast_fusion), channel_id=1, replica_groups=mesh['xb'=16,'yb'=8] {'yb'}, dimensions={0}, use_global_device_ids=true | all-gather | bytes 18432 | tf_op jit(solution)/shard_map/all_gather | solution.py:211
  121.2 26.0 %all_gather.7 = f32[128,512]{1,0:T(8,128)S(1)} all-gather(f32[8,512]{1,0:T(8,128)S(1)} %bitcast.157), channel_id=1, replica_groups=mesh['xb'=16,'yb'=8] {'xb'}, dimensions={0}, use_global_device_ids=true | all-gather | bytes 278528 | tf_op jit(solution)/shard_map/all_gather | solution.py:212
  147.6 1.0 fusion.183
  148.6 0.7 fusion.54
  149.3 0.7 fusion.70
  149.9 0.7 fusion.86
  150.6 0.7 fusion.102
  151.3 0.7 fusion.118
  152.0 0.7 fusion.134
  152.7 0.7 fusion.150
  153.4 1.5 fusion.205
  (258 shorter events, 17.0 us)
Async XLA Ops:
  0.6 2.8 %copy-start.9 = (f32[8,64,256]{2,1,0:T(8,128)S(1)}, f32[8,64,256]{2,1,0:T(8,128)}, u32[]{:S(2)}) copy-start(f32[8,64,256]{2,1,0:T(8,128)} %param.3) | copy-start | bytes 1572868
  0.7 15.5 %copy-start.42 = (s32[64]{0:T(128)}, s32[64]{0:T(128)S(1)}, u32[]{:S(2)}) copy-start(s32[64]{0:T(128)S(1)} %and_select_fusion.4) | copy-start | bytes 772
  0.7 2.8 %copy-start.46 = (s32[256]{0:T(256)}, s32[256]{0:T(256)S(1)}, u32[]{:S(2)}) copy-start(s32[256]{0:T(256)S(1)} %and_select_fusion.3) | copy-start | bytes 3076
  0.7 4.2 %copy-start.50 = (s32[128]{0:T(128)}, s32[128]{0:T(128)S(1)}, u32[]{:S(2)}) copy-start(s32[128]{0:T(128)S(1)} %and_select_fusion.1) | copy-start | bytes 1540
  0.7 2.8 %copy-start.29 = (f32[32,64]{1,0:T(8,128)}, f32[32,64]{1,0:T(8,128)S(1)}, u32[]{:S(2)}) copy-start(f32[32,64]{1,0:T(8,128)S(1)} %fusion.301) | copy-start | bytes 24580
  3.2 1.2 copy-start.3
  3.4 31.9 %copy-start.7 = (f32[4,32,128]{2,1,0:T(8,128)}, f32[4,32,128]{2,1,0:T(8,128)S(1)}, u32[]{:S(2)}) copy-start(f32[4,32,128]{2,1,0:T(8,128)S(1)} %convolution_multiply_fusion.1) | copy-start | bytes 196612
  4.9 21.2 %copy-start.37 = (f32[16,32]{1,0:T(8,128)}, f32[16,32]{1,0:T(8,128)S(1)}, u32[]{:S(2)}) copy-start(f32[16,32]{1,0:T(8,128)S(1)} %fusion.312) | copy-start | bytes 6148
  8.7 16.6 %collective-permute-start = (f32[145408]{0:T(1024)}, f32[145408]{0:T(1024)S(1)}, u32[]{:S(2)}, u32[]{:S(2)}) collective-permute-start(f32[145408]{0:T(1024)} %get-tuple-element.87), channel_id=1, source_target_pairs={{0,8},{8,16},{16,24},{24,32},{32,40},{40,48},{48,56},{56,64},{64,7... | collective-permute-start | bytes 1744904 | tf_op jit(solution)/shard_map/ppermute | solution.py:47
  12.7 16.9 %collective-permute-start.1 = (f32[145408]{0:T(1024)}, f32[145408]{0:T(1024)S(1)}, u32[]{:S(2)}, u32[]{:S(2)}) collective-permute-start(f32[145408]{0:T(1024)} %copy-done.39), channel_id=1, source_target_pairs={{8,0},{16,8},{24,16},{32,24},{40,32},{48,40},{56,48},{64,56},{72,6... | collective-permute-start | bytes 1744904 | tf_op jit(solution)/shard_map/ppermute | solution.py:47
  16.0 10.2 %copy-start.52 = (s32[16]{0:T(128)}, s32[16]{0:T(128)S(1)}, u32[]{:S(2)}) copy-start(s32[16]{0:T(128)S(1)} %and_select_fusion) | copy-start | bytes 196
  25.3 6.4 %copy-start.17 = (f32[145408]{0:T(1024)}, f32[145408]{0:T(1024)S(1)}, u32[]{:S(2)}) copy-start(f32[145408]{0:T(1024)S(1)} %collective-permute-done) | copy-start | bytes 1744900
  29.5 2.2 %copy-start.19 = (f32[145408]{0:T(1024)}, f32[145408]{0:T(1024)S(1)}, u32[]{:S(2)}) copy-start(f32[145408]{0:T(1024)S(1)} %collective-permute-done.1) | copy-start | bytes 1744900
  30.4 1.5 copy-start.6
  31.8 2.2 %copy-start.11 = (f32[49152]{0:T(1024)S(1)}, f32[49152]{0:T(1024)}, u32[]{:S(2)}) copy-start(f32[49152]{0:T(1024)} %get-tuple-element.55) | copy-start | bytes 589828
  31.9 2.2 %copy-start.5 = (f32[8,64,256]{2,1,0:T(8,128)S(1)}, f32[8,64,256]{2,1,0:T(8,128)}, u32[]{:S(2)}) copy-start(f32[8,64,256]{2,1,0:T(8,128)} %param.5) | copy-start | bytes 1572868
  32.7 1.6 copy-start.10
  32.8 1.5 copy-start.12
  34.1 1.2 copy-start.18
  34.2 1.2 slice-start
  34.2 1.3 slice-start.2
  34.2 1.5 copy-start.26
  34.2 2.9 %copy-start.31 = (f32[12,2,2,128]{3,1,2,0:T(2,128)S(1)}, f32[12,2,2,128]{3,1,2,0:T(2,128)}, u32[]{:S(2)}) copy-start(f32[12,2,2,128]{3,1,2,0:T(2,128)} %copy.30) | copy-start | bytes 73732
  34.2 9.6 %copy-start.25 = (f32[14,3,256]{2,1,0:T(4,128)S(1)}, f32[14,3,256]{2,1,0:T(4,128)}, u32[]{:S(2)}) copy-start(f32[14,3,256]{2,1,0:T(4,128)} %get-tuple-element.49) | copy-start | bytes 129028
  34.3 9.5 %copy-start.32 = (f32[12,2,2,128]{3,2,1,0:T(2,128)S(1)}, f32[12,2,2,128]{3,2,1,0:T(2,128)}, u32[]{:S(2)}) copy-start(f32[12,2,2,128]{3,2,1,0:T(2,128)} %get-tuple-element.52) | copy-start | bytes 73732
  34.3 9.6 %copy-start.56 = (f32[32640]{0:T(1024)S(1)}, f32[32640]{0:T(1024)}, u32[]{:S(2)}) copy-start(f32[32640]{0:T(1024)} %custom-call) | copy-start | bytes 391684
  34.4 11.0 %copy-start.54 = (pred[6,20,1]{1,0,2:T(8,128)(4,1)S(1)}, pred[6,20,1]{1,0,2:T(8,128)(4,1)}, u32[]{:S(2)}) copy-start(pred[6,20,1]{1,0,2:T(8,128)(4,1)} %broadcast_and_fusion.2) | copy-start | bytes 364
  35.3 15.6 %copy-start.21 = (f32[12288]{0:T(1024)}, f32[12288]{0:T(1024)S(1)}, u32[]{:S(2)}) copy-start(f32[12288]{0:T(1024)S(1)} %slice.1162) | copy-start | bytes 147460
  35.4 15.6 %copy-start.23 = (f32[12288]{0:T(1024)}, f32[12288]{0:T(1024)S(1)}, u32[]{:S(2)}) copy-start(f32[12288]{0:T(1024)S(1)} %slice.1161) | copy-start | bytes 147460
  35.5 15.5 %copy-start.13 = (f32[2,16,64]{2,1,0:T(8,128)}, f32[2,16,64]{2,1,0:T(8,128)S(1)}, u32[]{:S(2)}) copy-start(f32[2,16,64]{2,1,0:T(8,128)S(1)} %reshape.741) | copy-start | bytes 24580
  35.6 15.5 %copy-start.15 = (f32[2,16,64]{2,1,0:T(8,128)}, f32[2,16,64]{2,1,0:T(8,128)S(1)}, u32[]{:S(2)}) copy-start(f32[2,16,64]{2,1,0:T(8,128)S(1)} %reshape.742) | copy-start | bytes 24580
  42.5 3.5 %collective-permute-start.2 = (f32[32640]{0:T(1024)}, f32[32640]{0:T(1024)S(1)}, u32[]{:S(2)}, u32[]{:S(2)}) collective-permute-start(f32[32640]{0:T(1024)} %constant_dynamic-update-slice_fusion.21), channel_id=1, source_target_pairs={{0,1},{1,2},{2,3},{3,4},{4,5},{5,6},{6,7},{8,9},{9,10},{10,11},{11... | collective-permute-start | bytes 391688 | tf_op jit(solution)/shard_map/ppermute | solution.py:47
  44.1 5.0 %collective-permute-start.3 = (f32[32640]{0:T(1024)S(1)}, f32[32640]{0:T(1024)S(1)}, u32[]{:S(2)}, u32[]{:S(2)}) collective-permute-start(f32[32640]{0:T(1024)S(1)} %constant_dynamic-update-slice_fusion.22), channel_id=1, source_target_pairs={{1,0},{2,1},{3,2},{4,3},{5,4},{6,5},{7,6},{9,8},{10,9},{11,10},{12... | collective-permute-start | bytes 391688 | tf_op jit(solution)/shard_map/ppermute | solution.py:47
  46.0 5.0 %copy-start.27 = (f32[32640]{0:T(1024)}, f32[32640]{0:T(1024)S(1)}, u32[]{:S(2)}) copy-start(f32[32640]{0:T(1024)S(1)} %collective-permute-done.2) | copy-start | bytes 391684
  49.0 2.0 %copy-start.28 = (f32[32640]{0:T(1024)}, f32[32640]{0:T(1024)S(1)}, u32[]{:S(2)}) copy-start(f32[32640]{0:T(1024)S(1)} %collective-permute-done.3) | copy-start | bytes 391684
  61.8 1.5 copy-start
  61.8 1.8 %copy-start.1 = (f32[12,68,256]{2,1,0:T(8,128)S(1)}, f32[12,68,256]{2,1,0:T(8,128)}, u32[]{:S(2)}) copy-start(f32[12,68,256]{2,1,0:T(8,128)} %get-tuple-element.43) | copy-start | bytes 2506756
  61.8 1.8 %copy-start.33 = (f32[12,2,256]{2,1,0:T(2,128)S(1)}, f32[12,2,256]{2,1,0:T(2,128)}, u32[]{:S(2)}) copy-start(f32[12,2,256]{2,1,0:T(2,128)} %reshape.751) | copy-start | bytes 73732
  61.8 1.8 %copy-start.34 = (f32[12,2,256]{2,1,0:T(2,128)S(1)}, f32[12,2,256]{2,1,0:T(2,128)}, u32[]{:S(2)}) copy-start(f32[12,2,256]{2,1,0:T(2,128)} %reshape.752) | copy-start | bytes 73732
  61.9 1.8 %copy-start.41 = (pred[12,68]{1,0:T(8,128)(4,1)S(1)}, pred[12,68]{1,0:T(8,128)(4,1)}, u32[]{:S(2)}) copy-start(pred[12,68]{1,0:T(8,128)(4,1)} %broadcast_and_fusion) | copy-start | bytes 2452
  63.6 2.8 %copy-start.2 = (f32[12,68,256]{2,1,0:T(8,128)S(1)}, f32[12,68,256]{2,1,0:T(8,128)}, u32[]{:S(2)}) copy-start(f32[12,68,256]{2,1,0:T(8,128)} %get-tuple-element.37) | copy-start | bytes 2506756
  63.6 2.8 %copy-start.40 = (pred[10,66]{1,0:T(8,128)(4,1)S(1)}, pred[10,66]{1,0:T(8,128)(4,1)}, u32[]{:S(2)}) copy-start(pred[10,66]{1,0:T(8,128)(4,1)} %and_bitcast_fusion) | copy-start | bytes 1984
  66.4 1.9 %copy-start.4 = (f32[8,64,256]{2,1,0:T(8,128)S(1)}, f32[8,64,256]{2,1,0:T(8,128)}, u32[]{:S(2)}) copy-start(f32[8,64,256]{2,1,0:T(8,128)} %param.4) | copy-start | bytes 1572868
  68.3 1.7 %copy-start.47 = (s32[256]{0:T(256)S(1)}, s32[256]{0:T(256)}, u32[]{:S(2)}) copy-start(s32[256]{0:T(256)} %copy-done.46) | copy-start | bytes 3076
  68.3 2.0 %copy-start.30 = (f32[32,64]{1,0:T(8,128)S(1)}, f32[32,64]{1,0:T(8,128)}, u32[]{:S(2)}) copy-start(f32[32,64]{1,0:T(8,128)} %copy-done.29) | copy-start | bytes 24580
  68.3 7.2 %copy-start.8 = (f32[4,32,128]{2,1,0:T(8,128)S(1)}, f32[4,32,128]{2,1,0:T(8,128)}, u32[]{:S(2)}) copy-start(f32[4,32,128]{2,1,0:T(8,128)} %copy-done.7) | copy-start | bytes 196612
  68.3 7.2 %copy-start.22 = (f32[12288]{0:T(1024)S(1)}, f32[12288]{0:T(1024)}, u32[]{:S(2)}) copy-start(f32[12288]{0:T(1024)} %copy-done.21) | copy-start | bytes 147460
  68.3 7.2 %copy-start.24 = (f32[12288]{0:T(1024)S(1)}, f32[12288]{0:T(1024)}, u32[]{:S(2)}) copy-start(f32[12288]{0:T(1024)} %copy-done.23) | copy-start | bytes 147460
  68.3 7.2 %copy-start.35 = (f32[10,3,128]{2,1,0:T(4,128)S(1)}, f32[10,3,128]{2,1,0:T(4,128)}, u32[]{:S(2)}) copy-start(f32[10,3,128]{2,1,0:T(4,128)} %slice.982) | copy-start | bytes 46084
  68.3 7.2 %copy-start.36 = (f32[10,3,128]{2,1,0:T(4,128)S(1)}, f32[10,3,128]{2,1,0:T(4,128)}, u32[]{:S(2)}) copy-start(f32[10,3,128]{2,1,0:T(4,128)} %slice.984) | copy-start | bytes 46084
  69.9 15.4 %copy-start.14 = (f32[2,16,64]{2,1,0:T(8,128)S(1)}, f32[2,16,64]{2,1,0:T(8,128)}, u32[]{:S(2)}) copy-start(f32[2,16,64]{2,1,0:T(8,128)} %copy-done.13) | copy-start | bytes 24580
  69.9 15.4 %copy-start.16 = (f32[2,16,64]{2,1,0:T(8,128)S(1)}, f32[2,16,64]{2,1,0:T(8,128)}, u32[]{:S(2)}) copy-start(f32[2,16,64]{2,1,0:T(8,128)} %copy-done.15) | copy-start | bytes 24580
  70.0 17.9 %copy-start.44 = (pred[8,36]{1,0:T(8,128)(4,1)S(1)}, pred[8,36]{1,0:T(8,128)(4,1)}, u32[]{:S(2)}) copy-start(pred[8,36]{1,0:T(8,128)(4,1)} %broadcast_and_fusion.3) | copy-start | bytes 868
  70.5 6.6 %collective-permute-start.4 = (f32[8192]{0:T(1024)S(1)}, f32[8192]{0:T(1024)S(1)}, u32[]{:S(2)}, u32[]{:S(2)}) collective-permute-start(f32[8192]{0:T(1024)S(1)} %bitcast.159), channel_id=1, source_target_pairs={{0,8},{8,16},{16,24},{24,32},{32,40},{40,48},{48,56},{56,64},{64,7... | collective-permute-start | bytes 98312 | tf_op jit(solution)/shard_map/ppermute | solution.py:47
  74.1 5.8 %collective-permute-start.5 = (f32[8192]{0:T(1024)S(1)}, f32[8192]{0:T(1024)S(1)}, u32[]{:S(2)}, u32[]{:S(2)}) collective-permute-start(f32[8192]{0:T(1024)S(1)} %bitcast.158), channel_id=1, source_target_pairs={{8,0},{16,8},{24,16},{32,24},{40,32},{48,40},{56,48},{64,56},{72,6... | collective-permute-start | bytes 98312 | tf_op jit(solution)/shard_map/ppermute | solution.py:47
  80.0 5.5 %collective-permute-start.6 = (f32[2048]{0:T(1024)S(1)}, f32[2048]{0:T(1024)S(1)}, u32[]{:S(2)}, u32[]{:S(2)}) collective-permute-start(f32[2048]{0:T(1024)S(1)} %bitcast.163), channel_id=1, source_target_pairs={{0,1},{1,2},{2,3},{3,4},{4,5},{5,6},{6,7},{8,9},{9,10},{10,11},{11... | collective-permute-start | bytes 24584 | tf_op jit(solution)/shard_map/ppermute | solution.py:47
  84.0 3.9 %collective-permute-start.7 = (f32[2048]{0:T(1024)S(1)}, f32[2048]{0:T(1024)S(1)}, u32[]{:S(2)}, u32[]{:S(2)}) collective-permute-start(f32[2048]{0:T(1024)S(1)} %bitcast.162), channel_id=1, source_target_pairs={{1,0},{2,1},{3,2},{4,3},{5,4},{6,5},{7,6},{9,8},{10,9},{11,10},{12... | collective-permute-start | bytes 24584 | tf_op jit(solution)/shard_map/ppermute | solution.py:47
  88.8 17.9 %copy-start.49 = (pred[6,20]{1,0:T(8,128)(4,1)S(1)}, pred[6,20]{1,0:T(8,128)(4,1)}, u32[]{:S(2)}) copy-start(pred[6,20]{1,0:T(8,128)(4,1)} %broadcast_and_fusion.1) | copy-start | bytes 364
  89.9 17.1 %copy-start.55 = (pred[4,18]{1,0:T(4,128)(4,1)S(1)}, pred[4,18]{1,0:T(4,128)(4,1)}, u32[]{:S(2)}) copy-start(pred[4,18]{1,0:T(4,128)(4,1)} %slice_bitcast_fusion.15) | copy-start | bytes 220
  90.0 5.4 %collective-permute-start.8 = (f32[3456]{0:T(1024)S(1)}, f32[3456]{0:T(1024)S(1)}, u32[]{:S(2)}, u32[]{:S(2)}) collective-permute-start(f32[3456]{0:T(1024)S(1)} %get-tuple-element.84), channel_id=1, source_target_pairs={{0,8},{8,16},{16,24},{24,32},{32,40},{40,48},{48,56},{56,64},{64,7... | collective-permute-start | bytes 41480 | tf_op jit(solution)/shard_map/ppermute | solution.py:47
  93.9 5.6 %collective-permute-start.9 = (f32[3456]{0:T(1024)S(1)}, f32[3456]{0:T(1024)S(1)}, u32[]{:S(2)}, u32[]{:S(2)}) collective-permute-start(f32[3456]{0:T(1024)S(1)} %get-tuple-element.85), channel_id=1, source_target_pairs={{8,0},{16,8},{24,16},{32,24},{40,32},{48,40},{56,48},{64,56},{72,6... | collective-permute-start | bytes 41480 | tf_op jit(solution)/shard_map/ppermute | solution.py:47
  99.7 4.8 %collective-permute-start.10 = (f32[768]{0:T(1024)S(1)}, f32[768]{0:T(1024)S(1)}, u32[]{:S(2)}, u32[]{:S(2)}) collective-permute-start(f32[768]{0:T(1024)S(1)} %reshape.772), channel_id=1, source_target_pairs={{0,1},{1,2},{2,3},{3,4},{4,5},{5,6},{6,7},{8,9},{9,10},{10,11},{11... | collective-permute-start | bytes 9224 | tf_op jit(solution)/shard_map/ppermute | solution.py:47
  102.9 3.7 %collective-permute-start.11 = (f32[768]{0:T(1024)S(1)}, f32[768]{0:T(1024)S(1)}, u32[]{:S(2)}, u32[]{:S(2)}) collective-permute-start(f32[768]{0:T(1024)S(1)} %reshape.774), channel_id=1, source_target_pairs={{1,0},{2,1},{3,2},{4,3},{5,4},{6,5},{7,6},{9,8},{10,9},{11,10},{12... | collective-permute-start | bytes 9224 | tf_op jit(solution)/shard_map/ppermute | solution.py:47
  106.8 1.2 copy-start.48
  (8 other events, 7.1 us)

commit v4 on v2

--- a/solution.py
+++ b/solution.py
@@ -25,27 +25,25 @@
     for hop in range(1, reach + 1):
         for sign in (1, -1):
             pieces = []
-            for block, width in items:
+            owners = []
+            for index, (block, width) in enumerate(items):
                 size = block.shape[dim]
                 rows = min(size, width - (hop - 1) * size)
                 if rows <= 0:
-                    pieces.append(None)
-                elif sign == 1:
-                    pieces.append(lax.slice_in_dim(block, size - rows, size, axis=dim))
-                else:
-                    pieces.append(lax.slice_in_dim(block, 0, rows, axis=dim))
-            flat = jnp.concatenate([p.reshape(-1) for p in pieces if p is not None])
+                    continue
+                begin = size - rows if sign == 1 else 0
+                pieces.append(lax.slice_in_dim(block, begin, begin + rows, axis=dim))
+                owners.append(index)
+            joined = jnp.concatenate(pieces, axis=0)
             if sign == 1:
                 pairs = [(i, i + hop) for i in range(count - hop)]
             else:
                 pairs = [(i + hop, i) for i in range(count - hop)]
-            got = lax.ppermute(flat, axis, pairs)
+            got = lax.ppermute(joined, axis, pairs)
             offset = 0
-            for index, piece in enumerate(pieces):
-                if piece is None:
-                    continue
-                part = got[offset : offset + piece.size].reshape(piece.shape)
-                offset += piece.size
+            for index, piece in zip(owners, pieces):
+                part = lax.slice_in_dim(got, offset, offset + piece.shape[0], axis=0)
+                offset += piece.shape[0]
                 if sign == 1:
                     low[index].insert(0, part)
                 else:
@@ -57,9 +55,8 @@
 
 
 def exchange_xy(items):
-    widths = [width for _, width in items]
-    extended = exchange(items, "xb", 0)
-    return exchange(list(zip(extended, widths)), "yb", 1)
+    extended = exchange([(block, 3) for block, _ in items], "yb", 1)
+    return exchange([(block, item[1]) for block, item in zip(extended, items)], "xb", 0)
 
 
 def inside_mask(shape, halo):
@@ -208,18 +205,16 @@
 
 
 def per_device(initial_guess, right_side, coefficient):
+    guess_b, rhs_b, coef_b = exchange_xy([(initial_guess, 3), (right_side, 2), (coefficient, 3)])
+    fine, fine_res = smooth_box(guess_b, rhs_b[:, 1:-1], coef_b, 1.0, right_side.shape)
     mid_coef = restrict_field(coefficient)
+    mid_rhs = restrict_field(fine_res)
+    mid_rhs_b, mid_coef_b = exchange_xy([(mid_rhs, 2), (mid_coef, 3)])
+    middle, mid_res = smooth_box(None, mid_rhs_b[:, 1:-1], mid_coef_b, 0.25, mid_rhs.shape)
     low_coef = restrict_field(mid_coef)
-    guess_b, rhs_b, coef_b, mid_coef_b, low_coef_b = exchange_xy(
-        [(initial_guess, 3), (right_side, 2), (coefficient, 3), (mid_coef, 3), (low_coef, 3)]
-    )
-    fine, fine_res = smooth_box(guess_b, rhs_b, coef_b, 1.0, right_side.shape)
-    mid_rhs = restrict_field(fine_res)
-    (mid_rhs_b,) = exchange_xy([(mid_rhs, 2)])
-    middle, mid_res = smooth_box(None, mid_rhs_b, mid_coef_b, 0.25, mid_rhs.shape)
     low_rhs = restrict_field(mid_res)
-    (low_rhs_b,) = exchange_xy([(low_rhs, 2)])
-    lower, low_res = smooth_box(None, low_rhs_b, low_coef_b, 0.0625, low_rhs.shape)
+    low_rhs_b, low_coef_b = exchange_xy([(low_rhs, 2), (low_coef, 3)])
+    lower, low_res = smooth_box(None, low_rhs_b[:, 1:-1], low_coef_b, 0.0625, low_rhs.shape)
     coarse_rhs, coarse_coef = collect_grid(restrict_field(low_res), restrict_field(low_coef))
     coarse_whole = coarse_solve(coarse_rhs, coarse_coef, 0.015625, extend_all)
     sx, sy, sz = right_side.shape

time: 153 us -> 139 us (0.908)
  local copies, waits for them, and re-layouts: 27.1 us -> 5.48 us
  waiting for transfers between devices: 17.4 us -> 32.5 us
  starting transfers between devices: 36.5 us -> 33.7 us
  matrix products: 3.77 us -> 2.18 us
    ppermute x14, waiting for transfers between devices: 17.4 us -> 32.5 us  [exchange(): got = lax.ppermute(joined, axis, pairs)]
    slice x36 -> x26, local copies, waits for them, and re-layouts: 12.7 us -> 1 us  [the longest x1 0.41 us: restrict_field(): summed = halves[:, 0] + halves[:, 1]]
    reshape x32 -> x1, local copies, waits for them, and re-layouts: 5.66 us -> 0.31 us  [restrict_field(): halves = field.reshape(sx // 2, 2, sy, sz)]
    unnamed x139 -> x34, local copies, waits for them, and re-layouts: 7.57 us -> 3.57 us
    ppermute x14, starting transfers between devices: 36.5 us -> 33.7 us  [exchange(): got = lax.ppermute(joined, axis, pairs)]
  transfers between devices with their start and end apart: 14 -> 14, of which waited for: 6 -> 8; matrix products, arithmetic and copies ran while one was open for 6% -> 4% of each run, Pallas kernels for 0% -> 0%
where the time goes in v4:
time: 139 us; the launch traced here: 137 us
  blocking collectives  37.5 us (27%)
  starting transfers between devices  33.7 us (24%)
  waiting for transfers between devices  32.5 us (23%)
  other arithmetic  22.7 us (16%)
  local copies, waits for them, and re-layouts  5.48 us (4%)
  between operations  2.9 us (2%)
  matrix products  2.18 us (2%)
    all_gather x1, blocking collectives, collect_grid(): both = lax.all_gather(flat, ('xb', 'yb'), axis=0, tiled=True)  37.5 us
    ppermute x14, starting transfers between devices, exchange(): got = lax.ppermute(joined, axis, pairs)  33.7 us
    ppermute x14, waiting for transfers between devices, exchange(): got = lax.ppermute(joined, axis, pairs)  32.5 us
    add x7, other arithmetic, coarse_solve(): field + jacobi_weight * (right_side - apply_operator(extend(field), field...  4.78 us
    unnamed x34, local copies, waits for them, and re-layouts  3.57 us
    select_n x3, other arithmetic, smooth_box(): second = jnp.where(inside_mask(shape, 1), trim(first) + second_step, 0.0)  2.97 us
  transfers between devices with their start and end apart: 14, of which 8 were waited for; matrix products, arithmetic and copies ran while one was open for 4% of the time, Pallas kernels for 0%

profile of v4, /device:TPU:0, one launch (start us, length us, event | category | flops | bytes accessed | tf_op | source)
XLA Modules:
  0.0 137.0 jit_solution(16238281091451302690)
XLA Ops:
  0.7 1.4 %copy.7 = f32[8,64,256]{2,0,1:T(8,128)S(1)} copy(f32[8,64,256]{2,1,0:T(8,128)} %param.3) | data formatting | bytes 1048576 | tf_op args[0]
  2.1 0.3 copy.8
  2.4 0.3 copy.9
  2.8 1.3 collective-permute-start
  4.1 1.3 collective-permute-start.1
  5.7 0.3 fusion.214
  6.0 0.2 convolution_multiply_fusion
  6.2 0.2 fusion.283
  6.8 0.6 broadcast_and_fusion.3
  7.5 0.6 broadcast_and_fusion.4
  8.2 0.7 broadcast_and_fusion.2
  8.9 0.2 collective-permute-done.1
  9.4 1.2 fusion.35
  10.6 4.2 %collective-permute-start.2 = (f32[8,70,256]{2,0,1:T(8,128)}, f32[8,70,256]{2,0,1:T(8,128)S(1)}, u32[]{:S(2)}, u32[]{:S(2)}) collective-permute-start(f32[8,70,256]{2,0,1:T(8,128)} %get-tuple-element.54), channel_id=1, source_target_pairs={{0,8},{8,16},{16,24},{24,32},{32,40},{40,48},{48,56},{56,64},{64,7... | collective-permute-start | bytes 1720328 | tf_op jit(solution)/shard_map/ppermute | solution.py:42
  14.8 0.5 compare_and_fusion.3
  15.4 1.3 collective-permute-start.3
  16.7 0.5 compare_and_fusion.2
  17.2 9.6 %collective-permute-done.2 = f32[8,70,256]{2,0,1:T(8,128)S(1)} collective-permute-done((f32[8,70,256]{2,0,1:T(8,128)}, f32[8,70,256]{2,0,1:T(8,128)S(1)}, u32[]{:S(2)}, u32[]{:S(2)}) %collective-permute-start.2) | collective-permute-done | bytes 573472 | tf_op jit(solution)/shard_map/ppermute | solution.py:42
  26.9 4.7 %collective-permute-done.3 = f32[8,70,256]{2,0,1:T(8,128)S(1)} collective-permute-done((f32[8,70,256]{2,0,1:T(8,128)S(1)}, f32[8,70,256]{2,0,1:T(8,128)S(1)}, u32[]{:S(2)}, u32[]{:S(2)}) %collective-permute-start.3) | collective-permute-done | bytes 573472 | tf_op jit(solution)/shard_map/ppermute | solution.py:42
  31.7 0.2 pad_maximum_fusion.2
  31.9 1.4 %add_add_fusion = (f32[12,68,256]{2,0,1:T(8,128)S(1)}, f32[12,68,256]{2,0,1:T(8,128)S(1)}, f32[12,68,256]{2,0,1:T(8,128)S(1)}, f32[12,68,256]{2,0,1:T(8,128)S(1)...) fusion(f32[14,70,256]{2,0,1:T(8,128)S(1)} %pad_maximum_fusion.2), kind=kLoop, calls=%fused_computation.52 | loop fusion | flops 3760128 | bytes 12566528 | tf_op jit(solution)/shard_map/add | solution.py:95
  33.5 0.2 pad_maximum_fusion.1
  33.7 0.2 pad_maximum_fusion
  33.9 2.2 %add_select_fusion = (f32[12,68,256]{2,0,1:T(8,128)S(1)}, f32[12,68,256]{2,0,1:T(8,128)S(1)}) fusion(f32[14,70,256]{2,0,1:T(8,128)S(1)} %pad_maximum_fusion, pred[12,68]{0,1:T(8,128)(4,1)S(1)} %broadcast_and_fusion, f32[12,68,256]{2,0,1:T(8,128)S(1)} %get-tuple-element.44, f32[12,68,256]{2,0,1:T(8,128)S(1)} %get-tuple-element.45, ...), kind=kLoop, calls=%fused_computation.51 | loop fusion | flops 5013504 | bytes 16196608 | tf_op jit(solution)/shard_map/jit(_where)/select_n | solution.py:171
  36.1 2.6 %fusion.31 = f32[10,66,256]{2,0,1:T(8,128)S(1)} fusion(f32[12,68,256]{2,0,1:T(8,128)S(1)} %get-tuple-element.46, f32[12,68,256]{2,0,1:T(8,128)S(1)} %get-tuple-element.44, f32[12,68,256]{2,0,1:T(8,128)S(1)} %get-tuple-element.45, f32[12,68,256]{2,0,1:T(8,128)S(1)} %get-tuple-element.43, f32[12,68,256]{2,0,1:T(8,128)S(1)} %get-tuple-element.42, ...), kind=kLoop, calls=%fused_computation.75 | loop fusion | flops 3379200 | bytes 16937984 | tf_op jit(solution)/shard_map/jit(_where)/select_n | solution.py:177
  38.7 1.1 fusion.177
  39.8 0.3 reshape.570
  40.1 0.4 fusion.351
  40.5 0.3 fusion.217
  40.9 0.2 convolution_multiply_fusion.1
  41.1 3.2 %collective-permute-start.4 = (f32[8,3,128]{2,1,0:T(4,128)S(1)}, f32[8,3,128]{2,1,0:T(4,128)S(1)}, u32[]{:S(2)}, u32[]{:S(2)}) collective-permute-start(f32[8,3,128]{2,1,0:T(4,128)S(1)} %pad_maximum_fusion.25), channel_id=1, source_target_pairs={{0,1},{1,2},{2,3},{3,4},{4,5},{5,6},{6,7},{8,9},{9,10},{10,11},{11... | collective-permute-start | bytes 36872 | tf_op jit(solution)/shard_map/ppermute | solution.py:42
  44.4 1.3 collective-permute-start.5
  45.7 4.6 %collective-permute-done.5 = f32[8,3,128]{2,1,0:T(4,128)S(1)} collective-permute-done((f32[8,3,128]{2,1,0:T(4,128)S(1)}, f32[8,3,128]{2,1,0:T(4,128)S(1)}, u32[]{:S(2)}, u32[]{:S(2)}) %collective-permute-start.5) | collective-permute-done | bytes 12320 | tf_op jit(solution)/shard_map/ppermute | solution.py:42
  50.4 3.6 %collective-permute-start.6 = (f32[5,38,128]{2,1,0:T(8,128)S(1)}, f32[5,38,128]{2,1,0:T(8,128)S(1)}, u32[]{:S(2)}, u32[]{:S(2)}) collective-permute-start(f32[5,38,128]{2,1,0:T(8,128)S(1)} %pad_maximum_fusion.7), channel_id=1, source_target_pairs={{0,8},{8,16},{16,24},{24,32},{32,40},{40,48},{48,56},{56,64},{64,7... | collective-permute-start | bytes 291848 | tf_op jit(solution)/shard_map/ppermute | solution.py:42
  54.1 1.3 collective-permute-start.7
  55.5 1.0 copy.25
  56.5 4.1 %collective-permute-done.7 = f32[5,38,128]{2,1,0:T(8,128)S(1)} collective-permute-done((f32[5,38,128]{2,1,0:T(8,128)S(1)}, f32[5,38,128]{2,1,0:T(8,128)S(1)}, u32[]{:S(2)}, u32[]{:S(2)}) %collective-permute-start.7) | collective-permute-done | bytes 97312 | tf_op jit(solution)/shard_map/ppermute | solution.py:42
  60.7 0.2 broadcast_select_fusion
  60.9 0.4 copy-done.2
  61.4 0.3 fusion.244
  61.7 0.7 fusion.259
  62.7 3.0 %collective-permute-start.8 = (f32[4,3,64]{2,1,0:T(4,128)S(1)}, f32[4,3,64]{2,1,0:T(4,128)S(1)}, u32[]{:S(2)}, u32[]{:S(2)}) collective-permute-start(f32[4,3,64]{2,1,0:T(4,128)S(1)} %pad_maximum_fusion.27), channel_id=1, source_target_pairs={{0,1},{1,2},{2,3},{3,4},{4,5},{5,6},{6,7},{8,9},{9,10},{10,11},{11... | collective-permute-start | bytes 9224 | tf_op jit(solution)/shard_map/ppermute | solution.py:42
  65.7 1.3 collective-permute-start.9
  67.0 3.8 %collective-permute-done.9 = f32[4,3,64]{2,1,0:T(4,128)S(1)} collective-permute-done((f32[4,3,64]{2,1,0:T(4,128)S(1)}, f32[4,3,64]{2,1,0:T(4,128)S(1)}, u32[]{:S(2)}, u32[]{:S(2)}) %collective-permute-start.9) | collective-permute-done | bytes 3104 | tf_op jit(solution)/shard_map/ppermute | solution.py:42
  70.8 6.0 %collective-permute-start.13 = (f32[1,22,64]{2,1,0:T(8,128)S(1)}, f32[1,22,64]{2,1,0:T(8,128)S(1)}, u32[]{:S(2)}, u32[]{:S(2)}) collective-permute-start(f32[1,22,64]{2,1,0:T(8,128)S(1)} %get-tuple-element.90), channel_id=1, source_target_pairs={{0,16},{8,24},{16,32},{24,40},{32,48},{40,56},{48,64},{56,72},{64,... | collective-permute-start | bytes 16904 | tf_op jit(solution)/shard_map/ppermute | solution.py:42
  76.8 3.1 %collective-permute-start.10 = (f32[4,22,64]{2,1,0:T(8,128)S(1)}, f32[4,22,64]{2,1,0:T(8,128)S(1)}, u32[]{:S(2)}, u32[]{:S(2)}) collective-permute-start(f32[4,22,64]{2,1,0:T(8,128)S(1)} %maximum_maximum_fusion), channel_id=1, source_target_pairs={{0,8},{8,16},{16,24},{24,32},{32,40},{40,48},{48,56},{56,64},{64,7... | collective-permute-start | bytes 67592 | tf_op jit(solution)/shard_map/ppermute | solution.py:42
  79.9 1.3 collective-permute-start.11
  81.2 1.5 %collective-permute-start.12 = (f32[1,22,64]{2,1,0:T(8,128)S(1)}, f32[1,22,64]{2,1,0:T(8,128)S(1)}, u32[]{:S(2)}, u32[]{:S(2)}) collective-permute-start(f32[1,22,64]{2,1,0:T(8,128)S(1)} %get-tuple-element.91), channel_id=1, source_target_pairs={{16,0},{24,8},{32,16},{40,24},{48,32},{56,40},{64,48},{72,56},{80,... | collective-permute-start | bytes 16904 | tf_op jit(solution)/shard_map/ppermute | solution.py:42
  82.8 3.1 %collective-permute-done.11 = f32[4,22,64]{2,1,0:T(8,128)S(1)} collective-permute-done((f32[4,22,64]{2,1,0:T(8,128)S(1)}, f32[4,22,64]{2,1,0:T(8,128)S(1)}, u32[]{:S(2)}, u32[]{:S(2)}) %collective-permute-start.11) | collective-permute-done | bytes 22560 | tf_op jit(solution)/shard_map/ppermute | solution.py:42
  86.0 2.4 %collective-permute-done.12 = f32[1,22,64]{2,1,0:T(8,128)S(1)} collective-permute-done((f32[1,22,64]{2,1,0:T(8,128)S(1)}, f32[1,22,64]{2,1,0:T(8,128)S(1)}, u32[]{:S(2)}, u32[]{:S(2)}) %collective-permute-start.12) | collective-permute-done | bytes 5664 | tf_op jit(solution)/shard_map/ppermute | solution.py:42
  88.6 0.6 fusion.298
  89.6 37.5 %all-gather = f32[128,1,512]{2,1,0:T(1,128)S(1)} all-gather(f32[1,1,512]{2,1,0:T(1,128)S(1)} %maximum_bitcast_fusion), channel_id=1, replica_groups=mesh['xb'=16,'yb'=8] {'xb','yb'}, dimensions={0}, use_global_device_ids=true | all-gather | bytes 264192 | tf_op jit(solution)/shard_map/all_gather | solution.py:189
  127.1 0.2 reshape_transpose_reshape.6
  127.3 0.2 reshape_transpose_reshape.7
  127.5 1.0 fusion.188
  128.5 0.7 fusion.59
  129.2 0.7 fusion.75
  129.9 0.7 fusion.91
  130.6 0.7 fusion.107
  131.3 0.7 fusion.123
  132.0 0.7 fusion.139
  132.6 0.7 fusion.155
  133.4 1.6 %fusion.210 = (f32[]{:T(128)}, f32[]{:T(128)}) fusion(f32[16,64,32]{2,1,0:T(8,128)S(1)} %get-tuple-element.11, f32[16,64,32]{2,1,0:T(8,128)S(1)} %broadcast_in_dim.143, f32[16,64,32]{2,1,0:T(8,128)S(1)} %get-tuple-element.12, f32[16,64,32]{2,1,0:T(8,128)S(1)} %get-tuple-element.13, f32[16,64,32]{2,1,0:T(8,128)S(1)} %get-tuple-element.14, ...), kind=kLoop, calls=%fused_computation.322 | loop fusion | flops 1114110 | bytes 1179656 | tf_op jit(solution)/shard_map/reduce_sum | solution.py:155
  136.4 0.6 dynamic-slice_add_fusion
  (115 shorter events, 2.8 us)
Async XLA Ops:
  0.6 1.5 %copy-start = (f32[8,64,256]{2,1,0:T(8,128)S(1)}, f32[8,64,256]{2,1,0:T(8,128)}, u32[]{:S(2)}) copy-start(f32[8,64,256]{2,1,0:T(8,128)} %param.4) | copy-start | bytes 1572868
  0.6 1.8 %copy-start.1 = (f32[8,64,256]{2,1,0:T(8,128)S(1)}, f32[8,64,256]{2,1,0:T(8,128)}, u32[]{:S(2)}) copy-start(f32[8,64,256]{2,1,0:T(8,128)} %param.5) | copy-start | bytes 1572868
  2.8 6.1 %collective-permute-start = (f32[24,3,256]{2,0,1:T(8,128)S(1)}, f32[24,3,256]{2,0,1:T(8,128)S(1)}, u32[]{:S(2)}, u32[]{:S(2)}) collective-permute-start(f32[24,3,256]{2,0,1:T(8,128)S(1)} %pad_maximum_fusion.20), channel_id=1, source_target_pairs={{0,1},{1,2},{2,3},{3,4},{4,5},{5,6},{6,7},{8,9},{9,10},{10,11},{11... | collective-permute-start | bytes 221192 | tf_op jit(solution)/shard_map/ppermute | solution.py:42
  4.1 5.0 %collective-permute-start.1 = (f32[24,3,256]{2,0,1:T(8,128)S(1)}, f32[24,3,256]{2,0,1:T(8,128)S(1)}, u32[]{:S(2)}, u32[]{:S(2)}) collective-permute-start(f32[24,3,256]{2,0,1:T(8,128)S(1)} %pad_maximum_fusion.21), channel_id=1, source_target_pairs={{1,0},{2,1},{3,2},{4,3},{5,4},{6,5},{7,6},{9,8},{10,9},{11,10},{12... | collective-permute-start | bytes 221192 | tf_op jit(solution)/shard_map/ppermute | solution.py:42
  5.4 1.2 copy-start.4
  5.5 1.2 copy-start.7
  5.5 3.6 %copy-start.9 = (s32[16]{0:T(128)}, s32[16]{0:T(128)S(1)}, u32[]{:S(2)}) copy-start(s32[16]{0:T(128)S(1)} %and_select_fusion) | copy-start | bytes 196
  10.6 16.2 %collective-permute-start.2 = (f32[8,70,256]{2,0,1:T(8,128)}, f32[8,70,256]{2,0,1:T(8,128)S(1)}, u32[]{:S(2)}, u32[]{:S(2)}) collective-permute-start(f32[8,70,256]{2,0,1:T(8,128)} %get-tuple-element.54), channel_id=1, source_target_pairs={{0,8},{8,16},{16,24},{24,32},{32,40},{40,48},{48,56},{56,64},{64,7... | collective-permute-start | bytes 1720328 | tf_op jit(solution)/shard_map/ppermute | solution.py:42
  15.4 16.2 %collective-permute-start.3 = (f32[8,70,256]{2,0,1:T(8,128)S(1)}, f32[8,70,256]{2,0,1:T(8,128)S(1)}, u32[]{:S(2)}, u32[]{:S(2)}) collective-permute-start(f32[8,70,256]{2,0,1:T(8,128)S(1)} %get-tuple-element.55), channel_id=1, source_target_pairs={{8,0},{16,8},{24,16},{32,24},{40,32},{48,40},{56,48},{64,56},{72,6... | collective-permute-start | bytes 1720328 | tf_op jit(solution)/shard_map/ppermute | solution.py:42
  39.8 0.8 copy-start.5
  40.5 14.9 %copy-start.11 = (pred[4]{0:T(512)(128)(4,1)S(1)}, pred[4]{0:T(512)(128)(4,1)}, u32[]{:S(2)}) copy-start(pred[4]{0:T(512)(128)(4,1)} %compare_and_fusion.3) | copy-start | bytes 16
  40.5 14.9 %copy-start.12 = (pred[18]{0:T(512)(128)(4,1)S(1)}, pred[18]{0:T(512)(128)(4,1)}, u32[]{:S(2)}) copy-start(pred[18]{0:T(512)(128)(4,1)} %compare_and_fusion.2) | copy-start | bytes 58
  41.1 4.6 %collective-permute-start.4 = (f32[8,3,128]{2,1,0:T(4,128)S(1)}, f32[8,3,128]{2,1,0:T(4,128)S(1)}, u32[]{:S(2)}, u32[]{:S(2)}) collective-permute-start(f32[8,3,128]{2,1,0:T(4,128)S(1)} %pad_maximum_fusion.25), channel_id=1, source_target_pairs={{0,1},{1,2},{2,3},{3,4},{4,5},{5,6},{6,7},{8,9},{9,10},{10,11},{11... | collective-permute-start | bytes 36872 | tf_op jit(solution)/shard_map/ppermute | solution.py:42
  44.4 5.9 %collective-permute-start.5 = (f32[8,3,128]{2,1,0:T(4,128)S(1)}, f32[8,3,128]{2,1,0:T(4,128)S(1)}, u32[]{:S(2)}, u32[]{:S(2)}) collective-permute-start(f32[8,3,128]{2,1,0:T(4,128)S(1)} %pad_maximum_fusion.26), channel_id=1, source_target_pairs={{1,0},{2,1},{3,2},{4,3},{5,4},{6,5},{7,6},{9,8},{10,9},{11,10},{12... | collective-permute-start | bytes 36872 | tf_op jit(solution)/shard_map/ppermute | solution.py:42
  50.4 6.1 %collective-permute-start.6 = (f32[5,38,128]{2,1,0:T(8,128)S(1)}, f32[5,38,128]{2,1,0:T(8,128)S(1)}, u32[]{:S(2)}, u32[]{:S(2)}) collective-permute-start(f32[5,38,128]{2,1,0:T(8,128)S(1)} %pad_maximum_fusion.7), channel_id=1, source_target_pairs={{0,8},{8,16},{16,24},{24,32},{32,40},{40,48},{48,56},{56,64},{64,7... | collective-permute-start | bytes 291848 | tf_op jit(solution)/shard_map/ppermute | solution.py:42
  54.1 6.6 %copy-start.3 = (pred[8,36]{1,0:T(8,128)(4,1)S(1)}, pred[8,36]{1,0:T(8,128)(4,1)}, u32[]{:S(2)}) copy-start(pred[8,36]{1,0:T(8,128)(4,1)} %broadcast_and_fusion.3) | copy-start | bytes 868
  54.1 6.6 %collective-permute-start.7 = (f32[5,38,128]{2,1,0:T(8,128)S(1)}, f32[5,38,128]{2,1,0:T(8,128)S(1)}, u32[]{:S(2)}, u32[]{:S(2)}) collective-permute-start(f32[5,38,128]{2,1,0:T(8,128)S(1)} %pad_maximum_fusion.8), channel_id=1, source_target_pairs={{8,0},{16,8},{24,16},{32,24},{40,32},{48,40},{56,48},{64,56},{72,6... | collective-permute-start | bytes 291848 | tf_op jit(solution)/shard_map/ppermute | solution.py:42
  60.7 0.7 copy-start.2
  61.4 1.0 copy-start.8
  61.7 26.7 %copy-start.6 = (pred[6,20]{1,0:T(8,128)(4,1)S(1)}, pred[6,20]{1,0:T(8,128)(4,1)}, u32[]{:S(2)}) copy-start(pred[6,20]{1,0:T(8,128)(4,1)} %broadcast_and_fusion.2) | copy-start | bytes 364
  62.7 4.3 %collective-permute-start.8 = (f32[4,3,64]{2,1,0:T(4,128)S(1)}, f32[4,3,64]{2,1,0:T(4,128)S(1)}, u32[]{:S(2)}, u32[]{:S(2)}) collective-permute-start(f32[4,3,64]{2,1,0:T(4,128)S(1)} %pad_maximum_fusion.27), channel_id=1, source_target_pairs={{0,1},{1,2},{2,3},{3,4},{4,5},{5,6},{6,7},{8,9},{9,10},{10,11},{11... | collective-permute-start | bytes 9224 | tf_op jit(solution)/shard_map/ppermute | solution.py:42
  65.7 5.1 %collective-permute-start.9 = (f32[4,3,64]{2,1,0:T(4,128)S(1)}, f32[4,3,64]{2,1,0:T(4,128)S(1)}, u32[]{:S(2)}, u32[]{:S(2)}) collective-permute-start(f32[4,3,64]{2,1,0:T(4,128)S(1)} %pad_maximum_fusion.28), channel_id=1, source_target_pairs={{1,0},{2,1},{3,2},{4,3},{5,4},{6,5},{7,6},{9,8},{10,9},{11,10},{12... | collective-permute-start | bytes 9224 | tf_op jit(solution)/shard_map/ppermute | solution.py:42
  70.8 11.9 %collective-permute-start.13 = (f32[1,22,64]{2,1,0:T(8,128)S(1)}, f32[1,22,64]{2,1,0:T(8,128)S(1)}, u32[]{:S(2)}, u32[]{:S(2)}) collective-permute-start(f32[1,22,64]{2,1,0:T(8,128)S(1)} %get-tuple-element.90), channel_id=1, source_target_pairs={{0,16},{8,24},{16,32},{24,40},{32,48},{40,56},{48,64},{56,72},{64,... | collective-permute-start | bytes 16904 | tf_op jit(solution)/shard_map/ppermute | solution.py:42
  76.8 6.0 %collective-permute-start.10 = (f32[4,22,64]{2,1,0:T(8,128)S(1)}, f32[4,22,64]{2,1,0:T(8,128)S(1)}, u32[]{:S(2)}, u32[]{:S(2)}) collective-permute-start(f32[4,22,64]{2,1,0:T(8,128)S(1)} %maximum_maximum_fusion), channel_id=1, source_target_pairs={{0,8},{8,16},{16,24},{24,32},{32,40},{40,48},{48,56},{56,64},{64,7... | collective-permute-start | bytes 67592 | tf_op jit(solution)/shard_map/ppermute | solution.py:42
  79.9 6.0 %collective-permute-start.11 = (f32[4,22,64]{2,1,0:T(8,128)S(1)}, f32[4,22,64]{2,1,0:T(8,128)S(1)}, u32[]{:S(2)}, u32[]{:S(2)}) collective-permute-start(f32[4,22,64]{2,1,0:T(8,128)S(1)} %maximum_maximum_fusion), channel_id=1, source_target_pairs={{8,0},{16,8},{24,16},{32,24},{40,32},{48,40},{56,48},{64,56},{72,6... | collective-permute-start | bytes 67592 | tf_op jit(solution)/shard_map/ppermute | solution.py:42
  81.2 7.1 %collective-permute-start.12 = (f32[1,22,64]{2,1,0:T(8,128)S(1)}, f32[1,22,64]{2,1,0:T(8,128)S(1)}, u32[]{:S(2)}, u32[]{:S(2)}) collective-permute-start(f32[1,22,64]{2,1,0:T(8,128)S(1)} %get-tuple-element.91), channel_id=1, source_target_pairs={{16,0},{24,8},{32,16},{40,24},{48,32},{56,40},{64,48},{72,56},{80,... | collective-permute-start | bytes 16904 | tf_op jit(solution)/shard_map/ppermute | solution.py:42
  88.3 1.0 copy-start.10

commit v5 on v4

--- a/solution.py
+++ b/solution.py
@@ -17,10 +17,11 @@
 jacobi_weight = 0.8
 
 
-def exchange(items, axis, dim):
+def exchange(items, axis, dim, forwards=()):
     count = lax.axis_size(axis)
     low = [[] for _ in items]
     high = [[] for _ in items]
+    boxes = [box for box, _, _ in forwards]
     reach = max(-(-width // block.shape[dim]) for block, width in items)
     for hop in range(1, reach + 1):
         for sign in (1, -1):
@@ -34,7 +35,19 @@
                 begin = size - rows if sign == 1 else 0
                 pieces.append(lax.slice_in_dim(block, begin, begin + rows, axis=dim))
                 owners.append(index)
-            joined = jnp.concatenate(pieces, axis=0)
+            if hop == 1:
+                for index, (box, rows_low, rows_high) in enumerate(forwards):
+                    rows = rows_low if sign == 1 else rows_high
+                    pieces.append(lax.slice_in_dim(box, rows[0], rows[1], axis=dim))
+                    owners.append(-1 - index)
+            common = [max(p.shape[d] for p in pieces) for d in (1, 2)]
+            joined = jnp.concatenate(
+                [
+                    jnp.pad(p, ((0, 0), (0, common[0] - p.shape[1]), (0, common[1] - p.shape[2])))
+                    for p in pieces
+                ],
+                axis=0,
+            )
             if sign == 1:
                 pairs = [(i, i + hop) for i in range(count - hop)]
             else:
@@ -42,30 +55,21 @@
             got = lax.ppermute(joined, axis, pairs)
             offset = 0
             for index, piece in zip(owners, pieces):
-                part = lax.slice_in_dim(got, offset, offset + piece.shape[0], axis=0)
+                part = got[offset : offset + piece.shape[0], : piece.shape[1], : piece.shape[2]]
                 offset += piece.shape[0]
-                if sign == 1:
+                if index < 0:
+                    box = boxes[-1 - index]
+                    parts = [part, box] if sign == 1 else [box, part]
+                    boxes[-1 - index] = jnp.concatenate(parts, axis=dim)
+                elif sign == 1:
                     low[index].insert(0, part)
                 else:
                     high[index].append(part)
-    return [
+    extended = [
         jnp.concatenate(low[i] + [block] + high[i], axis=dim)
         for i, (block, width) in enumerate(items)
     ]
-
-
-def exchange_xy(items):
-    extended = exchange([(block, 3) for block, _ in items], "yb", 1)
-    return exchange([(block, item[1]) for block, item in zip(extended, items)], "xb", 0)
-
-
-def inside_mask(shape, halo):
-    sx, sy, _ = shape
-    gx = lax.axis_index("xb") * sx - halo + jnp.arange(sx + 2 * halo)
-    gy = lax.axis_index("yb") * sy - halo + jnp.arange(sy + 2 * halo)
-    in_x = (gx >= 0) & (gx < sx * lax.axis_size("xb"))
-    in_y = (gy >= 0) & (gy < sy * lax.axis_size("yb"))
-    return in_x[:, None, None] & in_y[None, :, None]
+    return extended, boxes
 
 
 def pad_z(box):
@@ -159,8 +163,21 @@
     return jnp.pad(field, 1)
 
 
-def smooth_box(start, right_side, coefficient, scale, shape):
-    weights, diagonal = face_weights(pad_z(coefficient), scale)
+def box_weights(padded_coef, scale):
+    centre = padded_coef[1:-1, 1:-1, 1:-1]
+    outside = centre == 0.0
+    weights = [
+        jnp.where(outside, 0.0, 0.5 * scale * (centre + other))
+        for other in neighbours(padded_coef)
+    ]
+    diagonal = damping_alpha + weights[0]
+    for other in weights[1:]:
+        diagonal = diagonal + other
+    return (weights, diagonal)
+
+
+def smooth_box(start, right_side, coefficient, scale):
+    weights, diagonal = box_weights(pad_z(coefficient), scale)
     if start is None:
         start = jnp.zeros_like(right_side)
         residual = right_side
@@ -168,13 +185,13 @@
         residual = right_side - apply_operator(pad_z(start), trim(start), weights, diagonal)
         start = trim(start)
     first_step = residual / (cheb_theta * diagonal)
-    first = jnp.where(inside_mask(shape, 2), start + first_step, 0.0)
+    first = start + first_step
     weights = [trim(w) for w in weights]
     diagonal = trim(diagonal)
     right_side = trim(right_side)
     residual = right_side - apply_operator(pad_z(first), trim(first), weights, diagonal)
     second_step = cheb_carry * trim(first_step) + cheb_resid * residual / diagonal
-    second = jnp.where(inside_mask(shape, 1), trim(first) + second_step, 0.0)
+    second = trim(first) + second_step
     weights = [trim(w) for w in weights]
     diagonal = trim(diagonal)
     residual = trim(right_side) - apply_operator(pad_z(second), trim(second), weights, diagonal)
@@ -205,16 +222,31 @@
 
 
 def per_device(initial_guess, right_side, coefficient):
-    guess_b, rhs_b, coef_b = exchange_xy([(initial_guess, 3), (right_side, 2), (coefficient, 3)])
-    fine, fine_res = smooth_box(guess_b, rhs_b[:, 1:-1], coef_b, 1.0, right_side.shape)
     mid_coef = restrict_field(coefficient)
+    low_coef = restrict_field(mid_coef)
+    low_size = low_coef.shape[0]
+    low_first = min(3, low_size)
+    assert low_first == 3 or 2 * low_size >= 3
+    guess_b, rhs_b, coef_b, low_coef_b = exchange(
+        [(initial_guess, 3), (right_side, 3), (coefficient, 3), (low_coef, 3)], "yb", 1
+    )[0]
+    guess_b, rhs_b, coef_b = exchange([(guess_b, 3), (rhs_b, 2), (coef_b, 3)], "xb", 0)[0]
+    fine, fine_res = smooth_box(guess_b, rhs_b[:, 1:-1], coef_b, 1.0)
     mid_rhs = restrict_field(fine_res)
-    mid_rhs_b, mid_coef_b = exchange_xy([(mid_rhs, 2), (mid_coef, 3)])
-    middle, mid_res = smooth_box(None, mid_rhs_b[:, 1:-1], mid_coef_b, 0.25, mid_rhs.shape)
-    low_coef = restrict_field(mid_coef)
+    mid_rhs_b, mid_coef_b = exchange([(mid_rhs, 3), (mid_coef, 3)], "yb", 1)[0]
+    mid_rhs_b, mid_coef_b, low_coef_b = exchange(
+        [(mid_rhs_b, 2), (mid_coef_b, 3), (low_coef_b, low_first)], "xb", 0
+    )[0]
+    middle, mid_res = smooth_box(None, mid_rhs_b[:, 1:-1], mid_coef_b, 0.25)
     low_rhs = restrict_field(mid_res)
-    low_rhs_b, low_coef_b = exchange_xy([(low_rhs, 2), (low_coef, 3)])
-    lower, low_res = smooth_box(None, low_rhs_b[:, 1:-1], low_coef_b, 0.0625, low_rhs.shape)
+    (low_rhs_b,) = exchange([(low_rhs, 3)], "yb", 1)[0]
+    forwards = ()
+    if low_first < 3:
+        forwards = ((low_coef_b, (2 * low_size - 3, low_size), (2 * low_size, low_size + 3)),)
+    (low_rhs_b,), boxes = exchange([(low_rhs_b, 2)], "xb", 0, forwards)
+    if low_first < 3:
+        (low_coef_b,) = boxes
+    lower, low_res = smooth_box(None, low_rhs_b[:, 1:-1], low_coef_b, 0.0625)
     coarse_rhs, coarse_coef = collect_grid(restrict_field(low_res), restrict_field(low_coef))
     coarse_whole = coarse_solve(coarse_rhs, coarse_coef, 0.015625, extend_all)
     sx, sy, sz = right_side.shape

time: 139 us -> 132 us (0.950)
  starting transfers between devices: 33.7 us -> 27.4 us
  other arithmetic: 22.7 us -> 17.3 us
  waiting for transfers between devices: 32.5 us -> 35.2 us
    ppermute x14 -> x12, starting transfers between devices: 33.7 us -> 27.4 us  [exchange(): got = lax.ppermute(joined, axis, pairs)]
    select_n x6 -> x0, other arithmetic: 5.52 us -> none  [the longest x3 2.97 us: smooth_box(): second = jnp.where(inside_mask(shape, 1), trim(first) + second_step, 0.0)]
    add x1 -> x5, other arithmetic: 1.39 us -> 5.34 us  [the longest x3 2.52 us: smooth_box(): second = trim(first) + second_step]
    and x18 -> x0, other arithmetic: 3.31 us -> none  [the longest x6 2.17 us: inside_mask(): return in_x[:, None, None] & in_y[None, :, None]]
    ppermute x14 -> x12, waiting for transfers between devices: 32.5 us -> 35.2 us  [exchange(): got = lax.ppermute(joined, axis, pairs)]
    slice x11, local copies, waits for them, and re-layouts: 0.24 us -> 2.21 us  [exchange(): pieces.append(lax.slice_in_dim(block, begin, begin + rows, axis=dim))]
    unnamed x34 -> x17, local copies, waits for them, and re-layouts: 3.57 us -> 2.53 us
  transfers between devices with their start and end apart: 14 -> 12, of which waited for: 8 -> 8; matrix products, arithmetic and copies ran while one was open for 4% -> 2% of each run, Pallas kernels for 0% -> 0%
where the time goes in v5:
time: 132 us; the launch traced here: 130 us
  blocking collectives  37.7 us (29%)
  waiting for transfers between devices  35.2 us (27%)
  starting transfers between devices  27.4 us (21%)
  other arithmetic  17.3 us (13%)
  local copies, waits for them, and re-layouts  6.47 us (5%)
  matrix products  3.22 us (2%)
  between operations  2.7 us (2%)
    all_gather x1, blocking collectives, collect_grid(): both = lax.all_gather(flat, ('xb', 'yb'), axis=0, tiled=True)  37.7 us
    ppermute x12, waiting for transfers between devices, exchange(): got = lax.ppermute(joined, axis, pairs)  35.2 us
    ppermute x12, starting transfers between devices, exchange(): got = lax.ppermute(joined, axis, pairs)  27.4 us
    add x7, other arithmetic, coarse_solve(): field + jacobi_weight * (right_side - apply_operator(extend(field), field...  4.78 us
  transfers between devices with their start and end apart: 12, of which 8 were waited for; matrix products, arithmetic and copies ran while one was open for 2% of the time, Pallas kernels for 0%

profile of v5, /device:TPU:0, one launch (start us, length us, event | category | flops | bytes accessed | tf_op | source)
XLA Modules:
  0.0 130.1 jit_solution(3670351548719010459)
XLA Ops:
  0.7 0.9 fusion.367
  1.6 1.3 %fusion.214 = f32[4,64,128]{2,1,0:T(8,128)S(1)} fusion(f32[4,2,64,256]{3,2,1,0:T(8,128)} %bitcast.81, s32[256]{0:T(256)S(1)} %and_select_fusion.2), kind=kOutput, calls=%fused_computation.331 | convolution fusion | flops 100761600 | bytes 656384 | tf_op jit(solution)/shard_map/xyZ,zZ->xyz/dot_general | solution.py:136
  3.0 0.2 convolution_multiply_fusion.1
  3.2 0.2 fusion.299
  3.4 0.1 convolution_multiply_fusion.3
  3.5 1.0 fusion.365
  4.5 1.3 collective-permute-start
  5.9 1.3 collective-permute-start.1
  7.3 0.3 copy_dynamic-update-slice_fusion.1
  7.6 3.4 %collective-permute-done.1 = f32[26,3,256]{2,1,0:T(4,128)S(1)} collective-permute-done((f32[26,3,256]{2,1,0:T(4,128)S(1)}, f32[26,3,256]{2,1,0:T(4,128)S(1)}, u32[]{:S(2)}, u32[]{:S(2)}) %collective-permute-start.1) | collective-permute-done | bytes 79904 | tf_op jit(solution)/shard_map/ppermute | solution.py:55
  11.1 0.3 copy_dynamic-update-slice_fusion.2
  11.5 0.6 copy-done.1
  12.1 0.3 copy_dynamic-update-slice_fusion
  12.5 0.2 pad_maximum_fusion.3
  12.7 3.8 %collective-permute-start.2 = (f32[8,70,256]{2,0,1:T(8,128)S(1)}, f32[8,70,256]{2,0,1:T(8,128)S(1)}, u32[]{:S(2)}, u32[]{:S(2)}) collective-permute-start(f32[8,70,256]{2,0,1:T(8,128)S(1)} %pad_maximum_fusion.3), channel_id=1, source_target_pairs={{0,8},{8,16},{16,24},{24,32},{32,40},{40,48},{48,56},{56,64},{64,7... | collective-permute-start | bytes 1720328 | tf_op jit(solution)/shard_map/ppermute | solution.py:55
  16.6 0.2 pad_maximum_fusion.4
  16.8 1.3 collective-permute-start.3
  18.1 9.4 %collective-permute-done.2 = f32[8,70,256]{2,0,1:T(8,128)S(1)} collective-permute-done((f32[8,70,256]{2,0,1:T(8,128)S(1)}, f32[8,70,256]{2,0,1:T(8,128)S(1)}, u32[]{:S(2)}, u32[]{:S(2)}) %collective-permute-start.2) | collective-permute-done | bytes 573472 | tf_op jit(solution)/shard_map/ppermute | solution.py:55
  27.6 4.7 %collective-permute-done.3 = f32[8,70,256]{2,0,1:T(8,128)S(1)} collective-permute-done((f32[8,70,256]{2,0,1:T(8,128)S(1)}, f32[8,70,256]{2,0,1:T(8,128)S(1)}, u32[]{:S(2)}, u32[]{:S(2)}) %collective-permute-start.3) | collective-permute-done | bytes 573472 | tf_op jit(solution)/shard_map/ppermute | solution.py:55
  32.4 0.2 pad_maximum_fusion.2
  32.6 1.4 %add_add_fusion = (f32[12,68,256]{2,0,1:T(8,128)S(1)}, f32[12,68,256]{2,0,1:T(8,128)S(1)}, f32[12,68,256]{2,0,1:T(8,128)S(1)}, f32[12,68,256]{2,0,1:T(8,128)S(1)...) fusion(f32[14,70,256]{2,0,1:T(8,128)S(1)} %pad_maximum_fusion.2), kind=kLoop, calls=%fused_computation.57 | loop fusion | flops 5222400 | bytes 12566528 | tf_op jit(solution)/shard_map/add | solution.py:175
  34.1 0.2 pad_maximum_fusion.1
  34.4 0.2 pad_maximum_fusion
  34.6 1.5 %slice_add_fusion.4 = (f32[12,68,256]{2,0,1:T(8,128)S(1)}, f32[12,68,256]{2,0,1:T(8,128)S(1)}) fusion(f32[14,70,256]{2,0,1:T(8,128)S(1)} %pad_maximum_fusion, f32[12,68,256]{2,0,1:T(8,128)S(1)} %get-tuple-element.42, f32[12,68,256]{2,0,1:T(8,128)S(1)} %get-tuple-element.43, f32[12,68,256]{2,0,1:T(8,128)S(1)} %get-tuple-element.41, ...), kind=kLoop, calls=%fused_computation.80 | loop fusion | flops 4804608 | bytes 16187392 | tf_op jit(solution)/shard_map/add | solution.py:188
  36.0 2.2 %fusion.31 = f32[10,66,256]{2,0,1:T(8,128)S(1)} fusion(f32[12,68,256]{2,0,1:T(8,128)S(1)} %get-tuple-element.44, f32[12,68,256]{2,0,1:T(8,128)S(1)} %get-tuple-element.42, f32[12,68,256]{2,0,1:T(8,128)S(1)} %get-tuple-element.43, f32[12,68,256]{2,0,1:T(8,128)S(1)} %get-tuple-element.41, f32[12,68,256]{2,0,1:T(8,128)S(1)} %get-tuple-element.40, ...), kind=kLoop, calls=%fused_computation.69 | loop fusion | flops 3210240 | bytes 16928768 | tf_op jit(solution)/shard_map/add | solution.py:194
  38.2 1.1 fusion.177
  39.3 0.3 reshape.296
  39.6 0.4 fusion.364
  40.0 0.3 fusion.217
  40.4 0.2 convolution_multiply_fusion
  40.6 4.0 %collective-permute-start.4 = (f32[8,3,128]{2,1,0:T(4,128)S(1)}, f32[8,3,128]{2,1,0:T(4,128)S(1)}, u32[]{:S(2)}, u32[]{:S(2)}) collective-permute-start(f32[8,3,128]{2,1,0:T(4,128)S(1)} %pad_maximum_fusion.24), channel_id=1, source_target_pairs={{0,1},{1,2},{2,3},{3,4},{4,5},{5,6},{6,7},{8,9},{9,10},{10,11},{11... | collective-permute-start | bytes 36872 | tf_op jit(solution)/shard_map/ppermute | solution.py:55
  44.6 1.3 collective-permute-start.5
  45.9 4.0 %collective-permute-done.5 = f32[8,3,128]{2,1,0:T(4,128)S(1)} collective-permute-done((f32[8,3,128]{2,1,0:T(4,128)S(1)}, f32[8,3,128]{2,1,0:T(4,128)S(1)}, u32[]{:S(2)}, u32[]{:S(2)}) %collective-permute-start.5) | collective-permute-done | bytes 12320 | tf_op jit(solution)/shard_map/ppermute | solution.py:55
  50.1 4.0 %collective-permute-start.6 = (f32[7,38,128]{2,1,0:T(8,128)S(1)}, f32[7,38,128]{2,1,0:T(8,128)S(1)}, u32[]{:S(2)}, u32[]{:S(2)}) collective-permute-start(f32[7,38,128]{2,1,0:T(8,128)S(1)} %get-tuple-element.92), channel_id=1, source_target_pairs={{0,8},{8,16},{16,24},{24,32},{32,40},{40,48},{48,56},{56,64},{64,7... | collective-permute-start | bytes 408584 | tf_op jit(solution)/shard_map/ppermute | solution.py:55
  54.0 1.3 collective-permute-start.7
  55.5 1.2 collective-permute-done.6
  56.7 4.7 %collective-permute-done.7 = f32[7,38,128]{2,1,0:T(8,128)S(1)} collective-permute-done((f32[7,38,128]{2,1,0:T(8,128)S(1)}, f32[7,38,128]{2,1,0:T(8,128)S(1)}, u32[]{:S(2)}, u32[]{:S(2)}) %collective-permute-start.7) | collective-permute-done | bytes 136224 | tf_op jit(solution)/shard_map/ppermute | solution.py:55
  61.4 0.2 slice_divide_fusion
  61.7 0.2 fusion.246
  61.9 0.7 fusion.272
  62.6 0.2 fusion.295
  62.8 0.1 convolution_multiply_fusion.2
  62.9 3.0 %collective-permute-start.8 = (f32[2,3,64]{2,1,0:T(4,128)S(1)}, f32[2,3,64]{2,1,0:T(4,128)S(1)}, u32[]{:S(2)}, u32[]{:S(2)}) collective-permute-start(f32[2,3,64]{2,1,0:T(4,128)S(1)} %get-tuple-element.94), channel_id=1, source_target_pairs={{0,1},{1,2},{2,3},{3,4},{4,5},{5,6},{6,7},{8,9},{9,10},{10,11},{11... | collective-permute-start | bytes 4616 | tf_op jit(solution)/shard_map/ppermute | solution.py:55
  65.9 1.3 collective-permute-start.9
  67.2 3.3 %collective-permute-done.9 = f32[2,3,64]{2,1,0:T(4,128)S(1)} collective-permute-done((f32[2,3,64]{2,1,0:T(4,128)S(1)}, f32[2,3,64]{2,1,0:T(4,128)S(1)}, u32[]{:S(2)}, u32[]{:S(2)}) %collective-permute-start.9) | collective-permute-done | bytes 1568 | tf_op jit(solution)/shard_map/ppermute | solution.py:55
  70.5 3.5 %collective-permute-start.10 = (f32[3,22,64]{2,1,0:T(8,128)S(1)}, f32[3,22,64]{2,1,0:T(8,128)S(1)}, u32[]{:S(2)}, u32[]{:S(2)}) collective-permute-start(f32[3,22,64]{2,1,0:T(8,128)S(1)} %get-tuple-element.90), channel_id=1, source_target_pairs={{0,8},{8,16},{16,24},{24,32},{32,40},{40,48},{48,56},{56,64},{64,7... | collective-permute-start | bytes 50696 | tf_op jit(solution)/shard_map/ppermute | solution.py:55
  74.2 1.0 copy.25
  75.2 1.5 %collective-permute-start.11 = (f32[3,22,64]{2,1,0:T(8,128)S(1)}, f32[3,22,64]{2,1,0:T(8,128)S(1)}, u32[]{:S(2)}, u32[]{:S(2)}) collective-permute-start(f32[3,22,64]{2,1,0:T(8,128)S(1)} %get-tuple-element.91), channel_id=1, source_target_pairs={{8,0},{16,8},{24,16},{32,24},{40,32},{48,40},{56,48},{64,56},{72,6... | collective-permute-start | bytes 50696 | tf_op jit(solution)/shard_map/ppermute | solution.py:55
  76.8 4.6 %collective-permute-done.11 = f32[3,22,64]{2,1,0:T(8,128)S(1)} collective-permute-done((f32[3,22,64]{2,1,0:T(8,128)S(1)}, f32[3,22,64]{2,1,0:T(8,128)S(1)}, u32[]{:S(2)}, u32[]{:S(2)}) %collective-permute-start.11) | collective-permute-done | bytes 16928 | tf_op jit(solution)/shard_map/ppermute | solution.py:55
  81.6 0.6 fusion.310
  82.3 0.1 convolution_multiply_fusion.5
  82.6 37.7 %all-gather = f32[128,1,512]{2,1,0:T(1,128)S(1)} all-gather(f32[1,1,512]{2,1,0:T(1,128)S(1)} %maximum_bitcast_fusion), channel_id=1, replica_groups=mesh['xb'=16,'yb'=8] {'xb','yb'}, dimensions={0}, use_global_device_ids=true | all-gather | bytes 264192 | tf_op jit(solution)/shard_map/all_gather | solution.py:206
  120.3 0.2 reshape_transpose_reshape.6
  120.5 0.2 reshape_transpose_reshape.7
  120.7 1.0 fusion.188
  121.7 0.7 fusion.59
  122.4 0.7 fusion.75
  123.1 0.7 fusion.91
  123.7 0.7 fusion.107
  124.4 0.7 fusion.123
  125.1 0.7 fusion.139
  125.8 0.7 fusion.155
  126.6 1.6 %fusion.210 = (f32[]{:T(128)}, f32[]{:T(128)}) fusion(f32[16,64,32]{2,1,0:T(8,128)S(1)} %get-tuple-element.11, f32[16,64,32]{2,1,0:T(8,128)S(1)} %broadcast_in_dim.36, f32[16,64,32]{2,1,0:T(8,128)S(1)} %get-tuple-element.12, f32[16,64,32]{2,1,0:T(8,128)S(1)} %get-tuple-element.13, f32[16,64,32]{2,1,0:T(8,128)S(1)} %get-tuple-element.14, ...), kind=kLoop, calls=%fused_computation.319 | loop fusion | flops 1114110 | bytes 1179656 | tf_op jit(solution)/shard_map/reduce_sum | solution.py:159
  129.5 0.6 dynamic-slice_add_fusion
  (79 shorter events, 1.9 us)
Async XLA Ops:
  0.6 6.6 %copy-start.2 = (f32[8,64,256]{2,1,0:T(8,128)S(1)}, f32[8,64,256]{2,1,0:T(8,128)}, u32[]{:S(2)}) copy-start(f32[8,64,256]{2,1,0:T(8,128)} %param.3) | copy-start | bytes 1572868
  4.5 2.6 %collective-permute-start = (f32[26,3,256]{2,1,0:T(4,128)S(1)}, f32[26,3,256]{2,1,0:T(4,128)S(1)}, u32[]{:S(2)}, u32[]{:S(2)}) collective-permute-start(f32[26,3,256]{2,1,0:T(4,128)S(1)} %select_maximum_fusion.1), channel_id=1, source_target_pairs={{0,1},{1,2},{2,3},{3,4},{4,5},{5,6},{6,7},{8,9},{9,10},{10,11},{11... | collective-permute-start | bytes 239624 | tf_op jit(solution)/shard_map/ppermute | solution.py:55
  5.9 5.0 %collective-permute-start.1 = (f32[26,3,256]{2,1,0:T(4,128)S(1)}, f32[26,3,256]{2,1,0:T(4,128)S(1)}, u32[]{:S(2)}, u32[]{:S(2)}) collective-permute-start(f32[26,3,256]{2,1,0:T(4,128)S(1)} %select_maximum_fusion), channel_id=1, source_target_pairs={{1,0},{2,1},{3,2},{4,3},{5,4},{6,5},{7,6},{9,8},{10,9},{11,10},{12... | collective-permute-start | bytes 239624 | tf_op jit(solution)/shard_map/ppermute | solution.py:55
  7.2 3.8 %copy-start = (f32[8,64,256]{2,1,0:T(8,128)S(1)}, f32[8,64,256]{2,1,0:T(8,128)}, u32[]{:S(2)}) copy-start(f32[8,64,256]{2,1,0:T(8,128)} %param.4) | copy-start | bytes 1572868
  11.1 1.0 copy-start.1
  12.7 14.8 %collective-permute-start.2 = (f32[8,70,256]{2,0,1:T(8,128)S(1)}, f32[8,70,256]{2,0,1:T(8,128)S(1)}, u32[]{:S(2)}, u32[]{:S(2)}) collective-permute-start(f32[8,70,256]{2,0,1:T(8,128)S(1)} %pad_maximum_fusion.3), channel_id=1, source_target_pairs={{0,8},{8,16},{16,24},{24,32},{32,40},{40,48},{48,56},{56,64},{64,7... | collective-permute-start | bytes 1720328 | tf_op jit(solution)/shard_map/ppermute | solution.py:55
  16.8 15.5 %collective-permute-start.3 = (f32[8,70,256]{2,0,1:T(8,128)S(1)}, f32[8,70,256]{2,0,1:T(8,128)S(1)}, u32[]{:S(2)}, u32[]{:S(2)}) collective-permute-start(f32[8,70,256]{2,0,1:T(8,128)S(1)} %pad_maximum_fusion.4), channel_id=1, source_target_pairs={{8,0},{16,8},{24,16},{32,24},{40,32},{48,40},{56,48},{64,56},{72,6... | collective-permute-start | bytes 1720328 | tf_op jit(solution)/shard_map/ppermute | solution.py:55
  40.6 5.3 %collective-permute-start.4 = (f32[8,3,128]{2,1,0:T(4,128)S(1)}, f32[8,3,128]{2,1,0:T(4,128)S(1)}, u32[]{:S(2)}, u32[]{:S(2)}) collective-permute-start(f32[8,3,128]{2,1,0:T(4,128)S(1)} %pad_maximum_fusion.24), channel_id=1, source_target_pairs={{0,1},{1,2},{2,3},{3,4},{4,5},{5,6},{6,7},{8,9},{9,10},{10,11},{11... | collective-permute-start | bytes 36872 | tf_op jit(solution)/shard_map/ppermute | solution.py:55
  44.6 5.4 %collective-permute-start.5 = (f32[8,3,128]{2,1,0:T(4,128)S(1)}, f32[8,3,128]{2,1,0:T(4,128)S(1)}, u32[]{:S(2)}, u32[]{:S(2)}) collective-permute-start(f32[8,3,128]{2,1,0:T(4,128)S(1)} %pad_maximum_fusion.25), channel_id=1, source_target_pairs={{1,0},{2,1},{3,2},{4,3},{5,4},{6,5},{7,6},{9,8},{10,9},{11,10},{12... | collective-permute-start | bytes 36872 | tf_op jit(solution)/shard_map/ppermute | solution.py:55
  50.1 6.6 %collective-permute-start.6 = (f32[7,38,128]{2,1,0:T(8,128)S(1)}, f32[7,38,128]{2,1,0:T(8,128)S(1)}, u32[]{:S(2)}, u32[]{:S(2)}) collective-permute-start(f32[7,38,128]{2,1,0:T(8,128)S(1)} %get-tuple-element.92), channel_id=1, source_target_pairs={{0,8},{8,16},{16,24},{24,32},{32,40},{40,48},{48,56},{56,64},{64,7... | collective-permute-start | bytes 408584 | tf_op jit(solution)/shard_map/ppermute | solution.py:55
  54.0 7.3 %collective-permute-start.7 = (f32[7,38,128]{2,1,0:T(8,128)S(1)}, f32[7,38,128]{2,1,0:T(8,128)S(1)}, u32[]{:S(2)}, u32[]{:S(2)}) collective-permute-start(f32[7,38,128]{2,1,0:T(8,128)S(1)} %get-tuple-element.93), channel_id=1, source_target_pairs={{8,0},{16,8},{24,16},{32,24},{40,32},{48,40},{56,48},{64,56},{72,6... | collective-permute-start | bytes 408584 | tf_op jit(solution)/shard_map/ppermute | solution.py:55
  62.9 4.3 %collective-permute-start.8 = (f32[2,3,64]{2,1,0:T(4,128)S(1)}, f32[2,3,64]{2,1,0:T(4,128)S(1)}, u32[]{:S(2)}, u32[]{:S(2)}) collective-permute-start(f32[2,3,64]{2,1,0:T(4,128)S(1)} %get-tuple-element.94), channel_id=1, source_target_pairs={{0,1},{1,2},{2,3},{3,4},{4,5},{5,6},{6,7},{8,9},{9,10},{10,11},{11... | collective-permute-start | bytes 4616 | tf_op jit(solution)/shard_map/ppermute | solution.py:55
  65.9 4.6 %collective-permute-start.9 = (f32[2,3,64]{2,1,0:T(4,128)S(1)}, f32[2,3,64]{2,1,0:T(4,128)S(1)}, u32[]{:S(2)}, u32[]{:S(2)}) collective-permute-start(f32[2,3,64]{2,1,0:T(4,128)S(1)} %get-tuple-element.95), channel_id=1, source_target_pairs={{1,0},{2,1},{3,2},{4,3},{5,4},{6,5},{7,6},{9,8},{10,9},{11,10},{12... | collective-permute-start | bytes 4616 | tf_op jit(solution)/shard_map/ppermute | solution.py:55
  70.5 6.2 %collective-permute-start.10 = (f32[3,22,64]{2,1,0:T(8,128)S(1)}, f32[3,22,64]{2,1,0:T(8,128)S(1)}, u32[]{:S(2)}, u32[]{:S(2)}) collective-permute-start(f32[3,22,64]{2,1,0:T(8,128)S(1)} %get-tuple-element.90), channel_id=1, source_target_pairs={{0,8},{8,16},{16,24},{24,32},{32,40},{40,48},{48,56},{56,64},{64,7... | collective-permute-start | bytes 50696 | tf_op jit(solution)/shard_map/ppermute | solution.py:55
  75.2 6.1 %collective-permute-start.11 = (f32[3,22,64]{2,1,0:T(8,128)S(1)}, f32[3,22,64]{2,1,0:T(8,128)S(1)}, u32[]{:S(2)}, u32[]{:S(2)}) collective-permute-start(f32[3,22,64]{2,1,0:T(8,128)S(1)} %get-tuple-element.91), channel_id=1, source_target_pairs={{8,0},{16,8},{24,16},{32,24},{40,32},{48,40},{56,48},{64,56},{72,6... | collective-permute-start | bytes 50696 | tf_op jit(solution)/shard_map/ppermute | solution.py:55

commit v6 on v5

--- a/solution.py
+++ b/solution.py
@@ -227,17 +227,19 @@
     low_size = low_coef.shape[0]
     low_first = min(3, low_size)
     assert low_first == 3 or 2 * low_size >= 3
-    guess_b, rhs_b, coef_b, low_coef_b = exchange(
-        [(initial_guess, 3), (right_side, 3), (coefficient, 3), (low_coef, 3)], "yb", 1
+    guess_b, rhs_b, coef_b, mid_coef_b, low_coef_b = exchange(
+        [(initial_guess, 7), (right_side, 7), (coefficient, 7), (mid_coef, 3), (low_coef, 3)],
+        "yb",
+        1,
     )[0]
     guess_b, rhs_b, coef_b = exchange([(guess_b, 3), (rhs_b, 2), (coef_b, 3)], "xb", 0)[0]
     fine, fine_res = smooth_box(guess_b, rhs_b[:, 1:-1], coef_b, 1.0)
+    fine = fine[:, 4:-4]
     mid_rhs = restrict_field(fine_res)
-    mid_rhs_b, mid_coef_b = exchange([(mid_rhs, 3), (mid_coef, 3)], "yb", 1)[0]
     mid_rhs_b, mid_coef_b, low_coef_b = exchange(
-        [(mid_rhs_b, 2), (mid_coef_b, 3), (low_coef_b, low_first)], "xb", 0
+        [(mid_rhs, 2), (mid_coef_b, 3), (low_coef_b, low_first)], "xb", 0
     )[0]
-    middle, mid_res = smooth_box(None, mid_rhs_b[:, 1:-1], mid_coef_b, 0.25)
+    middle, mid_res = smooth_box(None, mid_rhs_b, mid_coef_b, 0.25)
     low_rhs = restrict_field(mid_res)
     (low_rhs_b,) = exchange([(low_rhs, 3)], "yb", 1)[0]
     forwards = ()

time: 132 us -> 129 us (0.977)
  starting transfers between devices: 27.4 us -> 23.5 us
    ppermute x12 -> x10, starting transfers between devices: 27.4 us -> 23.5 us  [exchange(): got = lax.ppermute(joined, axis, pairs)]
    unnamed x17 -> x21, local copies, waits for them, and re-layouts: 2.53 us -> 4.42 us
    slice x11 -> x8, local copies, waits for them, and re-layouts: 2.21 us -> 0.34 us  [exchange(): pieces.append(lax.slice_in_dim(block, begin, begin + rows, axis=dim))]
    ppermute x12 -> x10, waiting for transfers between devices: 35.2 us -> 34.9 us  [exchange(): got = lax.ppermute(joined, axis, pairs)]
  transfers between devices with their start and end apart: 12 -> 10, of which waited for: 8 -> 7; matrix products, arithmetic and copies ran while one was open for 2% -> 2% of each run, Pallas kernels for 0% -> 0%
where the time goes in v6:
time: 129 us; the launch traced here: 127 us
  blocking collectives  37.7 us (29%)
  waiting for transfers between devices  34.9 us (27%)
  starting transfers between devices  23.5 us (18%)
  other arithmetic  18.3 us (14%)
  local copies, waits for them, and re-layouts  6.72 us (5%)
  matrix products  3.27 us (3%)
  between operations  2.69 us (2%)
    all_gather x1, blocking collectives, collect_grid(): both = lax.all_gather(flat, ('xb', 'yb'), axis=0, tiled=True)  37.7 us
    ppermute x10, waiting for transfers between devices, exchange(): got = lax.ppermute(joined, axis, pairs)  34.9 us
    ppermute x10, starting transfers between devices, exchange(): got = lax.ppermute(joined, axis, pairs)  23.5 us
    add x7, other arithmetic, coarse_solve(): field + jacobi_weight * (right_side - apply_operator(extend(field), field...  4.78 us
    unnamed x21, local copies, waits for them, and re-layouts  4.42 us
    add x3, other arithmetic, smooth_box(): second = trim(first) + second_step  2.77 us
  transfers between devices with their start and end apart: 10, of which 7 were waited for; matrix products, arithmetic and copies ran while one was open for 2% of the time, Pallas kernels for 0%

profile of v6, /device:TPU:0, one launch (start us, length us, event | category | flops | bytes accessed | tf_op | source)
XLA Modules:
  0.0 127.0 jit_solution(8711913986575202182)
XLA Ops:
  0.7 1.0 slice_dynamic-update-slice_fusion.2
  1.7 1.3 %fusion.218 = f32[4,64,128]{2,1,0:T(8,128)S(1)} fusion(f32[4,2,64,256]{3,2,1,0:T(8,128)} %bitcast.81, s32[256]{0:T(256)S(1)} %and_select_fusion.4), kind=kOutput, calls=%fused_computation.335 | convolution fusion | flops 100761600 | bytes 656384 | tf_op jit(solution)/shard_map/xyZ,zZ->xyz/dot_general | solution.py:136
  3.0 0.2 convolution_multiply_fusion.1
  3.3 0.2 fusion.300
  3.4 0.1 convolution_multiply_fusion.3
  3.6 0.9 slice_dynamic-update-slice_fusion.1
  4.5 1.3 %collective-permute-start = (f32[30,7,256]{2,1,0:T(8,128)S(1)}, f32[30,7,256]{2,1,0:T(8,128)S(1)}, u32[]{:S(2)}, u32[]{:S(2)}) collective-permute-start(f32[30,7,256]{2,1,0:T(8,128)S(1)} %constant_dynamic-update-slice_fusion), channel_id=1, source_target_pairs={{0,1},{1,2},{2,3},{3,4},{4,5},{5,6},{6,7},{8,9},{9,10},{10,11},{11... | collective-permute-start | bytes 645128 | tf_op jit(solution)/shard_map/ppermute | solution.py:55
  5.9 1.3 %collective-permute-start.1 = (f32[30,7,256]{2,1,0:T(8,128)S(1)}, f32[30,7,256]{2,1,0:T(8,128)S(1)}, u32[]{:S(2)}, u32[]{:S(2)}) collective-permute-start(f32[30,7,256]{2,1,0:T(8,128)S(1)} %constant_dynamic-update-slice_fusion.2), channel_id=1, source_target_pairs={{1,0},{2,1},{3,2},{4,3},{5,4},{6,5},{7,6},{9,8},{10,9},{11,10},{12... | collective-permute-start | bytes 645128 | tf_op jit(solution)/shard_map/ppermute | solution.py:55
  7.3 0.3 copy_dynamic-update-slice_fusion.1
  7.6 3.5 %collective-permute-done.1 = f32[30,7,256]{2,1,0:T(8,128)S(1)} collective-permute-done((f32[30,7,256]{2,1,0:T(8,128)S(1)}, f32[30,7,256]{2,1,0:T(8,128)S(1)}, u32[]{:S(2)}, u32[]{:S(2)}) %collective-permute-start.1) | collective-permute-done | bytes 215072 | tf_op jit(solution)/shard_map/ppermute | solution.py:55
  11.3 0.3 copy_dynamic-update-slice_fusion
  11.8 0.6 copy-done.2
  12.3 0.3 copy_dynamic-update-slice_fusion.2
  12.8 0.2 pad_maximum_fusion.3
  13.0 3.9 %collective-permute-start.2 = (f32[8,78,256]{2,0,1:T(8,128)S(1)}, f32[8,78,256]{2,0,1:T(8,128)S(1)}, u32[]{:S(2)}, u32[]{:S(2)}) collective-permute-start(f32[8,78,256]{2,0,1:T(8,128)S(1)} %pad_maximum_fusion.3), channel_id=1, source_target_pairs={{0,8},{8,16},{16,24},{24,32},{32,40},{40,48},{48,56},{56,64},{64,7... | collective-permute-start | bytes 1916936 | tf_op jit(solution)/shard_map/ppermute | solution.py:55
  16.9 0.2 pad_maximum_fusion.4
  17.1 1.3 %collective-permute-start.3 = (f32[8,78,256]{2,0,1:T(8,128)S(1)}, f32[8,78,256]{2,0,1:T(8,128)S(1)}, u32[]{:S(2)}, u32[]{:S(2)}) collective-permute-start(f32[8,78,256]{2,0,1:T(8,128)S(1)} %pad_maximum_fusion.4), channel_id=1, source_target_pairs={{8,0},{16,8},{24,16},{32,24},{40,32},{48,40},{56,48},{64,56},{72,6... | collective-permute-start | bytes 1916936 | tf_op jit(solution)/shard_map/ppermute | solution.py:55
  18.5 9.4 %collective-permute-done.2 = f32[8,78,256]{2,0,1:T(8,128)S(1)} collective-permute-done((f32[8,78,256]{2,0,1:T(8,128)S(1)}, f32[8,78,256]{2,0,1:T(8,128)S(1)}, u32[]{:S(2)}, u32[]{:S(2)}) %collective-permute-start.2) | collective-permute-done | bytes 639008 | tf_op jit(solution)/shard_map/ppermute | solution.py:55
  28.0 4.7 %collective-permute-done.3 = f32[8,78,256]{2,0,1:T(8,128)S(1)} collective-permute-done((f32[8,78,256]{2,0,1:T(8,128)S(1)}, f32[8,78,256]{2,0,1:T(8,128)S(1)}, u32[]{:S(2)}, u32[]{:S(2)}) %collective-permute-start.3) | collective-permute-done | bytes 639008 | tf_op jit(solution)/shard_map/ppermute | solution.py:55
  32.8 0.2 pad_maximum_fusion.2
  33.1 1.6 %add_add_fusion = (f32[12,76,256]{2,0,1:T(8,128)S(1)}, f32[12,76,256]{2,0,1:T(8,128)S(1)}, f32[12,76,256]{2,0,1:T(8,128)S(1)}, f32[12,76,256]{2,0,1:T(8,128)S(1)...) fusion(f32[14,78,256]{2,0,1:T(8,128)S(1)} %pad_maximum_fusion.2), kind=kLoop, calls=%fused_computation.55 | loop fusion | flops 5836800 | bytes 14041088 | tf_op jit(solution)/shard_map/add | solution.py:175
  34.8 0.3 pad_maximum_fusion.1
  35.1 0.2 pad_maximum_fusion
  35.3 2.1 %slice_add_fusion.4 = (f32[12,76,256]{2,0,1:T(8,128)S(1)}, f32[12,76,256]{2,0,1:T(8,128)S(1)}) fusion(f32[14,78,256]{2,0,1:T(8,128)S(1)} %pad_maximum_fusion, f32[12,76,256]{2,0,1:T(8,128)S(1)} %get-tuple-element.42, f32[12,76,256]{2,0,1:T(8,128)S(1)} %get-tuple-element.43, f32[12,76,256]{2,0,1:T(8,128)S(1)} %get-tuple-element.41, ...), kind=kLoop, calls=%fused_computation.74 | loop fusion | flops 5369856 | bytes 18087936 | tf_op jit(solution)/shard_map/add | solution.py:188
  37.4 2.4 %fusion.31 = f32[10,74,256]{2,0,1:T(8,128)S(1)} fusion(f32[12,76,256]{2,0,1:T(8,128)S(1)} %get-tuple-element.44, f32[12,76,256]{2,0,1:T(8,128)S(1)} %get-tuple-element.42, f32[12,76,256]{2,0,1:T(8,128)S(1)} %get-tuple-element.43, f32[12,76,256]{2,0,1:T(8,128)S(1)} %get-tuple-element.41, f32[12,76,256]{2,0,1:T(8,128)S(1)} %get-tuple-element.40, ...), kind=kLoop, calls=%fused_computation.63 | loop fusion | flops 3599360 | bytes 18976768 | tf_op jit(solution)/shard_map/add | solution.py:194
  39.8 0.9 fusion.40
  40.8 0.3 reshape.333
  41.1 0.5 fusion.365
  41.6 0.3 fusion.213
  41.9 0.3 convolution_multiply_fusion
  42.3 3.9 %collective-permute-start.4 = (f32[7,38,128]{2,1,0:T(8,128)S(1)}, f32[7,38,128]{2,1,0:T(8,128)S(1)}, u32[]{:S(2)}, u32[]{:S(2)}) collective-permute-start(f32[7,38,128]{2,1,0:T(8,128)S(1)} %get-tuple-element.89), channel_id=1, source_target_pairs={{0,8},{8,16},{16,24},{24,32},{32,40},{40,48},{48,56},{56,64},{64,7... | collective-permute-start | bytes 408584 | tf_op jit(solution)/shard_map/ppermute | solution.py:55
  46.2 1.3 %collective-permute-start.5 = (f32[7,38,128]{2,1,0:T(8,128)S(1)}, f32[7,38,128]{2,1,0:T(8,128)S(1)}, u32[]{:S(2)}, u32[]{:S(2)}) collective-permute-start(f32[7,38,128]{2,1,0:T(8,128)S(1)} %get-tuple-element.90), channel_id=1, source_target_pairs={{8,0},{16,8},{24,16},{32,24},{40,32},{48,40},{56,48},{64,56},{72,6... | collective-permute-start | bytes 408584 | tf_op jit(solution)/shard_map/ppermute | solution.py:55
  47.5 0.1 fusion.319
  47.6 1.2 collective-permute-done.4
  48.8 4.4 %collective-permute-done.5 = f32[7,38,128]{2,1,0:T(8,128)S(1)} collective-permute-done((f32[7,38,128]{2,1,0:T(8,128)S(1)}, f32[7,38,128]{2,1,0:T(8,128)S(1)}, u32[]{:S(2)}, u32[]{:S(2)}) %collective-permute-start.5) | collective-permute-done | bytes 136224 | tf_op jit(solution)/shard_map/ppermute | solution.py:55
  53.2 0.2 multiply_divide_fusion
  53.5 0.2 fusion.246
  53.7 0.7 fusion.272
  54.4 0.2 fusion.296
  54.6 0.1 convolution_multiply_fusion.2
  54.7 3.7 %collective-permute-start.6 = (f32[2,3,64]{2,1,0:T(4,128)S(1)}, f32[2,3,64]{2,1,0:T(4,128)S(1)}, u32[]{:S(2)}, u32[]{:S(2)}) collective-permute-start(f32[2,3,64]{2,1,0:T(4,128)S(1)} %get-tuple-element.91), channel_id=1, source_target_pairs={{0,1},{1,2},{2,3},{3,4},{4,5},{5,6},{6,7},{8,9},{9,10},{10,11},{11... | collective-permute-start | bytes 4616 | tf_op jit(solution)/shard_map/ppermute | solution.py:55
  58.4 1.3 %collective-permute-start.7 = (f32[2,3,64]{2,1,0:T(4,128)S(1)}, f32[2,3,64]{2,1,0:T(4,128)S(1)}, u32[]{:S(2)}, u32[]{:S(2)}) collective-permute-start(f32[2,3,64]{2,1,0:T(4,128)S(1)} %get-tuple-element.92), channel_id=1, source_target_pairs={{1,0},{2,1},{3,2},{4,3},{5,4},{6,5},{7,6},{9,8},{10,9},{11,10},{12... | collective-permute-start | bytes 4616 | tf_op jit(solution)/shard_map/ppermute | solution.py:55
  59.7 7.4 %collective-permute-done.7 = f32[2,3,64]{2,1,0:T(4,128)S(1)} collective-permute-done((f32[2,3,64]{2,1,0:T(4,128)S(1)}, f32[2,3,64]{2,1,0:T(4,128)S(1)}, u32[]{:S(2)}, u32[]{:S(2)}) %collective-permute-start.7) | collective-permute-done | bytes 1568 | tf_op jit(solution)/shard_map/ppermute | solution.py:55
  67.1 4.1 %collective-permute-start.8 = (f32[3,22,64]{2,1,0:T(8,128)S(1)}, f32[3,22,64]{2,1,0:T(8,128)S(1)}, u32[]{:S(2)}, u32[]{:S(2)}) collective-permute-start(f32[3,22,64]{2,1,0:T(8,128)S(1)} %get-tuple-element.87), channel_id=1, source_target_pairs={{0,8},{8,16},{16,24},{24,32},{32,40},{40,48},{48,56},{56,64},{64,7... | collective-permute-start | bytes 50696 | tf_op jit(solution)/shard_map/ppermute | solution.py:55
  71.5 1.0 copy.24
  72.5 1.5 %collective-permute-start.9 = (f32[3,22,64]{2,1,0:T(8,128)S(1)}, f32[3,22,64]{2,1,0:T(8,128)S(1)}, u32[]{:S(2)}, u32[]{:S(2)}) collective-permute-start(f32[3,22,64]{2,1,0:T(8,128)S(1)} %get-tuple-element.88), channel_id=1, source_target_pairs={{8,0},{16,8},{24,16},{32,24},{40,32},{48,40},{56,48},{64,56},{72,6... | collective-permute-start | bytes 50696 | tf_op jit(solution)/shard_map/ppermute | solution.py:55
  74.1 4.3 %collective-permute-done.9 = f32[3,22,64]{2,1,0:T(8,128)S(1)} collective-permute-done((f32[3,22,64]{2,1,0:T(8,128)S(1)}, f32[3,22,64]{2,1,0:T(8,128)S(1)}, u32[]{:S(2)}, u32[]{:S(2)}) %collective-permute-start.9) | collective-permute-done | bytes 16928 | tf_op jit(solution)/shard_map/ppermute | solution.py:55
  78.4 0.1 slice_divide_fusion
  78.6 0.6 fusion.311
  79.2 0.1 fusion.320
  79.4 0.1 convolution_multiply_fusion.5
  79.6 37.7 %all-gather = f32[128,1,512]{2,1,0:T(1,128)S(1)} all-gather(f32[1,1,512]{2,1,0:T(1,128)S(1)} %maximum_bitcast_fusion), channel_id=1, replica_groups=mesh['xb'=16,'yb'=8] {'xb','yb'}, dimensions={0}, use_global_device_ids=true | all-gather | bytes 264192 | tf_op jit(solution)/shard_map/all_gather | solution.py:206
  117.3 0.2 reshape_transpose_reshape.6
  117.5 0.2 reshape_transpose_reshape.7
  117.7 1.0 fusion.192
  118.7 0.7 fusion.68
  119.4 0.7 fusion.84
  120.0 0.7 fusion.100
  120.7 0.7 fusion.116
  121.4 0.7 fusion.132
  122.1 0.7 fusion.148
  122.8 0.7 fusion.164
  123.5 1.6 %fusion.210 = (f32[]{:T(128)}, f32[]{:T(128)}) fusion(f32[16,64,32]{2,1,0:T(8,128)S(1)} %get-tuple-element.11, f32[16,64,32]{2,1,0:T(8,128)S(1)} %broadcast_in_dim.37, f32[16,64,32]{2,1,0:T(8,128)S(1)} %get-tuple-element.12, f32[16,64,32]{2,1,0:T(8,128)S(1)} %get-tuple-element.13, f32[16,64,32]{2,1,0:T(8,128)S(1)} %get-tuple-element.14, ...), kind=kLoop, calls=%fused_computation.320 | loop fusion | flops 1114110 | bytes 1179656 | tf_op jit(solution)/shard_map/reduce_sum | solution.py:159
  126.4 0.6 dynamic-slice_add_fusion
  (75 shorter events, 1.7 us)
Async XLA Ops:
  0.6 3.9 %copy-start = (f32[8,64,256]{2,1,0:T(8,128)S(1)}, f32[8,64,256]{2,1,0:T(8,128)}, u32[]{:S(2)}) copy-start(f32[8,64,256]{2,1,0:T(8,128)} %param.5) | copy-start | bytes 1572868
  0.6 6.6 %copy-start.1 = (f32[8,64,256]{2,1,0:T(8,128)S(1)}, f32[8,64,256]{2,1,0:T(8,128)}, u32[]{:S(2)}) copy-start(f32[8,64,256]{2,1,0:T(8,128)} %param.4) | copy-start | bytes 1572868
  4.5 2.7 %collective-permute-start = (f32[30,7,256]{2,1,0:T(8,128)S(1)}, f32[30,7,256]{2,1,0:T(8,128)S(1)}, u32[]{:S(2)}, u32[]{:S(2)}) collective-permute-start(f32[30,7,256]{2,1,0:T(8,128)S(1)} %constant_dynamic-update-slice_fusion), channel_id=1, source_target_pairs={{0,1},{1,2},{2,3},{3,4},{4,5},{5,6},{6,7},{8,9},{9,10},{10,11},{11... | collective-permute-start | bytes 645128 | tf_op jit(solution)/shard_map/ppermute | solution.py:55
  5.9 5.2 %collective-permute-start.1 = (f32[30,7,256]{2,1,0:T(8,128)S(1)}, f32[30,7,256]{2,1,0:T(8,128)S(1)}, u32[]{:S(2)}, u32[]{:S(2)}) collective-permute-start(f32[30,7,256]{2,1,0:T(8,128)S(1)} %constant_dynamic-update-slice_fusion.2), channel_id=1, source_target_pairs={{1,0},{2,1},{3,2},{4,3},{5,4},{6,5},{7,6},{9,8},{10,9},{11,10},{12... | collective-permute-start | bytes 645128 | tf_op jit(solution)/shard_map/ppermute | solution.py:55
  11.3 1.0 copy-start.2
  13.0 14.9 %collective-permute-start.2 = (f32[8,78,256]{2,0,1:T(8,128)S(1)}, f32[8,78,256]{2,0,1:T(8,128)S(1)}, u32[]{:S(2)}, u32[]{:S(2)}) collective-permute-start(f32[8,78,256]{2,0,1:T(8,128)S(1)} %pad_maximum_fusion.3), channel_id=1, source_target_pairs={{0,8},{8,16},{16,24},{24,32},{32,40},{40,48},{48,56},{56,64},{64,7... | collective-permute-start | bytes 1916936 | tf_op jit(solution)/shard_map/ppermute | solution.py:55
  17.1 15.7 %collective-permute-start.3 = (f32[8,78,256]{2,0,1:T(8,128)S(1)}, f32[8,78,256]{2,0,1:T(8,128)S(1)}, u32[]{:S(2)}, u32[]{:S(2)}) collective-permute-start(f32[8,78,256]{2,0,1:T(8,128)S(1)} %pad_maximum_fusion.4), channel_id=1, source_target_pairs={{8,0},{16,8},{24,16},{32,24},{40,32},{48,40},{56,48},{64,56},{72,6... | collective-permute-start | bytes 1916936 | tf_op jit(solution)/shard_map/ppermute | solution.py:55
  42.3 6.5 %collective-permute-start.4 = (f32[7,38,128]{2,1,0:T(8,128)S(1)}, f32[7,38,128]{2,1,0:T(8,128)S(1)}, u32[]{:S(2)}, u32[]{:S(2)}) collective-permute-start(f32[7,38,128]{2,1,0:T(8,128)S(1)} %get-tuple-element.89), channel_id=1, source_target_pairs={{0,8},{8,16},{16,24},{24,32},{32,40},{40,48},{48,56},{56,64},{64,7... | collective-permute-start | bytes 408584 | tf_op jit(solution)/shard_map/ppermute | solution.py:55
  46.2 7.0 %collective-permute-start.5 = (f32[7,38,128]{2,1,0:T(8,128)S(1)}, f32[7,38,128]{2,1,0:T(8,128)S(1)}, u32[]{:S(2)}, u32[]{:S(2)}) collective-permute-start(f32[7,38,128]{2,1,0:T(8,128)S(1)} %get-tuple-element.90), channel_id=1, source_target_pairs={{8,0},{16,8},{24,16},{32,24},{40,32},{48,40},{56,48},{64,56},{72,6... | collective-permute-start | bytes 408584 | tf_op jit(solution)/shard_map/ppermute | solution.py:55
  54.7 5.0 %collective-permute-start.6 = (f32[2,3,64]{2,1,0:T(4,128)S(1)}, f32[2,3,64]{2,1,0:T(4,128)S(1)}, u32[]{:S(2)}, u32[]{:S(2)}) collective-permute-start(f32[2,3,64]{2,1,0:T(4,128)S(1)} %get-tuple-element.91), channel_id=1, source_target_pairs={{0,1},{1,2},{2,3},{3,4},{4,5},{5,6},{6,7},{8,9},{9,10},{10,11},{11... | collective-permute-start | bytes 4616 | tf_op jit(solution)/shard_map/ppermute | solution.py:55
  58.4 8.7 %collective-permute-start.7 = (f32[2,3,64]{2,1,0:T(4,128)S(1)}, f32[2,3,64]{2,1,0:T(4,128)S(1)}, u32[]{:S(2)}, u32[]{:S(2)}) collective-permute-start(f32[2,3,64]{2,1,0:T(4,128)S(1)} %get-tuple-element.92), channel_id=1, source_target_pairs={{1,0},{2,1},{3,2},{4,3},{5,4},{6,5},{7,6},{9,8},{10,9},{11,10},{12... | collective-permute-start | bytes 4616 | tf_op jit(solution)/shard_map/ppermute | solution.py:55
  67.1 6.8 %collective-permute-start.8 = (f32[3,22,64]{2,1,0:T(8,128)S(1)}, f32[3,22,64]{2,1,0:T(8,128)S(1)}, u32[]{:S(2)}, u32[]{:S(2)}) collective-permute-start(f32[3,22,64]{2,1,0:T(8,128)S(1)} %get-tuple-element.87), channel_id=1, source_target_pairs={{0,8},{8,16},{16,24},{24,32},{32,40},{40,48},{48,56},{56,64},{64,7... | collective-permute-start | bytes 50696 | tf_op jit(solution)/shard_map/ppermute | solution.py:55
  72.5 5.8 %collective-permute-start.9 = (f32[3,22,64]{2,1,0:T(8,128)S(1)}, f32[3,22,64]{2,1,0:T(8,128)S(1)}, u32[]{:S(2)}, u32[]{:S(2)}) collective-permute-start(f32[3,22,64]{2,1,0:T(8,128)S(1)} %get-tuple-element.88), channel_id=1, source_target_pairs={{8,0},{16,8},{24,16},{32,24},{40,32},{48,40},{56,48},{64,56},{72,6... | collective-permute-start | bytes 50696 | tf_op jit(solution)/shard_map/ppermute | solution.py:55
